TPU v7x, 256 devices: a whole 4x4x8 slice. The times are simulated.
256 devices in a mesh: ctx: 16 (over z, x_hi), head: 16 (over x_lo, y, core).
Axes of the slice: x: 4 (x_hi: 2, x_lo: 2; x = x_hi * 2 + x_lo), y: 4, z: 8, core: 2. Of those that a mesh axis runs over, the one named last changes fastest.
Arguments:
- queries: bfloat16 [16384, 8192], P('ctx', 'head'), may hold values from -5.5 to 5.5
- keys: bfloat16 [16384, 512], P(('ctx', 'head')), may hold values from -5.5 to 5.5
- values: bfloat16 [16384, 512], P(('ctx', 'head')), may hold values from -6 to 6
- comp_k_weight: float32 [32, 512], replicated, may hold values from -0.79549513 to 0.79549513
- comp_v_weight: float32 [32, 512], replicated, may hold values from -1 to 1
- gate_logits: float32 [3, 64, 16384], P(None, 'head', 'ctx'), may hold values from -6 to 6
- sel_tiles: int32 [64, 64], replicated, may hold values from 0 to 243, as said below
Outputs:
- attended: bfloat16 [16384, 8192], P('ctx', 'head')
Inputs may be any that keep to these rules, and one draw needn't show every extreme that they name: `sel_tiles`: among the indices of the query blocks of one ctx shard (4 blocks) for one group, exactly 2 distinct tiles lie in each ctx shard up to and including their own and none in later ones; the first index of every query block names a tile among the first 4 tiles of its own ctx shard; indices may repeat within a block.
All inputs are finite; a program needn't handle non-finite values.
Results may differ from a plain program's by a relative error of at most 0.012.
Values may be sent and summed in bfloat16 or wider, within the bound.
No kernel may reach another device: no remote copies, remote signals or barrier semaphores. Data moves between devices by JAX's collectives and lax.ppermute only.
A program may use at most 64 MiB of HBM per device.

v0:
```python
import jax
import jax.numpy as jnp
from jax import lax
from jax.sharding import PartitionSpec as P

H = 64
G = 4
HD = 128
KERN = 32
STRIDE = 16
TILE = 64
TOPK = 16
WIN = 512
QB = 256
CAP = 2


def shifted(block, axis, distance):
    devices = range(lax.axis_size(axis))
    route = [(i - distance, i) for i in devices if i - distance in devices]
    return lax.ppermute(block, axis, route)


def online_step(folded, query_head, block_kv, allowed):
    running_max, running_sum, accum_out = folded
    scores = jnp.einsum(
        "qd,kd->qk", query_head, block_kv[:, :HD], preferred_element_type=jnp.float32
    ) * HD ** (-0.5)
    block_peak = jnp.max(jnp.where(allowed, scores, -jnp.inf), axis=-1)
    fresh_max = jnp.maximum(running_max, block_peak)
    weights = jnp.where(allowed, jnp.exp(scores - fresh_max[:, None]), 0.0)
    shrink = jnp.exp(running_max - fresh_max)
    running_sum = running_sum * shrink + jnp.sum(weights, axis=-1)
    product = jnp.dot(
        weights.astype(jnp.bfloat16), block_kv[:, HD:], preferred_element_type=jnp.float32
    )
    accum_out = accum_out * shrink[:, None] + product
    return (fresh_max, running_sum, accum_out)


def heads_step(folded, query_heads, block_kv, allowed):

    def per_head(element):
        return online_step((element[0], element[1], element[2]), element[3], block_kv, allowed)

    return lax.map(per_head, (folded[0], folded[1], folded[2], query_heads))


def finish(folded):
    return folded[2] / folded[1][..., None]


def local(queries, keys, values, comp_k_weight, comp_v_weight, gate_logits, sel_tiles):
    ctx_count = lax.axis_size("ctx")
    ctx_index = lax.axis_index("ctx")
    head_index = lax.axis_index("head")
    local_rows = queries.shape[0]
    local_heads = queries.shape[1] // HD
    group_index = head_index * local_heads // (H // G)
    all_keys, all_values = (
        lax.all_gather(keys, "head", axis=0, tiled=True),
        lax.all_gather(values, "head", axis=0, tiled=True),
    )
    group_keys = lax.dynamic_slice_in_dim(all_keys, group_index * HD, HD, 1)
    group_values = lax.dynamic_slice_in_dim(all_values, group_index * HD, HD, 1)
    group_kv = jnp.concatenate([group_keys, group_values], axis=1)
    positions = ctx_index * local_rows + jnp.arange(local_rows)
    query_heads = queries.reshape(local_rows, local_heads, HD).transpose(1, 0, 2)
    tail_rows = shifted(group_kv[: KERN - STRIDE], "ctx", -1)
    extended = jnp.concatenate([group_kv, tail_rows], axis=0)
    comp_weight = jnp.concatenate(
        [
            lax.dynamic_slice_in_dim(comp_k_weight, group_index * HD, HD, 1),
            lax.dynamic_slice_in_dim(comp_v_weight, group_index * HD, HD, 1),
        ],
        axis=1,
    )
    comp_local = local_rows // STRIDE
    first_half = extended[:local_rows].reshape(comp_local, STRIDE, 2 * HD).astype(jnp.float32)
    second_half = (
        extended[STRIDE : STRIDE + local_rows]
        .reshape(comp_local, STRIDE, 2 * HD)
        .astype(jnp.float32)
    )
    compressed = (
        jnp.sum(first_half * comp_weight[None, :STRIDE], 1)
        + jnp.sum(second_half * comp_weight[None, STRIDE:], 1)
    ).astype(jnp.bfloat16)
    sink_init = (
        jnp.zeros((local_heads, local_rows), jnp.float32),
        jnp.ones((local_heads, local_rows), jnp.float32),
        jnp.zeros((local_heads, local_rows, HD), jnp.float32),
    )
    shard_rows = lax.all_gather(compressed, "ctx", axis=0, tiled=True)
    row_count = shard_rows.shape[0]
    wide_block = min(row_count, 512)
    grouped = shard_rows.reshape(row_count // wide_block, wide_block, 2 * HD)

    def scan_step(running, element):
        block_kv, block_index = element
        block_end = (block_index * wide_block + jnp.arange(wide_block)) * STRIDE + KERN - 1
        allowed = block_end[None, :] <= positions[:, None]
        return (heads_step(running, query_heads, block_kv, allowed), None)

    result, unused = lax.scan(scan_step, sink_init, (grouped, jnp.arange(row_count // wide_block)))
    comp_out = finish(result)
    previous = shifted(group_kv[local_rows - WIN :], "ctx", 1)
    window_kv = jnp.concatenate([previous, group_kv], axis=0)

    def window_block(block_index):
        row_begin = block_index * WIN
        query_part = lax.dynamic_slice_in_dim(query_heads, row_begin, WIN, 1)
        kv_part = lax.dynamic_slice_in_dim(window_kv, row_begin, 2 * WIN, 0)
        key_pos = ctx_index * local_rows + row_begin - WIN + jnp.arange(2 * WIN)
        query_pos = ctx_index * local_rows + row_begin + jnp.arange(WIN)
        allowed = (
            (key_pos[None, :] <= query_pos[:, None])
            & (key_pos[None, :] > query_pos[:, None] - WIN)
            & (key_pos[None, :] >= 0)
        )
        window_init = (
            jnp.full((local_heads, WIN), -jnp.inf, jnp.float32),
            jnp.zeros((local_heads, WIN), jnp.float32),
            jnp.zeros((local_heads, WIN, HD), jnp.float32),
        )
        return finish(heads_step(window_init, query_part, kv_part, allowed))

    win_blocks = lax.map(window_block, jnp.arange(local_rows // WIN))
    win_out = win_blocks.transpose(1, 0, 2, 3).reshape(local_heads, local_rows, HD)
    block_count = local_rows // QB
    tiles_shard = local_rows // TILE
    group_tiles = lax.dynamic_slice_in_dim(sel_tiles, group_index * TOPK, TOPK, 1)
    own_tiles = lax.dynamic_slice_in_dim(group_tiles, ctx_index * block_count, block_count, 0)
    own_flat = own_tiles.reshape(-1)
    query_blocks = query_heads.reshape(local_heads, block_count, QB, HD).transpose(1, 0, 2, 3)
    sel_init = (
        jnp.zeros((block_count, local_heads, QB), jnp.float32),
        jnp.ones((block_count, local_heads, QB), jnp.float32),
        jnp.zeros((block_count, local_heads, QB, HD), jnp.float32),
    )
    requests = group_tiles.reshape(ctx_count, block_count * TOPK)
    local_ids = ctx_index * tiles_shard + jnp.arange(tiles_shard)
    present = jnp.any(requests[:, :, None] == local_ids[None, None, :], axis=1)
    order_rank = jnp.cumsum(present.astype(jnp.int32), axis=1) - 1
    picked = present[:, None, :] & (order_rank[:, None, :] == jnp.arange(CAP)[None, :, None])
    outbox = jnp.einsum(
        "dct,tx->dcx",
        picked.astype(jnp.bfloat16),
        group_kv.reshape(tiles_shard, TILE * 2 * HD),
        preferred_element_type=jnp.float32,
    ).astype(jnp.bfloat16)
    received = lax.all_to_all(outbox, "ctx", split_axis=0, concat_axis=0, tiled=True)
    all_ids = jnp.arange(ctx_count * tiles_shard).reshape(ctx_count, tiles_shard)
    wanted = jnp.any(own_flat[:, None, None] == all_ids[None, :, :], axis=0)
    wanted_rank = jnp.cumsum(wanted.astype(jnp.int32), axis=1) - 1
    chosen = wanted[:, None, :] & (wanted_rank[:, None, :] == jnp.arange(CAP)[None, :, None])
    slot_tile = jnp.sum(jnp.where(chosen, all_ids[:, None, :], 0), axis=2).reshape(-1)
    slot_ok = jnp.any(chosen, axis=2).reshape(-1)
    slot_kv = received.reshape(ctx_count * CAP * TILE, 2 * HD)
    key_pos = (slot_tile[:, None] * TILE + jnp.arange(TILE)[None, :]).reshape(-1)

    def per_block(element):
        block_max, block_sum, block_out, block_query, block_tiles, block_index = element
        is_named = slot_ok & jnp.any(block_tiles[:, None] == slot_tile[None, :], axis=0)
        key_ok = jnp.repeat(is_named, TILE)
        query_pos = ctx_index * local_rows + block_index * QB + jnp.arange(QB)
        allowed = key_ok[None, :] & (key_pos[None, :] <= query_pos[:, None])
        return heads_step((block_max, block_sum, block_out), block_query, slot_kv, allowed)

    sel_state = lax.map(
        per_block,
        (sel_init[0], sel_init[1], sel_init[2], query_blocks, own_tiles, jnp.arange(block_count)),
    )
    sel_out = finish(sel_state).transpose(1, 0, 2, 3).reshape(local_heads, local_rows, HD)
    gate_values = jax.nn.sigmoid(gate_logits)
    combined = (
        gate_values[0][..., None] * comp_out
        + gate_values[1][..., None] * sel_out
        + gate_values[2][..., None] * win_out
    )
    return combined.transpose(1, 0, 2).reshape(local_rows, local_heads * HD).astype(jnp.bfloat16)


def solution(mesh):
    placed = (
        P("ctx", "head"),
        P(("ctx", "head"), None),
        P(("ctx", "head"), None),
        P(),
        P(),
        P(None, "head", "ctx"),
        P(),
    )
    return jax.shard_map(
        local, mesh=mesh, in_specs=placed, out_specs=P("ctx", "head"), check_vma=False
    )
```

profile of v0, /device:TPU:32, one launch (start us, length us, event | category | flops | bytes accessed | tf_op | source)
XLA Modules:
  0.0 361.6 jit_solution(1468088390830321323)
XLA Ops:
  16.6 29.9 %all-gather.5.cloned.1.call-done = bf16[1024,512]{1,0:T(8,128)(2,1)} async-done(((bf16[64,512]{1,0:T(8,128)(2,1)}), bf16[1024,512]{1,0:T(8,128)(2,1)}) %all-gather.5.cloned.1.call-update) | async-done | bytes 1048592 | tf_op jit(solution)/shard_map/all_gather | solution.py:62
  47.5 35.7 %all-gather.3.cloned.1.call-done = bf16[1024,512]{1,0:T(8,128)(2,1)} async-done(((bf16[64,512]{1,0:T(8,128)(2,1)}), bf16[1024,512]{1,0:T(8,128)(2,1)}) %all-gather.3.cloned.1.call-update) | async-done | bytes 1048592 | tf_op jit(solution)/shard_map/all_gather | solution.py:61
  84.8 4.5 %collective-permute-start = (bf16[16,256]{1,0:T(8,128)(2,1)S(1)}, bf16[16,256]{1,0:T(8,128)(2,1)S(1)}, u32[]{:S(2)}, u32[]{:S(2)}) collective-permute-start(bf16[16,256]{1,0:T(8,128)(2,1)S(1)} %fusion.73), channel_id=1, source_target_pairs={{16,0},{32,16},{48,32},{64,48},{80,64},{96,80},{112,96},{128,112},... | collective-permute-start | bytes 24584 | tf_op jit(solution)/shard_map/ppermute | solution.py:21
  90.3 2.1 copy.45
  92.4 7.9 %all-to-all-start = ((bf16[16,2,16384]{2,1,0:T(2,128)(2,1)}), bf16[16,2,16384]{2,1,0:T(2,128)(2,1)}, u32[]{:S(2)}, u32[]{:S(2)}) async-start(bf16[16,2,16384]{2,1,0:T(2,128)(2,1)} %copy.45), calls=%async_computation | async-start | bytes 2097152 | tf_op jit(solution)/shard_map/all_to_all | solution.py:152
  100.3 4.9 %collective-permute-start.1 = (bf16[512,256]{1,0:T(8,128)(2,1)}, bf16[512,256]{1,0:T(8,128)(2,1)}, u32[]{:S(2)}, u32[]{:S(2)}) collective-permute-start(bf16[512,256]{1,0:T(8,128)(2,1)} %fusion.67), channel_id=1, source_target_pairs={{0,16},{16,32},{32,48},{48,64},{64,80},{80,96},{96,112},{112,128},... | collective-permute-start | bytes 786440 | tf_op jit(solution)/shard_map/ppermute | solution.py:21
  105.5 56.8 %all_gather.11 = bf16[1024,256]{1,0:T(8,128)(2,1)S(1)} all-gather(bf16[64,256]{1,0:T(8,128)(2,1)S(1)} %add_convert_fusion), channel_id=1, replica_groups=mesh['ctx'=16,'head'=16] {'ctx'}, dimensions={0}, use_global_device_ids=true | all-gather | bytes 557056 | tf_op jit(solution)/shard_map/all_gather | solution.py:94
  163.7 40.8 %while.135 = (s32[]{:T(128)}, f32[4,1024]{1,0:T(4,128)S(1)}, f32[4,1024]{1,0:T(4,128)S(1)}, f32[4,1024,128]{2,1,0:T(8,128)}, bf16[2,512,256]{2,1,0:T(8,128)(2,1)...) while((s32[]{:T(128)}, f32[4,1024]{1,0:T(4,128)S(1)}, ...), condition=%wide.region_7.8_spmd.clone, body=%wide.region_2.7_spmd.clone.sunk | while | flops 276044288 | bytes 9548170 | solution.py:105
  165.1 19.0 %while.139 = (s32[]{:T(128)}, f32[4,1024]{1,0:T(4,128)S(1)}, f32[4,1024]{1,0:T(4,128)S(1)}, f32[4,1024,128]{2,1,0:T(8,128)}, bf16[4,1024,128]{2,1,0:T(8,128)(2,1...) while((s32[]{:T(128)}, f32[4,1024]{1,0:T(4,128)S(1)}, ...), condition=%wide.region_6.6_spmd.clone.clone, body=%wide.region_3.5_spmd.clone.clone.sunk | while | flops 276041728 | bytes 9017481 | solution.py:46
  185.5 19.0 %while.139 = (s32[]{:T(128)}, f32[4,1024]{1,0:T(4,128)S(1)}, f32[4,1024]{1,0:T(4,128)S(1)}, f32[4,1024,128]{2,1,0:T(8,128)}, bf16[4,1024,128]{2,1,0:T(8,128)(2,1...) while((s32[]{:T(128)}, f32[4,1024]{1,0:T(4,128)S(1)}, ...), condition=%wide.region_6.6_spmd.clone.clone, body=%wide.region_3.5_spmd.clone.clone.sunk | while | flops 276041728 | bytes 9017481 | solution.py:46
  205.6 49.2 %while.133 = (s32[]{:T(128)}, f32[2,4,512,128]{3,2,1,0:T(8,128)}, s32[2]{0:T(128)S(1)}, bf16[4,1024,128]{2,1,0:T(8,128)(2,1)}, bf16[1536,256]{1,0:T(8,128)(2,1)S...) while((s32[]{:T(128)}, f32[2,4,512,128]{3,2,1,0:T(8,128)}, ...), condition=%wide.region_26.27_spmd, body=%wide.region_21.26_spmd.sunk | while | flops 280826368 | bytes 17762856 | solution.py:128
  206.9 1.9 constant_dynamic-slice_fusion.14
  209.6 19.2 %while.138 = (s32[]{:T(128)}, f32[4,512]{1,0:T(4,128)S(1)}, f32[4,512,128]{2,1,0:T(8,128)S(1)}, bf16[4,512,128]{2,1,0:T(8,128)(2,1)}, bf16[1024,256]{1,0:T(8,128...) while((s32[]{:T(128)}, f32[4,512]{1,0:T(4,128)S(1)}, ...), condition=%wide.region_25.25_spmd.clone, body=%wide.region_22.24_spmd.clone.sunk | while | flops 280560128 | bytes 7259265 | solution.py:46
  212.6 1.9 fusion.107
  217.4 1.9 fusion.107
  222.2 1.9 fusion.107
  227.0 1.9 fusion.107
  231.4 1.9 constant_dynamic-slice_fusion.14
  234.2 19.2 %while.138 = (s32[]{:T(128)}, f32[4,512]{1,0:T(4,128)S(1)}, f32[4,512,128]{2,1,0:T(8,128)S(1)}, bf16[4,512,128]{2,1,0:T(8,128)(2,1)}, bf16[1024,256]{1,0:T(8,128...) while((s32[]{:T(128)}, f32[4,512]{1,0:T(4,128)S(1)}, ...), condition=%wide.region_25.25_spmd.clone, body=%wide.region_22.24_spmd.clone.sunk | while | flops 280560128 | bytes 7259265 | solution.py:46
  237.1 1.9 fusion.107
  242.0 1.9 fusion.107
  246.8 1.9 fusion.107
  251.6 1.9 fusion.107
  254.8 3.1 copy.52
  257.9 2.5 reshape.241
  260.5 86.8 %while.137 = (s32[]{:T(128)}, f32[4,4,256]{2,0,1:T(4,128)S(1)}, f32[4,4,256,128]{3,2,0,1:T(8,128)}, bf16[4,4,256,128]{3,2,0,1:T(8,128)(2,1)}, s32[4,16]{1,0:T(4,...) while((s32[]{:T(128)}, f32[4,4,256]{2,0,1:T(4,128)S(1)}, ...), condition=%wide.wide.region_20.21_spmd.clone, body=%wide.wide.region_14.20_spmd.clone.sunk | while | flops 276336640 | bytes 9205774 | solution.py:170
  263.8 17.5 %while.140 = (s32[]{:T(128)}, f32[4,256]{1,0:T(4,128)S(1)}, f32[4,256,128]{2,1,0:T(8,128)S(1)}, bf16[4,256,128]{2,1,0:T(8,128)(2,1)S(1)}, bf16[2048,256]{1,0:T(8...) while((s32[]{:T(128)}, f32[4,256]{1,0:T(4,128)S(1)}, ...), condition=%wide.region_19.19_spmd.clone, body=%wide.region_16.18_spmd.clone.sunk | while | flops 276333312 | bytes 7583865 | solution.py:46
  285.5 17.5 %while.140 = (s32[]{:T(128)}, f32[4,256]{1,0:T(4,128)S(1)}, f32[4,256,128]{2,1,0:T(8,128)S(1)}, bf16[4,256,128]{2,1,0:T(8,128)(2,1)S(1)}, bf16[2048,256]{1,0:T(8...) while((s32[]{:T(128)}, f32[4,256]{1,0:T(4,128)S(1)}, ...), condition=%wide.region_19.19_spmd.clone, body=%wide.region_16.18_spmd.clone.sunk | while | flops 276333312 | bytes 7583865 | solution.py:46
  307.1 17.5 %while.140 = (s32[]{:T(128)}, f32[4,256]{1,0:T(4,128)S(1)}, f32[4,256,128]{2,1,0:T(8,128)S(1)}, bf16[4,256,128]{2,1,0:T(8,128)(2,1)S(1)}, bf16[2048,256]{1,0:T(8...) while((s32[]{:T(128)}, f32[4,256]{1,0:T(4,128)S(1)}, ...), condition=%wide.region_19.19_spmd.clone, body=%wide.region_16.18_spmd.clone.sunk | while | flops 276333312 | bytes 7583865 | solution.py:46
  328.8 17.5 %while.140 = (s32[]{:T(128)}, f32[4,256]{1,0:T(4,128)S(1)}, f32[4,256,128]{2,1,0:T(8,128)S(1)}, bf16[4,256,128]{2,1,0:T(8,128)(2,1)S(1)}, bf16[2048,256]{1,0:T(8...) while((s32[]{:T(128)}, f32[4,256]{1,0:T(4,128)S(1)}, ...), condition=%wide.region_19.19_spmd.clone, body=%wide.region_16.18_spmd.clone.sunk | while | flops 276333312 | bytes 7583865 | solution.py:46
  347.3 2.1 broadcast_divide_fusion
  350.1 2.8 fusion.64
  (379 shorter events, 170.7 us)
Async XLA Ops:
  6.5 40.0 %all-gather.5.cloned.1.call-start = ((), (), s32[]{:S(2)}) async-start(), calls=%async_computation.2 | async-start | bytes 1114112 | tf_op jit(solution)/shard_map/all_gather | solution.py:62
  7.3 75.9 %all-gather.3.cloned.1.call-start = ((), (), s32[]{:S(2)}) async-start(), calls=%async_computation.1 | async-start | bytes 1114112 | tf_op jit(solution)/shard_map/all_gather | solution.py:61
  8.1 2.8 copy-start.10
  8.1 7.9 %copy-start.9 = (f32[3,4,1024]{2,1,0:T(4,128)S(1)}, f32[3,4,1024]{2,1,0:T(4,128)}, u32[]{:S(2)}) copy-start(f32[3,4,1024]{2,1,0:T(4,128)} %param.24) | copy-start | bytes 147460
  11.0 0.5 copy-start.14
  12.4 2.9 copy-start.11
  84.8 20.5 %collective-permute-start = (bf16[16,256]{1,0:T(8,128)(2,1)S(1)}, bf16[16,256]{1,0:T(8,128)(2,1)S(1)}, u32[]{:S(2)}, u32[]{:S(2)}) collective-permute-start(bf16[16,256]{1,0:T(8,128)(2,1)S(1)} %fusion.73), channel_id=1, source_target_pairs={{16,0},{32,16},{48,32},{64,48},{80,64},{96,80},{112,96},{128,112},... | collective-permute-start | bytes 24584 | tf_op jit(solution)/shard_map/ppermute | solution.py:21
  92.4 165.5 %all-to-all-start = ((bf16[16,2,16384]{2,1,0:T(2,128)(2,1)}), bf16[16,2,16384]{2,1,0:T(2,128)(2,1)}, u32[]{:S(2)}, u32[]{:S(2)}) async-start(bf16[16,2,16384]{2,1,0:T(2,128)(2,1)} %copy.45), calls=%async_computation | async-start | bytes 2097152 | tf_op jit(solution)/shard_map/all_to_all | solution.py:152
  100.3 104.2 %collective-permute-start.1 = (bf16[512,256]{1,0:T(8,128)(2,1)}, bf16[512,256]{1,0:T(8,128)(2,1)}, u32[]{:S(2)}, u32[]{:S(2)}) collective-permute-start(bf16[512,256]{1,0:T(8,128)(2,1)} %fusion.67), channel_id=1, source_target_pairs={{0,16},{16,32},{32,48},{48,64},{64,80},{80,96},{96,112},{112,128},... | collective-permute-start | bytes 786440 | tf_op jit(solution)/shard_map/ppermute | solution.py:21
  204.5 1.1 copy-start.4
  205.6 4.0 %copy-start.1 = (bf16[1536,256]{1,0:T(8,128)(2,1)}, bf16[1536,256]{1,0:T(8,128)(2,1)S(1)}, u32[]{:S(2)}) copy-start(bf16[1536,256]{1,0:T(8,128)(2,1)S(1)} %get-tuple-element.1592) | copy-start | bytes 2359300 | tf_op jit(solution)/shard_map/while
  228.9 1.4 copy-start.2
  230.2 4.0 %copy-start.1 = (bf16[1536,256]{1,0:T(8,128)(2,1)}, bf16[1536,256]{1,0:T(8,128)(2,1)S(1)}, u32[]{:S(2)}) copy-start(bf16[1536,256]{1,0:T(8,128)(2,1)S(1)} %get-tuple-element.1592) | copy-start | bytes 2359300 | tf_op jit(solution)/shard_map/while
  253.5 1.3 copy-start.2
  257.9 2.6 copy-start.12
  257.9 2.6 copy-start.13
  257.9 2.6 copy-start.15
  257.9 2.6 copy-start.16
  260.4 88.9 %copy-start.6 = (f32[4,1024]{1,0:T(4,128)S(1)}, f32[4,1024]{1,0:T(4,128)}, u32[]{:S(2)}) copy-start(f32[4,1024]{1,0:T(4,128)} %get-tuple-element.952) | copy-start | bytes 49156
  260.5 88.9 %copy-start.7 = (f32[4,1024]{1,0:T(4,128)S(1)}, f32[4,1024]{1,0:T(4,128)}, u32[]{:S(2)}) copy-start(f32[4,1024]{1,0:T(4,128)} %get-tuple-element.953) | copy-start | bytes 49156
  260.5 88.9 %copy-start.8 = (f32[4,1024]{1,0:T(4,128)S(1)}, f32[4,1024]{1,0:T(4,128)}, u32[]{:S(2)}) copy-start(f32[4,1024]{1,0:T(4,128)} %get-tuple-element.954) | copy-start | bytes 49156
  347.3 2.2 copy-start
  347.3 2.9 copy-start.3
  347.3 2.9 copy-start.5
Sparse Core Ops, SparseCore 0:
  9.2 37.3 all-gather.4
  48.4 34.7 all-gather.2
where the time goes:
time: 368 us; the launch traced here: 362 us
  matrix products  110 us (30%)
  waiting for transfers between devices  67 us (18%)
  blocking collectives  56.8 us (15%)
  local copies, waits for them, and re-layouts  53.5 us (15%)
  other arithmetic  37 us (10%)
  starting transfers between devices  17.3 us (5%)
  between operations  13.7 us (4%)
  loops' own time  6.32 us (2%)
    all_gather x1, blocking collectives, local(): shard_rows = lax.all_gather(compressed, 'ctx', axis=0, tiled=True)  56.8 us
    dot_general x32, matrix products, online_step(): jnp.dot(weights.astype(jnp.bfloat16), block_kv[:, HD:], preferred_element...  55.7 us
    dot_general x32, matrix products, online_step(): jnp.einsum('qd,kd->qk', query_head, block_kv[:, :HD], preferred_element_t...  53.9 us
    all_gather x1, waiting for transfers between devices, local(): lax.all_gather(keys, 'head', axis=0, tiled=True)  35.7 us
    all_gather x1, waiting for transfers between devices, local(): lax.all_gather(values, 'head', axis=0, tiled=True)  29.9 us
    reduce_sum x32, other arithmetic, online_step(): running_sum = running_sum * shrink + jnp.sum(weights, axis=-1)  24.2 us
    ppermute x2, starting transfers between devices, shifted(): return lax.ppermute(block, axis, route)  9.32 us
    dynamic_slice x16, local copies, waits for them, and re-layouts, heads_step(): return lax.map(per_head, (folded[0], folded[1], folded[2], query_heads))  8.75 us
  transfers between devices with their start and end apart: 5, of which 2 were waited for; matrix products, arithmetic and copies ran while one was open for 29% of the time, Pallas kernels for 0%

commit v1 on v0

v1 whole, which is shorter than its diff:
```python
import functools

import jax
import jax.numpy as jnp
from jax import lax
from jax.experimental import pallas as pl
from jax.experimental.pallas import tpu as pltpu
from jax.sharding import PartitionSpec as P

H = 64
G = 4
HD = 128
KERN = 32
STRIDE = 16
TILE = 64
TOPK = 16
WIN = 512
QB = 256
CAP = 2
BIG = 1 << 30


def shifted(block, axis, distance):
    devices = range(lax.axis_size(axis))
    route = [(i - distance, i) for i in devices if i - distance in devices]
    return lax.ppermute(block, axis, route)


def branch_kernel(q_ref, kv_ref, lo_ref, hi_ref, t_ref, g_ref, *rest, sink, key_rows, row_step, heads):
    if len(rest) == 2:
        acc_ref, o_ref = rest
    else:
        acc_ref = None
        (o_ref,) = rest
    block = pl.program_id(0)
    if row_step:
        start = pl.multiple_of(block * row_step, row_step)
        kv = kv_ref[pl.ds(start, key_rows), :]
    else:
        kv = kv_ref[...]
    keys = kv[:, :HD]
    vals = kv[:, HD:]
    lo = lo_ref[0]
    hi = hi_ref[0]
    t = t_ref[...]
    allowed = (lo <= t) & (t < hi)
    for h in range(heads):
        q = q_ref[:, h * HD : (h + 1) * HD]
        s = lax.dot_general(
            q, keys, (((1,), (1,)), ((), ())), preferred_element_type=jnp.float32
        ) * HD ** (-0.5)
        m = jnp.max(jnp.where(allowed, s, -jnp.inf), axis=1, keepdims=True)
        if sink:
            m = jnp.maximum(m, 0.0)
        p = jnp.where(allowed, jnp.exp(s - m), 0.0)
        l = jnp.sum(p, axis=1, keepdims=True)
        if sink:
            l = l + jnp.exp(-m)
        o = jnp.dot(p.astype(jnp.bfloat16), vals, preferred_element_type=jnp.float32) / l
        r = g_ref[:, h : h + 1] * o
        if acc_ref is not None:
            r = acc_ref[:, h * HD : (h + 1) * HD] + r
        o_ref[:, h * HD : (h + 1) * HD] = r.astype(o_ref.dtype)


def branch(q, kv, lo, hi, t, gate, acc, *, sink, key_rows, row_step, out_dtype):
    rows, width = q.shape
    heads = width // HD
    blocks = rows // QB
    lo_map = (lambda i: (i, 0, 0)) if lo.shape[0] > 1 else (lambda i: (0, 0, 0))
    hi_map = (lambda i: (i, 0, 0)) if hi.shape[0] > 1 else (lambda i: (0, 0, 0))
    in_specs = [
        pl.BlockSpec((QB, width), lambda i: (i, 0)),
        pl.BlockSpec(kv.shape, lambda i: (0, 0)),
        pl.BlockSpec((1,) + lo.shape[1:], lo_map),
        pl.BlockSpec((1,) + hi.shape[1:], hi_map),
        pl.BlockSpec((QB, 1), lambda i: (i, 0)),
        pl.BlockSpec((QB, gate.shape[1]), lambda i: (i, 0)),
    ]
    args = [q, kv, lo, hi, t, gate]
    aliases = {}
    if acc is not None:
        in_specs.append(pl.BlockSpec((QB, width), lambda i: (i, 0)))
        args.append(acc)
        if acc.dtype == out_dtype:
            aliases = {len(args) - 1: 0}
    kernel = functools.partial(
        branch_kernel, sink=sink, key_rows=key_rows, row_step=row_step, heads=heads
    )
    flops = 4 * rows * heads * key_rows * HD
    cost = pl.CostEstimate(
        flops=flops,
        transcendentals=rows * heads * key_rows,
        bytes_accessed=q.size * 2 + kv.size * 2 + rows * width * 8,
    )
    return pl.pallas_call(
        kernel,
        grid=(blocks,),
        in_specs=in_specs,
        out_specs=pl.BlockSpec((QB, width), lambda i: (i, 0)),
        out_shape=jax.ShapeDtypeStruct((rows, width), out_dtype),
        input_output_aliases=aliases,
        compiler_params=pltpu.CompilerParams(
            dimension_semantics=("arbitrary",), vmem_limit_bytes=48 * 1024 * 1024
        ),
        cost_estimate=cost,
    )(*args)


def local(queries, keys, values, comp_k_weight, comp_v_weight, gate_logits, sel_tiles):
    ctx_count = lax.axis_size("ctx")
    head_count = lax.axis_size("head")
    ctx_index = lax.axis_index("ctx")
    head_index = lax.axis_index("head")
    local_rows = queries.shape[0]
    local_heads = queries.shape[1] // HD
    group_index = head_index * local_heads // (H // G)
    dev_rows = keys.shape[0]
    kv_rows = jnp.concatenate(
        [keys.reshape(dev_rows, G, HD), values.reshape(dev_rows, G, HD)], axis=2
    ).transpose(1, 0, 2)
    dest_group = jnp.arange(head_count) * local_heads // (H // G)
    outbox_kv = kv_rows[dest_group]
    group_kv = lax.all_to_all(outbox_kv, "head", 0, 0, tiled=True).reshape(
        local_rows, 2 * HD
    )
    tail_rows = shifted(group_kv[: KERN - STRIDE], "ctx", -1)
    extended = jnp.concatenate([group_kv, tail_rows], axis=0)
    comp_weight = jnp.concatenate(
        [
            lax.dynamic_slice_in_dim(comp_k_weight, group_index * HD, HD, 1),
            lax.dynamic_slice_in_dim(comp_v_weight, group_index * HD, HD, 1),
        ],
        axis=1,
    )
    comp_local = local_rows // STRIDE
    first_half = extended[:local_rows].reshape(comp_local, STRIDE, 2 * HD).astype(jnp.float32)
    second_half = (
        extended[STRIDE : STRIDE + local_rows]
        .reshape(comp_local, STRIDE, 2 * HD)
        .astype(jnp.float32)
    )
    compressed = (
        jnp.sum(first_half * comp_weight[None, :STRIDE], 1)
        + jnp.sum(second_half * comp_weight[None, STRIDE:], 1)
    ).astype(jnp.bfloat16)
    comp_kv = lax.all_gather(compressed, "ctx", axis=0, tiled=True)
    comp_count = comp_kv.shape[0]
    previous = shifted(group_kv[local_rows - WIN :], "ctx", 1)
    window_kv = jnp.concatenate([previous, group_kv], axis=0)

    block_count = local_rows // QB
    tiles_shard = local_rows // TILE
    group_tiles = lax.dynamic_slice_in_dim(sel_tiles, group_index * TOPK, TOPK, 1)
    own_tiles = lax.dynamic_slice_in_dim(group_tiles, ctx_index * block_count, block_count, 0)
    own_flat = own_tiles.reshape(-1)
    requests = group_tiles.reshape(ctx_count, block_count * TOPK)
    local_ids = ctx_index * tiles_shard + jnp.arange(tiles_shard)
    present = jnp.any(requests[:, :, None] == local_ids[None, None, :], axis=1)
    order_rank = jnp.cumsum(present.astype(jnp.int32), axis=1) - 1
    picked = present[:, None, :] & (order_rank[:, None, :] == jnp.arange(CAP)[None, :, None])
    outbox = jnp.einsum(
        "dct,tx->dcx",
        picked.astype(jnp.bfloat16),
        group_kv.reshape(tiles_shard, TILE * 2 * HD),
        preferred_element_type=jnp.float32,
    ).astype(jnp.bfloat16)
    received = lax.all_to_all(outbox, "ctx", split_axis=0, concat_axis=0, tiled=True)
    all_ids = jnp.arange(ctx_count * tiles_shard).reshape(ctx_count, tiles_shard)
    wanted = jnp.any(own_flat[:, None, None] == all_ids[None, :, :], axis=0)
    wanted_rank = jnp.cumsum(wanted.astype(jnp.int32), axis=1) - 1
    chosen = wanted[:, None, :] & (wanted_rank[:, None, :] == jnp.arange(CAP)[None, :, None])
    slot_tile = jnp.sum(jnp.where(chosen, all_ids[:, None, :], 0), axis=2).reshape(-1)
    slot_ok = jnp.any(chosen, axis=2).reshape(-1)
    sel_kv = received.reshape(ctx_count * CAP * TILE, 2 * HD)
    sel_rows = sel_kv.shape[0]
    key_pos = (slot_tile[:, None] * TILE + jnp.arange(TILE)[None, :]).reshape(-1)
    is_named = slot_ok[None, :] & jnp.any(
        own_tiles[:, :, None] == slot_tile[None, None, :], axis=1
    )
    sel_lo = jnp.where(jnp.repeat(is_named, TILE, axis=1), key_pos[None, :], BIG).reshape(
        block_count, 1, sel_rows
    )
    never = jnp.full((1, 1, sel_rows), BIG, jnp.int32)

    comp_lo = (jnp.arange(comp_count, dtype=jnp.int32) * STRIDE + KERN - 1).reshape(
        1, 1, comp_count
    )
    comp_hi = jnp.full((1, 1, comp_count), BIG, jnp.int32)

    win_rows = QB + WIN
    win_pos = (
        ctx_index * local_rows
        - WIN
        + jnp.arange(block_count)[:, None] * QB
        + jnp.arange(win_rows)[None, :]
    )
    win_lo = jnp.where(win_pos >= 0, win_pos, BIG).reshape(block_count, 1, win_rows)
    win_hi = (win_pos + WIN).reshape(block_count, 1, win_rows)

    positions = (ctx_index * local_rows + jnp.arange(local_rows, dtype=jnp.int32)).reshape(
        local_rows, 1
    )
    gate_values = jax.nn.sigmoid(gate_logits).transpose(0, 2, 1)

    acc = branch(
        queries, window_kv, win_lo, win_hi, positions, gate_values[2], None,
        sink=False, key_rows=win_rows, row_step=QB, out_dtype=jnp.float32,
    )
    acc = branch(
        queries, comp_kv, comp_lo, comp_hi, positions, gate_values[0], acc,
        sink=True, key_rows=comp_count, row_step=0, out_dtype=jnp.float32,
    )
    return branch(
        queries, sel_kv, sel_lo, never, positions, gate_values[1], acc,
        sink=True, key_rows=sel_rows, row_step=0, out_dtype=jnp.bfloat16,
    )


def solution(mesh):
    placed = (
        P("ctx", "head"),
        P(("ctx", "head"), None),
        P(("ctx", "head"), None),
        P(),
        P(),
        P(None, "head", "ctx"),
        P(),
    )
    return jax.shard_map(
        local, mesh=mesh, in_specs=placed, out_specs=P("ctx", "head"), check_vma=False
    )
```

time: 368 us -> 147 us (0.40)
  matrix products: 110 us -> 0.41 us
  waiting for transfers between devices: 67 us -> 17.5 us
  Pallas kernels: 0 us -> 41 us
  local copies, waits for them, and re-layouts: 53.5 us -> 14.9 us
  other arithmetic: 37 us -> 3.94 us
  blocking collectives: 56.8 us -> 42.5 us
  between operations: 13.7 us -> 0.33 us
  loops' own time: 6.32 us -> 0 us
  starting transfers between devices: 17.3 us -> 23.6 us
    dot_general x64 -> x0, matrix products: 110 us -> none  [the longest x32 55.7 us: online_step(): jnp.dot(weights.astype(jnp.bfloat16), block_kv[:, HD:], preferred_element...]
    all_gather x2 -> x0, waiting for transfers between devices: 65.6 us -> none  [the longest x1 35.7 us: local(): lax.all_gather(keys, 'head', axis=0, tiled=True)]
    pallas_call x0 -> x3, Pallas kernels: none -> 41 us  [branch(): pl.pallas_call(kernel, grid=(blocks,), in_specs=in_specs, out_specs=pl.Bl...]
    reduce_sum x32 -> x0, other arithmetic: 24.2 us -> none  [online_step(): running_sum = running_sum * shrink + jnp.sum(weights, axis=-1)]
    dynamic_slice x30 -> x0, local copies, waits for them, and re-layouts: 21.2 us -> none  [the longest x16 8.75 us: heads_step(): return lax.map(per_head, (folded[0], folded[1], folded[2], query_heads))]
    all_gather x1, blocking collectives: 56.8 us -> 42.5 us  [local(): comp_kv = lax.all_gather(compressed, 'ctx', axis=0, tiled=True)]
    ppermute x2, waiting for transfers between devices: 0.01 us -> 13.5 us  [shifted(): return lax.ppermute(block, axis, route)]
    another operation x11 -> x0, loops' own time: 6.32 us -> none  [the longest x1 2.68 us: local(): lax.map(per_block, (sel_init[0], sel_init[1], sel_init[2], query_blocks,...]
  transfers between devices with their start and end apart: 5 -> 4, of which waited for: 2 -> 2; matrix products, arithmetic and copies ran while one was open for 29% -> 5% of each run, Pallas kernels for 0% -> 14%
where the time goes in v1:
time: 147 us; the launch traced here: 144 us
  blocking collectives  42.5 us (29%)
  Pallas kernels  41 us (28%)
  starting transfers between devices  23.6 us (16%)
  waiting for transfers between devices  17.5 us (12%)
  local copies, waits for them, and re-layouts  14.9 us (10%)
  other arithmetic  3.94 us (3%)
    all_gather x1, blocking collectives, local(): comp_kv = lax.all_gather(compressed, 'ctx', axis=0, tiled=True)  42.5 us
    pallas_call x3, Pallas kernels, branch(): pl.pallas_call(kernel, grid=(blocks,), in_specs=in_specs, out_specs=pl.Bl...  41 us
    ppermute x2, waiting for transfers between devices, shifted(): return lax.ppermute(block, axis, route)  13.5 us
    all_to_all x1, starting transfers between devices, local(): lax.all_to_all(outbox, 'ctx', split_axis=0, concat_axis=0, tiled=True)  10.7 us
    ppermute x2, starting transfers between devices, shifted(): return lax.ppermute(block, axis, route)  7.35 us
    all_to_all x1, starting transfers between devices, local(): lax.all_to_all(outbox_kv, 'head', 0, 0, tiled=True)  5.5 us
    unnamed x15, local copies, waits for them, and re-layouts  5.47 us
    all_to_all x1, waiting for transfers between devices, local(): lax.all_to_all(outbox_kv, 'head', 0, 0, tiled=True)  4 us
  transfers between devices with their start and end apart: 4, of which 2 were waited for; matrix products, arithmetic and copies ran while one was open for 5% of the time, Pallas kernels for 14%

profile of v1, /device:TPU:32, one launch (start us, length us, event | category | flops | bytes accessed | tf_op | source)
XLA Modules:
  0.0 144.1 jit_solution(571577699230577749)
XLA Ops:
  0.0 0.8 copy-done
  0.8 0.9 copy_bitcast_fusion
  1.7 1.4 gather_fusion
  3.1 5.5 %all-to-all-start = ((bf16[16,64,256]{2,1,0:T(8,128)(2,1)}), bf16[16,64,256]{2,1,0:T(8,128)(2,1)S(1)}, u32[]{:S(2)}, u32[]{:S(2)}) async-start(bf16[16,64,256]{2,1,0:T(8,128)(2,1)} %gather_fusion), calls=%async_computation | async-start | bytes 1048576 | tf_op jit(solution)/shard_map/all_to_all | solution.py:124
  8.9 0.4 compare_reduce_fusion
  9.4 0.2 reduce_window_sum.18
  9.5 0.1 select_reduce_fusion
  9.7 0.1 fusion.6
  10.2 0.5 copy.37
  10.7 1.6 %divide_bitcast_fusion = f32[3,1024,4]{2,1,0:T(8,128)} fusion(f32[3,4,1024]{1,2,0:T(8,128)S(1)} %copy.37), kind=kLoop, calls=%fused_computation.2 | loop fusion | flops 36864 | bytes 98304 | tf_op jit(solution)/shard_map/transpose | solution.py:204
  12.3 0.4 compare_reduce_fusion.1
  12.8 0.2 reduce_window_sum.17
  13.2 0.7 constant_dynamic-slice_fusion
  14.0 1.5 %slice_bitcast_fusion = (f32[1024,4]{1,0:T(8,128)S(1)}, f32[1024,4]{1,0:T(8,128)S(1)}, f32[1024,4]{1,0:T(8,128)S(1)}) fusion(f32[3,1024,4]{2,1,0:T(8,128)} %divide_bitcast_fusion), kind=kLoop, calls=%fused_computation.8 | loop fusion | bytes 98304 | tf_op jit(solution)/shard_map/squeeze | solution.py:207
  15.4 4.0 %all-to-all-done = bf16[16,64,256]{2,1,0:T(8,128)(2,1)S(1)} async-done(((bf16[16,64,256]{2,1,0:T(8,128)(2,1)}), bf16[16,64,256]{2,1,0:T(8,128)(2,1)S(1)}, u32[]{:S(2)}, u32[]{:S(2)}) %all-to-all-start) | async-done | bytes 524320 | tf_op jit(solution)/shard_map/all_to_all | solution.py:124
  19.4 0.2 reshape.286
  19.7 0.4 convolution_convert_fusion
  20.1 2.1 %copy.33 = bf16[16,2,16384]{2,1,0:T(2,128)(2,1)} copy(bf16[16,2,16384]{2,0,1:T(8,128)(2,1)S(1)} %convolution_convert_fusion) | data formatting | bytes 2097152 | tf_op jit(solution)/shard_map/convert_element_type | solution.py:167
  22.2 10.7 %all-to-all-start.1 = ((bf16[16,2,16384]{2,1,0:T(2,128)(2,1)}), bf16[16,2,16384]{2,1,0:T(2,128)(2,1)}, u32[]{:S(2)}, u32[]{:S(2)}) async-start(bf16[16,2,16384]{2,1,0:T(2,128)(2,1)} %copy.33), calls=%async_computation.1 | async-start | bytes 2097152 | tf_op jit(solution)/shard_map/all_to_all | solution.py:168
  33.3 4.9 %collective-permute-start = (bf16[16,256]{1,0:T(8,128)(2,1)S(1)}, bf16[16,256]{1,0:T(8,128)(2,1)S(1)}, u32[]{:S(2)}, u32[]{:S(2)}) collective-permute-start(bf16[16,256]{1,0:T(8,128)(2,1)S(1)} %slice.41), channel_id=1, source_target_pairs={{16,0},{32,16},{48,32},{64,48},{80,64},{96,80},{112,96},{128,112},... | collective-permute-start | bytes 24584 | tf_op jit(solution)/shard_map/ppermute | solution.py:26
  38.2 2.5 %collective-permute-start.1 = (bf16[512,256]{1,0:T(8,128)(2,1)S(1)}, bf16[512,256]{1,0:T(8,128)(2,1)S(1)}, u32[]{:S(2)}, u32[]{:S(2)}) collective-permute-start(bf16[512,256]{1,0:T(8,128)(2,1)S(1)} %bitcast.34), channel_id=1, source_target_pairs={{0,16},{16,32},{32,48},{48,64},{64,80},{80,96},{96,112},{112,128},... | collective-permute-start | bytes 786440 | tf_op jit(solution)/shard_map/ppermute | solution.py:26
  40.7 0.2 fusion.1
  40.9 13.5 %collective-permute-done = bf16[16,256]{1,0:T(8,128)(2,1)S(1)} collective-permute-done((bf16[16,256]{1,0:T(8,128)(2,1)S(1)}, bf16[16,256]{1,0:T(8,128)(2,1)S(1)}, u32[]{:S(2)}, u32[]{:S(2)}) %collective-permute-start) | collective-permute-done | bytes 8224 | tf_op jit(solution)/shard_map/ppermute | solution.py:26
  54.4 0.2 fusion
  54.7 42.5 %all_gather.3.kv_ref = bf16[1024,256]{1,0:T(8,128)(2,1)S(1)} all-gather(bf16[64,256]{1,0:T(8,128)(2,1)S(1)} %add_convert_fusion), channel_id=1, replica_groups=mesh['ctx'=16,'head'=16] {'ctx'}, dimensions={0}, use_global_device_ids=true | all-gather | bytes 557056 | tf_op jit(solution)/shard_map/all_gather | solution.py:147
  97.2 9.0 %shard_map.73.rest_0_ = f32[1024,512]{1,0:T(8,128)S(1)} custom-call(bf16[1024,512]{1,0:T(8,128)(2,1)S(1)} %copy-done.1, bf16[1536,256]{1,0:T(8,128)(2,1)S(1)} %pad_maximum_fusion.kv_ref, s32[4,1,768]{2,1,0:T(1,128)S(1)} %get-tuple-element.11.lo_ref, s32[4,1,768]{2,1,0:T(1,128)S(1)} %get-tuple-element.10.hi_ref, s32[1024,1]{1,0:T(8,128)S(1)} %iota_add_fusion.t_ref, ...), custom_call_target="tpu_custom_call" | custom-call | flops 1610612736 | bytes 6029312 | tf_op jit(solution)/shard_map/pallas_call | solution.py:96
  106.2 11.0 %shard_map.74.rest_0_ = f32[1024,512]{1,0:T(8,128)S(1)} custom-call(bf16[1024,512]{1,0:T(8,128)(2,1)S(1)} %copy-done.1, bf16[1024,256]{1,0:T(8,128)(2,1)S(1)} %all_gather.3.kv_ref, s32[1,1,1024]{2,1,0:T(1,128)S(1)} %multiply_add_fusion.1.lo_ref, s32[1,1,1024]{2,1,0:T(1,128)S(1)} %broadcast_in_dim.57.hi_ref, ...), custom_call_target="tpu_custom_call", output_to_operand_aliasing={{}: (6, {})} | custom-call | flops 2147483648 | bytes 5767168 | tf_op jit(solution)/shard_map/pallas_call | solution.py:96
  117.3 1.3 copy-done.3
  118.6 1.7 %reshape.273.kv_ref = bf16[2048,256]{1,0:T(8,128)(2,1)S(1)} reshape(bf16[16,2,16384]{2,1,0:T(2,128)(2,1)} %all-to-all-done.1) | data formatting | bytes 2097152 | tf_op jit(solution)/shard_map/reshape | solution.py:175
  120.4 1.2 copy-done.2
  121.6 1.6 %copy-done.4 = f32[1024,512]{1,0:T(8,128)S(1)} copy-done((f32[1024,512]{1,0:T(8,128)S(1)}, f32[1024,512]{1,0:T(8,128)}, u32[]{:S(2)}) %copy-start.4) | copy-done | bytes 2097176
  123.2 20.9 %shard_map.75 = bf16[1024,512]{1,0:T(8,128)(2,1)} custom-call(bf16[1024,512]{1,0:T(8,128)(2,1)S(1)} %copy-done.2, bf16[2048,256]{1,0:T(8,128)(2,1)S(1)} %reshape.273.kv_ref, s32[4,1,2048]{2,1,0:T(1,128)S(1)} %broadcast_select_fusion.lo_ref, s32[1,1,2048]{2,1,0:T(1,128)S(1)} %broadcast_in_dim.56.hi_ref, s32[1024,1]{1,0:T(8,128)S(1)} %iota_add_fusion.t_ref, ...), custom_call_target="tpu_custom_call" | custom-call | flops 4294967296 | bytes 6291456 | tf_op jit(solution)/shard_map/pallas_call | solution.py:96
  (48 shorter events, 1.5 us)
Async XLA Ops:
  0.0 0.8 copy-start
  0.0 8.7 %copy-start.6 = (s32[64,64]{1,0:T(8,128)S(1)}, s32[64,64]{1,0:T(8,128)}, u32[]{:S(2)}) copy-start(s32[64,64]{1,0:T(8,128)} %param.13) | copy-start | bytes 49156
  0.0 10.2 %copy-start.5 = (f32[3,4,1024]{2,1,0:T(4,128)S(1)}, f32[3,4,1024]{2,1,0:T(4,128)}, u32[]{:S(2)}) copy-start(f32[3,4,1024]{2,1,0:T(4,128)} %param.12) | copy-start | bytes 147460
  3.1 16.3 %all-to-all-start = ((bf16[16,64,256]{2,1,0:T(8,128)(2,1)}), bf16[16,64,256]{2,1,0:T(8,128)(2,1)S(1)}, u32[]{:S(2)}, u32[]{:S(2)}) async-start(bf16[16,64,256]{2,1,0:T(8,128)(2,1)} %gather_fusion), calls=%async_computation | async-start | bytes 1048576 | tf_op jit(solution)/shard_map/all_to_all | solution.py:124
  22.2 96.5 %all-to-all-start.1 = ((bf16[16,2,16384]{2,1,0:T(2,128)(2,1)}), bf16[16,2,16384]{2,1,0:T(2,128)(2,1)}, u32[]{:S(2)}, u32[]{:S(2)}) async-start(bf16[16,2,16384]{2,1,0:T(2,128)(2,1)} %copy.33), calls=%async_computation.1 | async-start | bytes 2097152 | tf_op jit(solution)/shard_map/all_to_all | solution.py:168
  33.3 21.1 %collective-permute-start = (bf16[16,256]{1,0:T(8,128)(2,1)S(1)}, bf16[16,256]{1,0:T(8,128)(2,1)S(1)}, u32[]{:S(2)}, u32[]{:S(2)}) collective-permute-start(bf16[16,256]{1,0:T(8,128)(2,1)S(1)} %slice.41), channel_id=1, source_target_pairs={{16,0},{32,16},{48,32},{64,48},{80,64},{96,80},{112,96},{128,112},... | collective-permute-start | bytes 24584 | tf_op jit(solution)/shard_map/ppermute | solution.py:26
  38.2 58.9 %collective-permute-start.1 = (bf16[512,256]{1,0:T(8,128)(2,1)S(1)}, bf16[512,256]{1,0:T(8,128)(2,1)S(1)}, u32[]{:S(2)}, u32[]{:S(2)}) collective-permute-start(bf16[512,256]{1,0:T(8,128)(2,1)S(1)} %bitcast.34), channel_id=1, source_target_pairs={{0,16},{16,32},{32,48},{48,64},{64,80},{80,96},{96,112},{112,128},... | collective-permute-start | bytes 786440 | tf_op jit(solution)/shard_map/ppermute | solution.py:26
  40.9 56.3 %copy-start.1 = (bf16[1024,512]{1,0:T(8,128)(2,1)S(1)}, bf16[1024,512]{1,0:T(8,128)(2,1)}, u32[]{:S(2)}) copy-start(bf16[1024,512]{1,0:T(8,128)(2,1)} %q_ref.5) | copy-start | bytes 3145732
  117.3 1.4 copy-start.3
  120.4 1.2 copy-start.2
  121.6 1.6 %copy-start.4 = (f32[1024,512]{1,0:T(8,128)S(1)}, f32[1024,512]{1,0:T(8,128)}, u32[]{:S(2)}) copy-start(f32[1024,512]{1,0:T(8,128)} %copy-done.3) | copy-start | bytes 6291460

commit v2 on v1

--- a/solution.py
+++ b/solution.py
@@ -43,16 +43,16 @@
     lo = lo_ref[0]
     hi = hi_ref[0]
     t = t_ref[...]
-    allowed = (lo <= t) & (t < hi)
+    bias = jnp.where((lo <= t) & (t < hi), 0.0, -jnp.inf)
     for h in range(heads):
         q = q_ref[:, h * HD : (h + 1) * HD]
         s = lax.dot_general(
             q, keys, (((1,), (1,)), ((), ())), preferred_element_type=jnp.float32
-        ) * HD ** (-0.5)
-        m = jnp.max(jnp.where(allowed, s, -jnp.inf), axis=1, keepdims=True)
+        ) * HD ** (-0.5) + bias
+        m = jnp.max(s, axis=1, keepdims=True)
         if sink:
             m = jnp.maximum(m, 0.0)
-        p = jnp.where(allowed, jnp.exp(s - m), 0.0)
+        p = jnp.exp(s - m)
         l = jnp.sum(p, axis=1, keepdims=True)
         if sink:
             l = l + jnp.exp(-m)
@@ -144,8 +144,6 @@
         jnp.sum(first_half * comp_weight[None, :STRIDE], 1)
         + jnp.sum(second_half * comp_weight[None, STRIDE:], 1)
     ).astype(jnp.bfloat16)
-    comp_kv = lax.all_gather(compressed, "ctx", axis=0, tiled=True)
-    comp_count = comp_kv.shape[0]
     previous = shifted(group_kv[local_rows - WIN :], "ctx", 1)
     window_kv = jnp.concatenate([previous, group_kv], axis=0)
 
@@ -165,7 +163,14 @@
         group_kv.reshape(tiles_shard, TILE * 2 * HD),
         preferred_element_type=jnp.float32,
     ).astype(jnp.bfloat16)
-    received = lax.all_to_all(outbox, "ctx", split_axis=0, concat_axis=0, tiled=True)
+    comp_slot = jnp.broadcast_to(
+        compressed.reshape(1, 1, comp_local * 2 * HD), (ctx_count, 1, comp_local * 2 * HD)
+    )
+    mail = jnp.concatenate([outbox, comp_slot], axis=1)
+    arrived = lax.all_to_all(mail, "ctx", split_axis=0, concat_axis=0, tiled=True)
+    received = arrived[:, :CAP]
+    comp_kv = arrived[:, CAP].reshape(ctx_count * comp_local, 2 * HD)
+    comp_count = comp_kv.shape[0]
     all_ids = jnp.arange(ctx_count * tiles_shard).reshape(ctx_count, tiles_shard)
     wanted = jnp.any(own_flat[:, None, None] == all_ids[None, :, :], axis=0)
     wanted_rank = jnp.cumsum(wanted.astype(jnp.int32), axis=1) - 1

time: 147 us -> 149 us (1.014)
  blocking collectives: 42.5 us -> 0 us
  waiting for transfers between devices: 17.5 us -> 55.3 us
  local copies, waits for them, and re-layouts: 14.9 us -> 27.3 us
  Pallas kernels: 41 us -> 34 us
  starting transfers between devices: 23.6 us -> 26.5 us
    all_gather x1 -> x0, blocking collectives: 42.5 us -> none  [local(): comp_kv = lax.all_gather(compressed, 'ctx', axis=0, tiled=True)]
    ppermute x2, waiting for transfers between devices: 13.5 us -> 46.8 us  [shifted(): return lax.ppermute(block, axis, route)]
    slice x0 -> x2, local copies, waits for them, and re-layouts: none -> 8.85 us  [the longest x1 5.51 us: local(): comp_kv = arrived[:, CAP].reshape(ctx_count * comp_local, 2 * HD)]
    pallas_call x3, Pallas kernels: 41 us -> 34 us  [branch(): pl.pallas_call(kernel, grid=(blocks,), in_specs=in_specs, out_specs=pl.Bl...]
    all_to_all x1, waiting for transfers between devices: 4 us -> 8.47 us  [local(): lax.all_to_all(outbox_kv, 'head', 0, 0, tiled=True)]
    unnamed x15 -> x20, local copies, waits for them, and re-layouts: 5.47 us -> 8.42 us
    concatenate x0 -> x1, local copies, waits for them, and re-layouts: none -> 2.65 us  [local(): mail = jnp.concatenate([outbox, comp_slot], axis=1)]
    convert_element_type x1 -> x0, local copies, waits for them, and re-layouts: 2.05 us -> none  [local(): outbox = jnp.einsum('dct,tx->dcx', picked.astype(jnp.bfloat16), group_kv....]
  transfers between devices with their start and end apart: 4 -> 4, of which waited for: 2 -> 3; matrix products, arithmetic and copies ran while one was open for 5% -> 4% of each run, Pallas kernels for 14% -> 5%
where the time goes in v2:
time: 149 us; the launch traced here: 147 us
  waiting for transfers between devices  55.3 us (37%)
  Pallas kernels  34 us (23%)
  local copies, waits for them, and re-layouts  27.3 us (18%)
  starting transfers between devices  26.5 us (18%)
  other arithmetic  2.92 us (2%)
    ppermute x2, waiting for transfers between devices, shifted(): return lax.ppermute(block, axis, route)  46.8 us
    pallas_call x3, Pallas kernels, branch(): pl.pallas_call(kernel, grid=(blocks,), in_specs=in_specs, out_specs=pl.Bl...  34 us
    all_to_all x1, starting transfers between devices, local(): lax.all_to_all(mail, 'ctx', split_axis=0, concat_axis=0, tiled=True)  11.8 us
    ppermute x2, starting transfers between devices, shifted(): return lax.ppermute(block, axis, route)  9.23 us
    all_to_all x1, waiting for transfers between devices, local(): lax.all_to_all(outbox_kv, 'head', 0, 0, tiled=True)  8.47 us
    unnamed x20, local copies, waits for them, and re-layouts  8.42 us
    slice x1, local copies, waits for them, and re-layouts, local(): comp_kv = arrived[:, CAP].reshape(ctx_count * comp_local, 2 * HD)  5.51 us
    all_to_all x1, starting transfers between devices, local(): lax.all_to_all(outbox_kv, 'head', 0, 0, tiled=True)  5.5 us
  transfers between devices with their start and end apart: 4, of which 3 were waited for; matrix products, arithmetic and copies ran while one was open for 4% of the time, Pallas kernels for 5%

profile of v2, /device:TPU:32, one launch (start us, length us, event | category | flops | bytes accessed | tf_op | source)
XLA Modules:
  0.0 146.7 jit_solution(17765252712555645456)
XLA Ops:
  0.0 0.8 copy-done
  0.8 0.9 copy_bitcast_fusion
  1.7 1.4 gather_fusion
  3.1 5.5 %all-to-all-start = ((bf16[16,64,256]{2,1,0:T(8,128)(2,1)}), bf16[16,64,256]{2,1,0:T(8,128)(2,1)S(1)}, u32[]{:S(2)}, u32[]{:S(2)}) async-start(bf16[16,64,256]{2,1,0:T(8,128)(2,1)} %gather_fusion), calls=%async_computation | async-start | bytes 1048576 | tf_op jit(solution)/shard_map/all_to_all | solution.py:124
  9.0 0.4 compare_reduce_fusion
  9.4 0.4 compare_reduce_fusion.1
  9.9 0.7 constant_dynamic-slice_fusion
  11.0 8.5 %all-to-all-done = bf16[16,64,256]{2,1,0:T(8,128)(2,1)S(1)} async-done(((bf16[16,64,256]{2,1,0:T(8,128)(2,1)}), bf16[16,64,256]{2,1,0:T(8,128)(2,1)S(1)}, u32[]{:S(2)}, u32[]{:S(2)}) %all-to-all-start) | async-done | bytes 524320 | tf_op jit(solution)/shard_map/all_to_all | solution.py:124
  19.4 4.2 %collective-permute-start = (bf16[16,256]{1,0:T(8,128)(2,1)S(1)}, bf16[16,256]{1,0:T(8,128)(2,1)S(1)}, u32[]{:S(2)}, u32[]{:S(2)}) collective-permute-start(bf16[16,256]{1,0:T(8,128)(2,1)S(1)} %slice.48), channel_id=1, source_target_pairs={{16,0},{32,16},{48,32},{64,48},{80,64},{96,80},{112,96},{128,112},... | collective-permute-start | bytes 24584 | tf_op jit(solution)/shard_map/ppermute | solution.py:26
  23.6 0.2 reshape.301
  23.9 0.4 convolution_convert_fusion
  24.3 0.2 fusion.1
  24.5 2.0 %collective-permute-done = bf16[16,256]{1,0:T(8,128)(2,1)S(1)} collective-permute-done((bf16[16,256]{1,0:T(8,128)(2,1)S(1)}, bf16[16,256]{1,0:T(8,128)(2,1)S(1)}, u32[]{:S(2)}, u32[]{:S(2)}) %collective-permute-start) | collective-permute-done | bytes 8224 | tf_op jit(solution)/shard_map/ppermute | solution.py:26
  26.5 0.2 fusion
  26.9 2.6 %copy.38 = bf16[16,3,16384]{2,1,0:T(4,128)(2,1)} copy(bf16[16,3,16384]{2,0,1:T(8,128)(2,1)S(1)} %pad_maximum_fusion) | data formatting | bytes 3145728 | tf_op jit(solution)/shard_map/concatenate | solution.py:169
  29.6 11.8 %all-to-all-start.1 = ((bf16[16,3,16384]{2,1,0:T(4,128)(2,1)}), bf16[16,3,16384]{2,1,0:T(4,128)(2,1)}, u32[]{:S(2)}, u32[]{:S(2)}) async-start(bf16[16,3,16384]{2,1,0:T(4,128)(2,1)} %copy.38), calls=%async_computation.1 | async-start | bytes 4194304 | tf_op jit(solution)/shard_map/all_to_all | solution.py:170
  42.5 0.5 copy.42
  43.1 0.4 divide_bitcast_fusion
  43.6 5.1 %collective-permute-start.1 = (bf16[512,256]{1,0:T(8,128)(2,1)S(1)}, bf16[512,256]{1,0:T(8,128)(2,1)S(1)}, u32[]{:S(2)}, u32[]{:S(2)}) collective-permute-start(bf16[512,256]{1,0:T(8,128)(2,1)S(1)} %bitcast.37), channel_id=1, source_target_pairs={{0,16},{16,32},{32,48},{48,64},{64,80},{80,96},{96,112},{112,128},... | collective-permute-start | bytes 786440 | tf_op jit(solution)/shard_map/ppermute | solution.py:26
  48.8 44.8 %collective-permute-done.1 = bf16[512,256]{1,0:T(8,128)(2,1)S(1)} collective-permute-done((bf16[512,256]{1,0:T(8,128)(2,1)S(1)}, bf16[512,256]{1,0:T(8,128)(2,1)S(1)}, u32[]{:S(2)}, u32[]{:S(2)}) %collective-permute-start.1) | collective-permute-done | bytes 262176 | tf_op jit(solution)/shard_map/ppermute | solution.py:26
  93.7 7.9 %shard_map.73.rest_0_ = f32[1024,512]{1,0:T(8,128)S(1)} custom-call(bf16[1024,512]{1,0:T(8,128)(2,1)S(1)} %copy-done.1, bf16[1536,256]{1,0:T(8,128)(2,1)S(1)} %pad_maximum_fusion.1.kv_ref, s32[4,1,768]{2,1,0:T(1,128)S(1)} %get-tuple-element.11.lo_ref, s32[4,1,768]{2,1,0:T(1,128)S(1)} %get-tuple-element.10.hi_ref, s32[1024,1]{1,0:T(8,128)S(1)} %iota_add_fusion.t_ref, ...), custom_call_target="tpu_custom_call" | custom-call | flops 1610612736 | bytes 6029312 | tf_op jit(solution)/shard_map/pallas_call | solution.py:96
  101.7 1.3 copy-done.3
  103.0 3.3 %slice.49 = bf16[16,2,16384]{2,1,0:T(2,128)(2,1)} slice(bf16[16,3,16384]{2,1,0:T(4,128)(2,1)} %all-to-all-done.1), slice={[0:16], [0:2], [0:16384]} | slice | bytes 2097152 | tf_op jit(solution)/shard_map/slice | solution.py:171
  106.4 1.7 %reshape.289.kv_ref = bf16[2048,256]{1,0:T(8,128)(2,1)S(1)} reshape(bf16[16,2,16384]{2,1,0:T(2,128)(2,1)} %slice.49) | data formatting | bytes 2097152 | tf_op jit(solution)/shard_map/reshape | solution.py:180
  108.1 5.5 %slice_reduce_fusion = bf16[16,16384]{1,0:T(8,128)(2,1)} fusion(bf16[16,3,16384]{2,1,0:T(4,128)(2,1)} %all-to-all-done.1), kind=kLoop, calls=%fused_computation.4 | loop fusion | bytes 1048576 | tf_op jit(solution)/shard_map/slice | solution.py:172
  113.6 1.3 reshape_squeeze.3.kv_ref
  114.9 1.2 copy-done.2
  116.1 1.6 %copy-done.4 = f32[1024,512]{1,0:T(8,128)S(1)} copy-done((f32[1024,512]{1,0:T(8,128)S(1)}, f32[1024,512]{1,0:T(8,128)}, u32[]{:S(2)}) %copy-start.4) | copy-done | bytes 2097176
  117.7 9.5 %shard_map.74.rest_0_ = f32[1024,512]{1,0:T(8,128)S(1)} custom-call(bf16[1024,512]{1,0:T(8,128)(2,1)S(1)} %copy-done.2, bf16[1024,256]{1,0:T(8,128)(2,1)S(1)} %reshape_squeeze.3.kv_ref, s32[1,1,1024]{2,1,0:T(1,128)S(1)} %multiply_add_fusion.1.lo_ref, s32[1,1,1024]{2,1,0:T(1,128)S(1)} %broadcast_in_dim.63.hi_ref, ...), custom_call_target="tpu_custom_call", output_to_operand_aliasing={{}: (6, {})} | custom-call | flops 2147483648 | bytes 5767168 | tf_op jit(solution)/shard_map/pallas_call | solution.py:96
  127.2 1.3 copy-done.5
  128.6 1.6 %copy-done.6 = f32[1024,512]{1,0:T(8,128)S(1)} copy-done((f32[1024,512]{1,0:T(8,128)S(1)}, f32[1024,512]{1,0:T(8,128)}, u32[]{:S(2)}) %copy-start.6) | copy-done | bytes 2097176
  130.2 16.5 %shard_map.75 = bf16[1024,512]{1,0:T(8,128)(2,1)} custom-call(bf16[1024,512]{1,0:T(8,128)(2,1)S(1)} %copy-done.2, bf16[2048,256]{1,0:T(8,128)(2,1)S(1)} %reshape.289.kv_ref, s32[4,1,2048]{2,1,0:T(1,128)S(1)} %broadcast_select_fusion.lo_ref, s32[1,1,2048]{2,1,0:T(1,128)S(1)} %broadcast_in_dim.62.hi_ref, s32[1024,1]{1,0:T(8,128)S(1)} %iota_add_fusion.t_ref, ...), custom_call_target="tpu_custom_call" | custom-call | flops 4294967296 | bytes 6291456 | tf_op jit(solution)/shard_map/pallas_call | solution.py:96
  (57 shorter events, 2.4 us)
Async XLA Ops:
  0.0 0.8 copy-start
  0.0 8.7 %copy-start.8 = (s32[64,64]{1,0:T(8,128)S(1)}, s32[64,64]{1,0:T(8,128)}, u32[]{:S(2)}) copy-start(s32[64,64]{1,0:T(8,128)} %param.13) | copy-start | bytes 49156
  3.1 16.3 %all-to-all-start = ((bf16[16,64,256]{2,1,0:T(8,128)(2,1)}), bf16[16,64,256]{2,1,0:T(8,128)(2,1)S(1)}, u32[]{:S(2)}, u32[]{:S(2)}) async-start(bf16[16,64,256]{2,1,0:T(8,128)(2,1)} %gather_fusion), calls=%async_computation | async-start | bytes 1048576 | tf_op jit(solution)/shard_map/all_to_all | solution.py:124
  19.4 7.0 %collective-permute-start = (bf16[16,256]{1,0:T(8,128)(2,1)S(1)}, bf16[16,256]{1,0:T(8,128)(2,1)S(1)}, u32[]{:S(2)}, u32[]{:S(2)}) collective-permute-start(bf16[16,256]{1,0:T(8,128)(2,1)S(1)} %slice.48), channel_id=1, source_target_pairs={{16,0},{32,16},{48,32},{64,48},{80,64},{96,80},{112,96},{128,112},... | collective-permute-start | bytes 24584 | tf_op jit(solution)/shard_map/ppermute | solution.py:26
  29.6 12.9 %copy-start.7 = (f32[3,4,1024]{2,1,0:T(4,128)S(1)}, f32[3,4,1024]{2,1,0:T(4,128)}, u32[]{:S(2)}) copy-start(f32[3,4,1024]{2,1,0:T(4,128)} %param.12) | copy-start | bytes 147460
  29.6 73.4 %all-to-all-start.1 = ((bf16[16,3,16384]{2,1,0:T(4,128)(2,1)}), bf16[16,3,16384]{2,1,0:T(4,128)(2,1)}, u32[]{:S(2)}, u32[]{:S(2)}) async-start(bf16[16,3,16384]{2,1,0:T(4,128)(2,1)} %copy.38), calls=%async_computation.1 | async-start | bytes 4194304 | tf_op jit(solution)/shard_map/all_to_all | solution.py:170
  43.6 50.0 %collective-permute-start.1 = (bf16[512,256]{1,0:T(8,128)(2,1)S(1)}, bf16[512,256]{1,0:T(8,128)(2,1)S(1)}, u32[]{:S(2)}, u32[]{:S(2)}) collective-permute-start(bf16[512,256]{1,0:T(8,128)(2,1)S(1)} %bitcast.37), channel_id=1, source_target_pairs={{0,16},{16,32},{32,48},{48,64},{64,80},{80,96},{96,112},{112,128},... | collective-permute-start | bytes 786440 | tf_op jit(solution)/shard_map/ppermute | solution.py:26
  48.8 44.9 %copy-start.1 = (bf16[1024,512]{1,0:T(8,128)(2,1)S(1)}, bf16[1024,512]{1,0:T(8,128)(2,1)}, u32[]{:S(2)}) copy-start(bf16[1024,512]{1,0:T(8,128)(2,1)} %q_ref.5) | copy-start | bytes 3145732
  101.7 1.3 copy-start.3
  114.9 1.2 copy-start.2
  116.1 1.6 %copy-start.4 = (f32[1024,512]{1,0:T(8,128)S(1)}, f32[1024,512]{1,0:T(8,128)}, u32[]{:S(2)}) copy-start(f32[1024,512]{1,0:T(8,128)} %copy-done.3) | copy-start | bytes 6291460
  127.2 1.4 copy-start.5
  128.6 1.6 %copy-start.6 = (f32[1024,512]{1,0:T(8,128)S(1)}, f32[1024,512]{1,0:T(8,128)}, u32[]{:S(2)}) copy-start(f32[1024,512]{1,0:T(8,128)} %copy-done.5) | copy-start | bytes 6291460

commit v3 on v2

--- a/solution.py
+++ b/solution.py
@@ -149,6 +149,11 @@
 
     block_count = local_rows // QB
     tiles_shard = local_rows // TILE
+    share = (H // G) // local_heads
+    part = head_index % share
+    groups = [[g * share + i for i in range(share)] for g in range(head_count // share)]
+    sel_share = CAP * TILE // share
+    comp_share = comp_local // share
     group_tiles = lax.dynamic_slice_in_dim(sel_tiles, group_index * TOPK, TOPK, 1)
     own_tiles = lax.dynamic_slice_in_dim(group_tiles, ctx_index * block_count, block_count, 0)
     own_flat = own_tiles.reshape(-1)
@@ -156,41 +161,53 @@
     local_ids = ctx_index * tiles_shard + jnp.arange(tiles_shard)
     present = jnp.any(requests[:, :, None] == local_ids[None, None, :], axis=1)
     order_rank = jnp.cumsum(present.astype(jnp.int32), axis=1) - 1
-    picked = present[:, None, :] & (order_rank[:, None, :] == jnp.arange(CAP)[None, :, None])
-    outbox = jnp.einsum(
-        "dct,tx->dcx",
+    my_slot = part * sel_share // TILE
+    my_row = part * sel_share % TILE
+    picked = present & (order_rank == my_slot)
+    tile_rows = lax.dynamic_slice_in_dim(
+        group_kv.reshape(tiles_shard, TILE, 2 * HD), my_row, sel_share, 1
+    )
+    sel_part = jnp.einsum(
+        "dt,tx->dx",
         picked.astype(jnp.bfloat16),
-        group_kv.reshape(tiles_shard, TILE * 2 * HD),
+        tile_rows.reshape(tiles_shard, sel_share * 2 * HD),
         preferred_element_type=jnp.float32,
-    ).astype(jnp.bfloat16)
-    comp_slot = jnp.broadcast_to(
-        compressed.reshape(1, 1, comp_local * 2 * HD), (ctx_count, 1, comp_local * 2 * HD)
-    )
-    mail = jnp.concatenate([outbox, comp_slot], axis=1)
+    ).astype(jnp.bfloat16).reshape(ctx_count, sel_share, 2 * HD)
+    comp_part = jnp.broadcast_to(
+        lax.dynamic_slice_in_dim(compressed, part * comp_share, comp_share, 0)[None],
+        (ctx_count, comp_share, 2 * HD),
+    )
+    mail = jnp.concatenate([sel_part, comp_part], axis=1)
     arrived = lax.all_to_all(mail, "ctx", split_axis=0, concat_axis=0, tiled=True)
-    received = arrived[:, :CAP]
-    comp_kv = arrived[:, CAP].reshape(ctx_count * comp_local, 2 * HD)
+    gathered = lax.all_gather(arrived, "head", axis=0, axis_index_groups=groups)
+    sel_kv = gathered[:, :, :sel_share].reshape(share * ctx_count * sel_share, 2 * HD)
+    comp_kv = gathered[:, :, sel_share:].reshape(share * ctx_count * comp_share, 2 * HD)
+    sel_rows = sel_kv.shape[0]
     comp_count = comp_kv.shape[0]
     all_ids = jnp.arange(ctx_count * tiles_shard).reshape(ctx_count, tiles_shard)
     wanted = jnp.any(own_flat[:, None, None] == all_ids[None, :, :], axis=0)
     wanted_rank = jnp.cumsum(wanted.astype(jnp.int32), axis=1) - 1
     chosen = wanted[:, None, :] & (wanted_rank[:, None, :] == jnp.arange(CAP)[None, :, None])
-    slot_tile = jnp.sum(jnp.where(chosen, all_ids[:, None, :], 0), axis=2).reshape(-1)
-    slot_ok = jnp.any(chosen, axis=2).reshape(-1)
-    sel_kv = received.reshape(ctx_count * CAP * TILE, 2 * HD)
-    sel_rows = sel_kv.shape[0]
-    key_pos = (slot_tile[:, None] * TILE + jnp.arange(TILE)[None, :]).reshape(-1)
-    is_named = slot_ok[None, :] & jnp.any(
-        own_tiles[:, :, None] == slot_tile[None, None, :], axis=1
-    )
-    sel_lo = jnp.where(jnp.repeat(is_named, TILE, axis=1), key_pos[None, :], BIG).reshape(
-        block_count, 1, sel_rows
-    )
+    slot_tile = jnp.sum(jnp.where(chosen, all_ids[:, None, :], 0), axis=2)
+    slot_ok = jnp.any(chosen, axis=2)
+    payload_row = jnp.arange(share)[:, None, None] * sel_share + jnp.arange(sel_share)[None, None, :]
+    source = jnp.arange(ctx_count)[None, :, None]
+    key_slot = payload_row // TILE + 0 * source
+    key_tile = slot_tile[source, key_slot]
+    key_pos = (key_tile * TILE + payload_row % TILE).reshape(-1)
+    is_named = slot_ok[None] & jnp.any(
+        own_tiles[:, :, None, None] == slot_tile[None, None], axis=1
+    )
+    key_named = is_named[:, source, key_slot].reshape(block_count, -1)
+    sel_lo = jnp.where(key_named, key_pos[None, :], BIG).reshape(block_count, 1, sel_rows)
     never = jnp.full((1, 1, sel_rows), BIG, jnp.int32)
 
-    comp_lo = (jnp.arange(comp_count, dtype=jnp.int32) * STRIDE + KERN - 1).reshape(
-        1, 1, comp_count
-    )
+    comp_index = (
+        jnp.arange(ctx_count)[None, :, None] * comp_local
+        + jnp.arange(share)[:, None, None] * comp_share
+        + jnp.arange(comp_share)[None, None, :]
+    ).reshape(-1)
+    comp_lo = (comp_index * STRIDE + KERN - 1).astype(jnp.int32).reshape(1, 1, comp_count)
     comp_hi = jnp.full((1, 1, comp_count), BIG, jnp.int32)
 
     win_rows = QB + WIN

time: 149 us -> 132 us (0.89); the launches traced: 147 us -> 132 us
  waiting for transfers between devices: 55.3 us -> 15.7 us
  between operations: 0.36 us -> 13.8 us
  local copies, waits for them, and re-layouts: 27.3 us -> 38 us
    ppermute x2, waiting for transfers between devices: 46.8 us -> 7.65 us  [shifted(): return lax.ppermute(block, axis, route)]
    gather x0 -> x3, local copies, waits for them, and re-layouts: none -> 27.9 us  [the longest x1 17.2 us: local(): key_tile = slot_tile[source, key_slot]]
    slice x2, local copies, waits for them, and re-layouts: 8.85 us -> 2.54 us  [the longest x1 1.31 us: local(): gathered[:, :, :sel_share].reshape(share * ctx_count * sel_share, 2 * HD)]
    unnamed x20 -> x17, local copies, waits for them, and re-layouts: 8.42 us -> 3.62 us
    concatenate x1, local copies, waits for them, and re-layouts: 2.65 us -> 0.07 us  [local(): key_named = is_named[:, source, key_slot].reshape(block_count, -1)]
    reshape x2 -> x1, local copies, waits for them, and re-layouts: 1.83 us -> 0.12 us  [local(): key_named = is_named[:, source, key_slot].reshape(block_count, -1)]
    another operation x2 -> x0, local copies, waits for them, and re-layouts: 1.52 us -> none  [the longest x1 1.28 us: local(): comp_kv = arrived[:, CAP].reshape(ctx_count * comp_local, 2 * HD)]
  transfers between devices with their start and end apart: 4 -> 5, of which waited for: 3 -> 3; matrix products, arithmetic and copies ran while one was open for 4% -> 25% of each run, Pallas kernels for 5% -> 6%
where the time goes in v3:
time: 132 us
  local copies, waits for them, and re-layouts  38 us (29%)
  Pallas kernels  33.4 us (25%)
  starting transfers between devices  26.4 us (20%)
  waiting for transfers between devices  15.7 us (12%)
  between operations  13.8 us (10%)
  other arithmetic  3.9 us (3%)
    pallas_call x3, Pallas kernels, branch(): pl.pallas_call(kernel, grid=(blocks,), in_specs=in_specs, out_specs=pl.Bl...  33.4 us
    gather x1, local copies, waits for them, and re-layouts, local(): key_tile = slot_tile[source, key_slot]  17.2 us
    all_to_all x1, starting transfers between devices, local(): lax.all_to_all(mail, 'ctx', split_axis=0, concat_axis=0, tiled=True)  11.7 us
    gather x2, local copies, waits for them, and re-layouts, local(): key_named = is_named[:, source, key_slot].reshape(block_count, -1)  10.7 us
    ppermute x2, starting transfers between devices, shifted(): return lax.ppermute(block, axis, route)  9.23 us
    all_to_all x1, waiting for transfers between devices, local(): lax.all_to_all(outbox_kv, 'head', 0, 0, tiled=True)  8.05 us
    ppermute x2, waiting for transfers between devices, shifted(): return lax.ppermute(block, axis, route)  7.65 us
    all_to_all x1, starting transfers between devices, local(): lax.all_to_all(outbox_kv, 'head', 0, 0, tiled=True)  5.5 us
  transfers between devices with their start and end apart: 5, of which 3 were waited for; matrix products, arithmetic and copies ran while one was open for 25% of the time, Pallas kernels for 6%

profile of v3, /device:TPU:32, one launch (start us, length us, event | category | flops | bytes accessed | tf_op | source)
XLA Modules:
  0.0 131.6 jit_solution(18383090717107531817)
XLA Ops:
  6.6 0.8 copy-done
  7.4 0.9 copy_bitcast_fusion
  8.3 1.4 %gather_fusion = bf16[16,64,256]{2,1,0:T(8,128)(2,1)} fusion(bf16[4,64,256]{2,1,0:T(8,128)(2,1)S(1)} %maximum_bitcast_fusion, s32[1024]{0:T(1024)S(1)} %pad_clamp_fusion), kind=kCustom, calls=%fused_computation | custom fusion | bytes 1048640 | tf_op jit(solution)/shard_map/gather | solution.py:123
  9.6 5.5 %all-to-all-start = ((bf16[16,64,256]{2,1,0:T(8,128)(2,1)}), bf16[16,64,256]{2,1,0:T(8,128)(2,1)S(1)}, u32[]{:S(2)}, u32[]{:S(2)}) async-start(bf16[16,64,256]{2,1,0:T(8,128)(2,1)} %gather_fusion), calls=%async_computation | async-start | bytes 1048576 | tf_op jit(solution)/shard_map/all_to_all | solution.py:124
  15.6 0.4 compare_reduce_fusion
  16.0 0.2 reduce_window_sum.18
  16.4 0.4 compare_reduce_fusion.1
  16.8 0.7 constant_dynamic-slice_fusion
  17.6 0.2 reduce_window_sum.17
  17.9 8.0 %all-to-all-done = bf16[16,64,256]{2,1,0:T(8,128)(2,1)S(1)} async-done(((bf16[16,64,256]{2,1,0:T(8,128)(2,1)}), bf16[16,64,256]{2,1,0:T(8,128)(2,1)S(1)}, u32[]{:S(2)}, u32[]{:S(2)}) %all-to-all-start) | async-done | bytes 524320 | tf_op jit(solution)/shard_map/all_to_all | solution.py:124
  26.0 4.2 %collective-permute-start = (bf16[16,256]{1,0:T(8,128)(2,1)S(1)}, bf16[16,256]{1,0:T(8,128)(2,1)S(1)}, u32[]{:S(2)}, u32[]{:S(2)}) collective-permute-start(bf16[16,256]{1,0:T(8,128)(2,1)S(1)} %slice.52), channel_id=1, source_target_pairs={{16,0},{32,16},{48,32},{64,48},{80,64},{96,80},{112,96},{128,112},... | collective-permute-start | bytes 24584 | tf_op jit(solution)/shard_map/ppermute | solution.py:26
  30.2 0.2 copy.47
  30.3 0.2 convolution_convert_fusion
  30.6 0.2 fusion.1
  30.8 2.2 %collective-permute-done = bf16[16,256]{1,0:T(8,128)(2,1)S(1)} collective-permute-done((bf16[16,256]{1,0:T(8,128)(2,1)S(1)}, bf16[16,256]{1,0:T(8,128)(2,1)S(1)}, u32[]{:S(2)}, u32[]{:S(2)}) %collective-permute-start) | collective-permute-done | bytes 8224 | tf_op jit(solution)/shard_map/ppermute | solution.py:26
  33.0 0.2 fusion
  33.3 0.8 pad_maximum_fusion.2
  34.1 11.7 %all-to-all-start.1 = ((bf16[16,48,256]{2,1,0:T(8,128)(2,1)}), bf16[16,48,256]{2,1,0:T(8,128)(2,1)S(1)}, u32[]{:S(2)}, u32[]{:S(2)}) async-start(bf16[16,48,256]{2,1,0:T(8,128)(2,1)} %pad_maximum_fusion.2), calls=%async_computation.1 | async-start | bytes 786432 | tf_op jit(solution)/shard_map/all_to_all | solution.py:181
  46.2 17.2 %gather_fusion.2 = s32[2048]{0:T(1024)S(1)} fusion(s32[16,2]{0,1:T(2,128)S(1)} %select_reduce_fusion, s32[2048]{0:T(1024)S(1)} %reshape.445), kind=kCustom, calls=%fused_computation.2 | custom fusion | bytes 32768 | tf_op jit(solution)/shard_map/gather | solution.py:196
  63.5 0.7 copy-done.4
  64.5 10.2 %gather_fusion.1 = pred[2048,4]{1,0:T(8,128)(4,1)S(1)} fusion(pred[4,16,2]{0,1,2:T(8,128)(4,1)S(1)} %broadcast_and_fusion, s32[2048]{0:T(1024)S(1)} %reshape.445), kind=kCustom, calls=%fused_computation.1 | custom fusion | bytes 32768 | tf_op jit(solution)/shard_map/gather | solution.py:201
  74.7 0.5 copy.40
  75.4 0.5 copy.42
  76.1 0.4 divide_bitcast_fusion
  76.6 5.1 %collective-permute-start.1 = (bf16[512,256]{1,0:T(8,128)(2,1)S(1)}, bf16[512,256]{1,0:T(8,128)(2,1)S(1)}, u32[]{:S(2)}, u32[]{:S(2)}) collective-permute-start(bf16[512,256]{1,0:T(8,128)(2,1)S(1)} %bitcast.58), channel_id=1, source_target_pairs={{0,16},{16,32},{32,48},{48,64},{64,80},{80,96},{96,112},{112,128},... | collective-permute-start | bytes 786440 | tf_op jit(solution)/shard_map/ppermute | solution.py:26
  81.8 5.5 %collective-permute-done.1 = bf16[512,256]{1,0:T(8,128)(2,1)S(1)} collective-permute-done((bf16[512,256]{1,0:T(8,128)(2,1)S(1)}, bf16[512,256]{1,0:T(8,128)(2,1)S(1)}, u32[]{:S(2)}, u32[]{:S(2)}) %collective-permute-start.1) | collective-permute-done | bytes 262176 | tf_op jit(solution)/shard_map/ppermute | solution.py:26
  87.3 7.9 %shard_map.73.rest_0_ = f32[1024,512]{1,0:T(8,128)S(1)} custom-call(bf16[1024,512]{1,0:T(8,128)(2,1)S(1)} %copy-done.1, bf16[1536,256]{1,0:T(8,128)(2,1)S(1)} %pad_maximum_fusion.kv_ref, s32[4,1,768]{2,1,0:T(1,128)S(1)} %get-tuple-element.11.lo_ref, s32[4,1,768]{2,1,0:T(1,128)S(1)} %get-tuple-element.10.hi_ref, s32[1024,1]{1,0:T(8,128)S(1)} %iota_add_fusion.t_ref, ...), custom_call_target="tpu_custom_call" | custom-call | flops 1610612736 | bytes 6029312 | tf_op jit(solution)/shard_map/pallas_call | solution.py:96
  95.3 1.3 %copy-done.2 = f32[1024,512]{1,0:T(8,128)} copy-done((f32[1024,512]{1,0:T(8,128)}, f32[1024,512]{1,0:T(8,128)S(1)}, u32[]{:S(2)}) %copy-start.2) | copy-done | bytes 2097176
  96.6 1.2 slice.55
  97.8 1.3 slice.53
  99.2 9.5 %shard_map.74.rest_0_ = f32[1024,512]{1,0:T(8,128)S(1)} custom-call(bf16[1024,512]{1,0:T(8,128)(2,1)S(1)} %copy-done.1, bf16[1024,256]{1,0:T(8,128)(2,1)S(1)} %bitcast.46, s32[1,1,1024]{2,1,0:T(1,128)S(1)} %sub.42.lo_ref, s32[1,1,1024]{2,1,0:T(1,128)S(1)} %broadcast_in_dim.38.hi_ref, ...), custom_call_target="tpu_custom_call", output_to_operand_aliasing={{}: (6, {})} | custom-call | flops 2147483648 | bytes 5767168 | tf_op jit(solution)/shard_map/pallas_call | solution.py:96
  108.7 16.0 %shard_map.75 = bf16[1024,512]{1,0:T(8,128)(2,1)} custom-call(bf16[1024,512]{1,0:T(8,128)(2,1)S(1)} %copy-done.1, bf16[2048,256]{1,0:T(8,128)(2,1)S(1)} %bitcast.45, s32[4,1,2048]{2,1,0:T(1,128)S(1)} %broadcast_select_fusion.lo_ref, s32[1,1,2048]{2,1,0:T(1,128)S(1)} %broadcast_in_dim.37.hi_ref, s32[1024,1]{1,0:T(8,128)S(1)} %iota_add_fusion.t_ref, ...), custom_call_target="tpu_custom_call" | custom-call | flops 4294967296 | bytes 6291456 | tf_op jit(solution)/shard_map/pallas_call | solution.py:96
  (62 shorter events, 2.2 us)
Async XLA Ops:
  6.5 0.8 copy-start
  6.5 8.8 %copy-start.6 = (s32[64,64]{1,0:T(8,128)S(1)}, s32[64,64]{1,0:T(8,128)}, u32[]{:S(2)}) copy-start(s32[64,64]{1,0:T(8,128)} %param.13) | copy-start | bytes 49156
  9.6 16.3 %all-to-all-start = ((bf16[16,64,256]{2,1,0:T(8,128)(2,1)}), bf16[16,64,256]{2,1,0:T(8,128)(2,1)S(1)}, u32[]{:S(2)}, u32[]{:S(2)}) async-start(bf16[16,64,256]{2,1,0:T(8,128)(2,1)} %gather_fusion), calls=%async_computation | async-start | bytes 1048576 | tf_op jit(solution)/shard_map/all_to_all | solution.py:124
  26.0 7.0 %collective-permute-start = (bf16[16,256]{1,0:T(8,128)(2,1)S(1)}, bf16[16,256]{1,0:T(8,128)(2,1)S(1)}, u32[]{:S(2)}, u32[]{:S(2)}) collective-permute-start(bf16[16,256]{1,0:T(8,128)(2,1)S(1)} %slice.52), channel_id=1, source_target_pairs={{16,0},{32,16},{48,32},{64,48},{80,64},{96,80},{112,96},{128,112},... | collective-permute-start | bytes 24584 | tf_op jit(solution)/shard_map/ppermute | solution.py:26
  34.1 29.4 %all-to-all-start.1 = ((bf16[16,48,256]{2,1,0:T(8,128)(2,1)}), bf16[16,48,256]{2,1,0:T(8,128)(2,1)S(1)}, u32[]{:S(2)}, u32[]{:S(2)}) async-start(bf16[16,48,256]{2,1,0:T(8,128)(2,1)} %pad_maximum_fusion.2), calls=%async_computation.1 | async-start | bytes 786432 | tf_op jit(solution)/shard_map/all_to_all | solution.py:181
  45.7 50.9 %all-gather.3.cloned.1.call-start = ((), (), s32[]{:S(2)}) async-start(), calls=%async_computation.2 | async-start | bytes 1966080 | tf_op jit(solution)/shard_map/all_gather | solution.py:182
  63.4 12.0 %copy-start.5 = (f32[3,4,1024]{2,1,0:T(4,128)S(1)}, f32[3,4,1024]{2,1,0:T(4,128)}, u32[]{:S(2)}) copy-start(f32[3,4,1024]{2,1,0:T(4,128)} %param.12) | copy-start | bytes 147460
  63.5 0.8 copy-start.4
  76.6 10.7 %collective-permute-start.1 = (bf16[512,256]{1,0:T(8,128)(2,1)S(1)}, bf16[512,256]{1,0:T(8,128)(2,1)S(1)}, u32[]{:S(2)}, u32[]{:S(2)}) collective-permute-start(bf16[512,256]{1,0:T(8,128)(2,1)S(1)} %bitcast.58), channel_id=1, source_target_pairs={{0,16},{16,32},{32,48},{48,64},{64,80},{80,96},{96,112},{112,128},... | collective-permute-start | bytes 786440 | tf_op jit(solution)/shard_map/ppermute | solution.py:26
  81.7 5.6 %copy-start.1 = (bf16[1024,512]{1,0:T(8,128)(2,1)S(1)}, bf16[1024,512]{1,0:T(8,128)(2,1)}, u32[]{:S(2)}) copy-start(bf16[1024,512]{1,0:T(8,128)(2,1)} %q_ref.5) | copy-start | bytes 3145732
  95.3 1.4 %copy-start.2 = (f32[1024,512]{1,0:T(8,128)}, f32[1024,512]{1,0:T(8,128)S(1)}, u32[]{:S(2)}) copy-start(f32[1024,512]{1,0:T(8,128)S(1)} %shard_map.73.rest_0_) | copy-start | bytes 6291460
  96.6 2.6 %copy-start.3 = (f32[1024,512]{1,0:T(8,128)S(1)}, f32[1024,512]{1,0:T(8,128)}, u32[]{:S(2)}) copy-start(f32[1024,512]{1,0:T(8,128)} %copy-done.2) | copy-start | bytes 6291460
Sparse Core Ops, SparseCore 0:
  64.4 25.9 all-gather.2

commit v4 on v3

--- a/solution.py
+++ b/solution.py
@@ -119,8 +119,7 @@
     kv_rows = jnp.concatenate(
         [keys.reshape(dev_rows, G, HD), values.reshape(dev_rows, G, HD)], axis=2
     ).transpose(1, 0, 2)
-    dest_group = jnp.arange(head_count) * local_heads // (H // G)
-    outbox_kv = kv_rows[dest_group]
+    outbox_kv = jnp.repeat(kv_rows, (H // G) // local_heads, axis=0)
     group_kv = lax.all_to_all(outbox_kv, "head", 0, 0, tiled=True).reshape(
         local_rows, 2 * HD
     )
@@ -190,15 +189,20 @@
     chosen = wanted[:, None, :] & (wanted_rank[:, None, :] == jnp.arange(CAP)[None, :, None])
     slot_tile = jnp.sum(jnp.where(chosen, all_ids[:, None, :], 0), axis=2)
     slot_ok = jnp.any(chosen, axis=2)
-    payload_row = jnp.arange(share)[:, None, None] * sel_share + jnp.arange(sel_share)[None, None, :]
-    source = jnp.arange(ctx_count)[None, :, None]
-    key_slot = payload_row // TILE + 0 * source
-    key_tile = slot_tile[source, key_slot]
-    key_pos = (key_tile * TILE + payload_row % TILE).reshape(-1)
+    parts_per_slot = share // CAP
+    row_in_tile = (
+        jnp.arange(share)[:, None, None] % parts_per_slot * sel_share
+        + jnp.arange(sel_share)[None, None, :]
+    )
+    key_tile = jnp.repeat(slot_tile, parts_per_slot, axis=1).T[:, :, None]
+    key_pos = (key_tile * TILE + row_in_tile).reshape(-1)
     is_named = slot_ok[None] & jnp.any(
         own_tiles[:, :, None, None] == slot_tile[None, None], axis=1
     )
-    key_named = is_named[:, source, key_slot].reshape(block_count, -1)
+    key_named = jnp.broadcast_to(
+        jnp.repeat(is_named, parts_per_slot, axis=2).transpose(0, 2, 1)[:, :, :, None],
+        (block_count, share, ctx_count, sel_share),
+    ).reshape(block_count, -1)
     sel_lo = jnp.where(key_named, key_pos[None, :], BIG).reshape(block_count, 1, sel_rows)
     never = jnp.full((1, 1, sel_rows), BIG, jnp.int32)
 

time: 132 us -> 118 us (0.89); the launches traced: 132 us -> 116 us
  local copies, waits for them, and re-layouts: 38 us -> 9.56 us
  waiting for transfers between devices: 15.7 us -> 31.1 us
  starting transfers between devices: 26.4 us -> 23.8 us
    gather x4 -> x0, local copies, waits for them, and re-layouts: 29.3 us -> none  [the longest x1 17.2 us: local(): key_tile = slot_tile[source, key_slot]]
    all_to_all x1, waiting for transfers between devices: 0.01 us -> 12.6 us  [local(): lax.all_to_all(mail, 'ctx', split_axis=0, concat_axis=0, tiled=True)]
    ppermute x2, starting transfers between devices: 9.23 us -> 6.64 us  [shifted(): return lax.ppermute(block, axis, route)]
    ppermute x2, waiting for transfers between devices: 7.65 us -> 10.2 us  [shifted(): return lax.ppermute(block, axis, route)]
    unnamed x17 -> x15, local copies, waits for them, and re-layouts: 3.62 us -> 2.81 us
  transfers between devices with their start and end apart: 5 -> 5, of which waited for: 3 -> 5; matrix products, arithmetic and copies ran while one was open for 25% -> 5% of each run, Pallas kernels for 6% -> 7%
where the time goes in v4:
time: 118 us; the launch traced here: 116 us
  Pallas kernels  33.6 us (28%)
  waiting for transfers between devices  31.1 us (26%)
  starting transfers between devices  23.8 us (20%)
  between operations  13.8 us (12%)
  local copies, waits for them, and re-layouts  9.56 us (8%)
  other arithmetic  3.82 us (3%)
    pallas_call x3, Pallas kernels, branch(): pl.pallas_call(kernel, grid=(blocks,), in_specs=in_specs, out_specs=pl.Bl...  33.6 us
    all_to_all x1, waiting for transfers between devices, local(): lax.all_to_all(mail, 'ctx', split_axis=0, concat_axis=0, tiled=True)  12.6 us
    all_to_all x1, starting transfers between devices, local(): lax.all_to_all(mail, 'ctx', split_axis=0, concat_axis=0, tiled=True)  11.7 us
    ppermute x2, waiting for transfers between devices, shifted(): return lax.ppermute(block, axis, route)  10.2 us
    all_to_all x1, waiting for transfers between devices, local(): lax.all_to_all(outbox_kv, 'head', 0, 0, tiled=True)  8.05 us
    ppermute x2, starting transfers between devices, shifted(): return lax.ppermute(block, axis, route)  6.64 us
    all_to_all x1, starting transfers between devices, local(): lax.all_to_all(outbox_kv, 'head', 0, 0, tiled=True)  5.5 us
    unnamed x15, local copies, waits for them, and re-layouts  2.81 us
  transfers between devices with their start and end apart: 5, of which 5 were waited for; matrix products, arithmetic and copies ran while one was open for 5% of the time, Pallas kernels for 7%

profile of v4, /device:TPU:32, one launch (start us, length us, event | category | flops | bytes accessed | tf_op | source)
XLA Modules:
  0.0 115.9 jit_solution(15455545391912154709)
XLA Ops:
  6.5 0.9 reshape.317
  7.4 0.9 reshape.318
  8.4 0.8 broadcast_in_dim.41
  9.2 5.5 %all-to-all-start = ((bf16[16,64,256]{2,1,0:T(8,128)(2,1)}), bf16[16,64,256]{2,1,0:T(8,128)(2,1)S(1)}, u32[]{:S(2)}, u32[]{:S(2)}) async-start(bf16[16,64,256]{2,1,0:T(8,128)(2,1)} %bitcast.1), calls=%async_computation | async-start | bytes 1048576 | tf_op jit(solution)/shard_map/all_to_all | solution.py:123
  15.0 0.4 compare_reduce_fusion
  15.5 0.2 reduce_window_sum.18
  15.7 0.1 fusion.5
  15.9 0.4 compare_reduce_fusion.1
  16.3 0.7 constant_dynamic-slice_fusion
  17.1 0.2 reduce_window_sum.17
  17.5 8.1 %all-to-all-done = bf16[16,64,256]{2,1,0:T(8,128)(2,1)S(1)} async-done(((bf16[16,64,256]{2,1,0:T(8,128)(2,1)}), bf16[16,64,256]{2,1,0:T(8,128)(2,1)S(1)}, u32[]{:S(2)}, u32[]{:S(2)}) %all-to-all-start) | async-done | bytes 524320 | tf_op jit(solution)/shard_map/all_to_all | solution.py:123
  25.5 4.2 %collective-permute-start = (bf16[16,256]{1,0:T(8,128)(2,1)S(1)}, bf16[16,256]{1,0:T(8,128)(2,1)S(1)}, u32[]{:S(2)}, u32[]{:S(2)}) collective-permute-start(bf16[16,256]{1,0:T(8,128)(2,1)S(1)} %slice.46), channel_id=1, source_target_pairs={{16,0},{32,16},{48,32},{64,48},{80,64},{96,80},{112,96},{128,112},... | collective-permute-start | bytes 24584 | tf_op jit(solution)/shard_map/ppermute | solution.py:26
  29.8 0.2 copy.34
  29.9 0.2 convolution_convert_fusion
  30.1 0.2 fusion.1
  30.4 2.2 %collective-permute-done = bf16[16,256]{1,0:T(8,128)(2,1)S(1)} collective-permute-done((bf16[16,256]{1,0:T(8,128)(2,1)S(1)}, bf16[16,256]{1,0:T(8,128)(2,1)S(1)}, u32[]{:S(2)}, u32[]{:S(2)}) %collective-permute-start) | collective-permute-done | bytes 8224 | tf_op jit(solution)/shard_map/ppermute | solution.py:26
  32.6 0.2 fusion
  32.8 0.8 pad_maximum_fusion.2
  33.6 11.7 %all-to-all-start.1 = ((bf16[16,48,256]{2,1,0:T(8,128)(2,1)}), bf16[16,48,256]{2,1,0:T(8,128)(2,1)S(1)}, u32[]{:S(2)}, u32[]{:S(2)}) async-start(bf16[16,48,256]{2,1,0:T(8,128)(2,1)} %pad_maximum_fusion.2), calls=%async_computation.1 | async-start | bytes 786432 | tf_op jit(solution)/shard_map/all_to_all | solution.py:180
  45.5 12.6 %all-to-all-done.1 = bf16[16,48,256]{2,1,0:T(8,128)(2,1)S(1)} async-done(((bf16[16,48,256]{2,1,0:T(8,128)(2,1)}), bf16[16,48,256]{2,1,0:T(8,128)(2,1)S(1)}, u32[]{:S(2)}, u32[]{:S(2)}) %all-to-all-start.1) | async-done | bytes 393248 | tf_op jit(solution)/shard_map/all_to_all | solution.py:180
  58.1 0.7 copy-done.3
  59.5 0.5 copy.31
  60.1 0.4 divide_bitcast_fusion
  60.6 2.5 %collective-permute-start.1 = (bf16[512,256]{1,0:T(8,128)(2,1)S(1)}, bf16[512,256]{1,0:T(8,128)(2,1)S(1)}, u32[]{:S(2)}, u32[]{:S(2)}) collective-permute-start(bf16[512,256]{1,0:T(8,128)(2,1)S(1)} %bitcast.46), channel_id=1, source_target_pairs={{0,16},{16,32},{32,48},{48,64},{64,80},{80,96},{96,112},{112,128},... | collective-permute-start | bytes 786440 | tf_op jit(solution)/shard_map/ppermute | solution.py:26
  63.2 8.1 %collective-permute-done.1 = bf16[512,256]{1,0:T(8,128)(2,1)S(1)} collective-permute-done((bf16[512,256]{1,0:T(8,128)(2,1)S(1)}, bf16[512,256]{1,0:T(8,128)(2,1)S(1)}, u32[]{:S(2)}, u32[]{:S(2)}) %collective-permute-start.1) | collective-permute-done | bytes 262176 | tf_op jit(solution)/shard_map/ppermute | solution.py:26
  71.4 8.0 %shard_map.73.rest_0_ = f32[1024,512]{1,0:T(8,128)S(1)} custom-call(bf16[1024,512]{1,0:T(8,128)(2,1)S(1)} %copy-done, bf16[1536,256]{1,0:T(8,128)(2,1)S(1)} %pad_maximum_fusion.kv_ref, s32[4,1,768]{2,1,0:T(1,128)S(1)} %get-tuple-element.11.lo_ref, s32[4,1,768]{2,1,0:T(1,128)S(1)} %get-tuple-element.10.hi_ref, s32[1024,1]{1,0:T(8,128)S(1)} %iota_add_fusion.t_ref, ...), custom_call_target="tpu_custom_call" | custom-call | flops 1610612736 | bytes 6029312 | tf_op jit(solution)/shard_map/pallas_call | solution.py:96
  79.4 1.3 %copy-done.1 = f32[1024,512]{1,0:T(8,128)} copy-done((f32[1024,512]{1,0:T(8,128)}, f32[1024,512]{1,0:T(8,128)S(1)}, u32[]{:S(2)}) %copy-start.1) | copy-done | bytes 2097176
  80.7 0.2 all-gather.3.cloned.1.call-done
  80.9 1.2 %slice.49 = bf16[4,16,16,256]{3,2,1,0:T(8,128)(2,1)S(1)} slice(bf16[4,16,48,256]{3,2,1,0:T(8,128)(2,1)} %bitcast.40), slice={[0:4], [0:16], [32:48], [0:256]} | slice | bytes 1048576 | tf_op jit(solution)/shard_map/slice | solution.py:183
  82.1 1.3 %slice.47 = bf16[4,16,32,256]{3,2,1,0:T(8,128)(2,1)S(1)} slice(bf16[4,16,48,256]{3,2,1,0:T(8,128)(2,1)} %bitcast.41), slice={[0:4], [0:16], [0:32], [0:256]} | slice | bytes 2097152 | tf_op jit(solution)/shard_map/slice | solution.py:182
  83.5 9.5 %shard_map.74.rest_0_ = f32[1024,512]{1,0:T(8,128)S(1)} custom-call(bf16[1024,512]{1,0:T(8,128)(2,1)S(1)} %copy-done, bf16[1024,256]{1,0:T(8,128)(2,1)S(1)} %bitcast.35, s32[1,1,1024]{2,1,0:T(1,128)S(1)} %sub.30.lo_ref, s32[1,1,1024]{2,1,0:T(1,128)S(1)} %broadcast_in_dim.82.hi_ref, ...), custom_call_target="tpu_custom_call", output_to_operand_aliasing={{}: (6, {})} | custom-call | flops 2147483648 | bytes 5767168 | tf_op jit(solution)/shard_map/pallas_call | solution.py:96
  93.0 16.1 %shard_map.75 = bf16[1024,512]{1,0:T(8,128)(2,1)} custom-call(bf16[1024,512]{1,0:T(8,128)(2,1)S(1)} %copy-done, bf16[2048,256]{1,0:T(8,128)(2,1)S(1)} %bitcast.34, s32[4,1,2048]{2,1,0:T(1,128)S(1)} %broadcast_select_fusion.lo_ref, s32[1,1,2048]{2,1,0:T(1,128)S(1)} %broadcast_in_dim.81.hi_ref, s32[1024,1]{1,0:T(8,128)S(1)} %iota_add_fusion.t_ref, ...), custom_call_target="tpu_custom_call" | custom-call | flops 4294967296 | bytes 6291456 | tf_op jit(solution)/shard_map/pallas_call | solution.py:96
  (57 shorter events, 1.9 us)
Async XLA Ops:
  6.5 8.3 %copy-start.5 = (s32[64,64]{1,0:T(8,128)S(1)}, s32[64,64]{1,0:T(8,128)}, u32[]{:S(2)}) copy-start(s32[64,64]{1,0:T(8,128)} %param.13) | copy-start | bytes 49156
  9.2 16.3 %all-to-all-start = ((bf16[16,64,256]{2,1,0:T(8,128)(2,1)}), bf16[16,64,256]{2,1,0:T(8,128)(2,1)S(1)}, u32[]{:S(2)}, u32[]{:S(2)}) async-start(bf16[16,64,256]{2,1,0:T(8,128)(2,1)} %bitcast.1), calls=%async_computation | async-start | bytes 1048576 | tf_op jit(solution)/shard_map/all_to_all | solution.py:123
  25.5 7.0 %collective-permute-start = (bf16[16,256]{1,0:T(8,128)(2,1)S(1)}, bf16[16,256]{1,0:T(8,128)(2,1)S(1)}, u32[]{:S(2)}, u32[]{:S(2)}) collective-permute-start(bf16[16,256]{1,0:T(8,128)(2,1)S(1)} %slice.46), channel_id=1, source_target_pairs={{16,0},{32,16},{48,32},{64,48},{80,64},{96,80},{112,96},{128,112},... | collective-permute-start | bytes 24584 | tf_op jit(solution)/shard_map/ppermute | solution.py:26
  30.4 29.0 %copy-start.4 = (f32[3,4,1024]{2,1,0:T(4,128)S(1)}, f32[3,4,1024]{2,1,0:T(4,128)}, u32[]{:S(2)}) copy-start(f32[3,4,1024]{2,1,0:T(4,128)} %param.12) | copy-start | bytes 147460
  33.6 24.5 %all-to-all-start.1 = ((bf16[16,48,256]{2,1,0:T(8,128)(2,1)}), bf16[16,48,256]{2,1,0:T(8,128)(2,1)S(1)}, u32[]{:S(2)}, u32[]{:S(2)}) async-start(bf16[16,48,256]{2,1,0:T(8,128)(2,1)} %pad_maximum_fusion.2), calls=%async_computation.1 | async-start | bytes 786432 | tf_op jit(solution)/shard_map/all_to_all | solution.py:180
  45.3 35.6 %all-gather.3.cloned.1.call-start = ((), (), s32[]{:S(2)}) async-start(), calls=%async_computation.2 | async-start | bytes 1966080 | tf_op jit(solution)/shard_map/all_gather | solution.py:181
  58.1 0.7 copy-start.3
  60.6 10.7 %collective-permute-start.1 = (bf16[512,256]{1,0:T(8,128)(2,1)S(1)}, bf16[512,256]{1,0:T(8,128)(2,1)S(1)}, u32[]{:S(2)}, u32[]{:S(2)}) collective-permute-start(bf16[512,256]{1,0:T(8,128)(2,1)S(1)} %bitcast.46), channel_id=1, source_target_pairs={{0,16},{16,32},{32,48},{48,64},{64,80},{80,96},{96,112},{112,128},... | collective-permute-start | bytes 786440 | tf_op jit(solution)/shard_map/ppermute | solution.py:26
  63.2 8.1 %copy-start = (bf16[1024,512]{1,0:T(8,128)(2,1)S(1)}, bf16[1024,512]{1,0:T(8,128)(2,1)}, u32[]{:S(2)}) copy-start(bf16[1024,512]{1,0:T(8,128)(2,1)} %q_ref.5) | copy-start | bytes 3145732
  79.4 1.4 %copy-start.1 = (f32[1024,512]{1,0:T(8,128)}, f32[1024,512]{1,0:T(8,128)S(1)}, u32[]{:S(2)}) copy-start(f32[1024,512]{1,0:T(8,128)S(1)} %shard_map.73.rest_0_) | copy-start | bytes 6291460
  80.9 2.6 %copy-start.2 = (f32[1024,512]{1,0:T(8,128)S(1)}, f32[1024,512]{1,0:T(8,128)}, u32[]{:S(2)}) copy-start(f32[1024,512]{1,0:T(8,128)} %copy-done.1) | copy-start | bytes 6291460
Sparse Core Ops, SparseCore 0:
  59.0 21.8 all-gather.2

commit v5 on v4

--- a/solution.py
+++ b/solution.py
@@ -6,6 +6,7 @@
 from jax.experimental import pallas as pl
 from jax.experimental.pallas import tpu as pltpu
 from jax.sharding import PartitionSpec as P
+
 
 H = 64
 G = 4
@@ -123,8 +124,9 @@
     group_kv = lax.all_to_all(outbox_kv, "head", 0, 0, tiled=True).reshape(
         local_rows, 2 * HD
     )
-    tail_rows = shifted(group_kv[: KERN - STRIDE], "ctx", -1)
-    extended = jnp.concatenate([group_kv, tail_rows], axis=0)
+    previous = shifted(group_kv[local_rows - WIN :], "ctx", 1)
+    window_kv = jnp.concatenate([previous, group_kv], axis=0)
+    extended = window_kv[WIN - STRIDE :]
     comp_weight = jnp.concatenate(
         [
             lax.dynamic_slice_in_dim(comp_k_weight, group_index * HD, HD, 1),
@@ -143,8 +145,6 @@
         jnp.sum(first_half * comp_weight[None, :STRIDE], 1)
         + jnp.sum(second_half * comp_weight[None, STRIDE:], 1)
     ).astype(jnp.bfloat16)
-    previous = shifted(group_kv[local_rows - WIN :], "ctx", 1)
-    window_kv = jnp.concatenate([previous, group_kv], axis=0)
 
     block_count = local_rows // QB
     tiles_shard = local_rows // TILE
@@ -211,7 +211,9 @@
         + jnp.arange(share)[:, None, None] * comp_share
         + jnp.arange(comp_share)[None, None, :]
     ).reshape(-1)
-    comp_lo = (comp_index * STRIDE + KERN - 1).astype(jnp.int32).reshape(1, 1, comp_count)
+    comp_block = comp_index - 1
+    comp_lo = jnp.where(comp_block >= 0, comp_block * STRIDE + KERN - 1, BIG)
+    comp_lo = comp_lo.astype(jnp.int32).reshape(1, 1, comp_count)
     comp_hi = jnp.full((1, 1, comp_count), BIG, jnp.int32)
 
     win_rows = QB + WIN
@@ -253,6 +255,7 @@
         P(None, "head", "ctx"),
         P(),
     )
+
     return jax.shard_map(
         local, mesh=mesh, in_specs=placed, out_specs=P("ctx", "head"), check_vma=False
     )

time: 118 us -> 123 us (1.042)
  waiting for transfers between devices: 31.1 us -> 38.4 us
  starting transfers between devices: 23.8 us -> 20 us
    all_gather x1, waiting for transfers between devices: 0.19 us -> 10.8 us  [local(): gathered = lax.all_gather(arrived, 'head', axis=0, axis_index_groups=groups)]
    ppermute x2 -> x1, waiting for transfers between devices: 10.2 us -> 6.61 us  [shifted(): return lax.ppermute(block, axis, route)]
    ppermute x2 -> x1, starting transfers between devices: 6.64 us -> 4.64 us  [shifted(): return lax.ppermute(block, axis, route)]
    all_to_all x1, starting transfers between devices: 11.7 us -> 9.85 us  [local(): lax.all_to_all(mail, 'ctx', split_axis=0, concat_axis=0, tiled=True)]
  transfers between devices with their start and end apart: 5 -> 4, of which waited for: 5 -> 4; matrix products, arithmetic and copies ran while one was open for 5% -> 4% of each run, Pallas kernels for 7% -> 7%
where the time goes in v5:
time: 123 us; the launch traced here: 120 us
  waiting for transfers between devices  38.4 us (31%)
  Pallas kernels  33.6 us (27%)
  starting transfers between devices  20 us (16%)
  between operations  13.8 us (11%)
  local copies, waits for them, and re-layouts  10.6 us (9%)
  other arithmetic  3.83 us (3%)
    pallas_call x3, Pallas kernels, branch(): pl.pallas_call(kernel, grid=(blocks,), in_specs=in_specs, out_specs=pl.Bl...  33.6 us
    all_to_all x1, waiting for transfers between devices, local(): lax.all_to_all(mail, 'ctx', split_axis=0, concat_axis=0, tiled=True)  12.9 us
    all_gather x1, waiting for transfers between devices, local(): gathered = lax.all_gather(arrived, 'head', axis=0, axis_index_groups=groups)  10.8 us
    all_to_all x1, starting transfers between devices, local(): lax.all_to_all(mail, 'ctx', split_axis=0, concat_axis=0, tiled=True)  9.85 us
    all_to_all x1, waiting for transfers between devices, local(): lax.all_to_all(outbox_kv, 'head', 0, 0, tiled=True)  8.05 us
    ppermute x1, waiting for transfers between devices, shifted(): return lax.ppermute(block, axis, route)  6.61 us
    all_to_all x1, starting transfers between devices, local(): lax.all_to_all(outbox_kv, 'head', 0, 0, tiled=True)  5.5 us
    ppermute x1, starting transfers between devices, shifted(): return lax.ppermute(block, axis, route)  4.64 us
  transfers between devices with their start and end apart: 4, of which 4 were waited for; matrix products, arithmetic and copies ran while one was open for 4% of the time, Pallas kernels for 7%

profile of v5, /device:TPU:32, one launch (start us, length us, event | category | flops | bytes accessed | tf_op | source)
XLA Modules:
  0.0 120.5 jit_solution(11524001458498586045)
XLA Ops:
  6.5 0.9 reshape.332
  7.4 0.9 reshape.333
  8.4 0.8 broadcast_in_dim.42
  9.2 5.5 %all-to-all-start = ((bf16[16,64,256]{2,1,0:T(8,128)(2,1)}), bf16[16,64,256]{2,1,0:T(8,128)(2,1)S(1)}, u32[]{:S(2)}, u32[]{:S(2)}) async-start(bf16[16,64,256]{2,1,0:T(8,128)(2,1)} %bitcast.1), calls=%async_computation | async-start | bytes 1048576 | tf_op jit(solution)/shard_map/all_to_all | solution.py:124
  15.0 0.4 compare_reduce_fusion
  15.5 0.2 reduce_window_sum.18
  15.7 0.1 fusion.7
  15.9 0.4 compare_reduce_fusion.1
  16.3 0.7 constant_dynamic-slice_fusion
  17.1 0.2 reduce_window_sum.17
  17.3 0.1 select_reduce_fusion
  17.5 8.1 %all-to-all-done = bf16[16,64,256]{2,1,0:T(8,128)(2,1)S(1)} async-done(((bf16[16,64,256]{2,1,0:T(8,128)(2,1)}), bf16[16,64,256]{2,1,0:T(8,128)(2,1)S(1)}, u32[]{:S(2)}, u32[]{:S(2)}) %all-to-all-start) | async-done | bytes 524320 | tf_op jit(solution)/shard_map/all_to_all | solution.py:124
  25.6 0.2 copy.34
  25.8 4.6 %collective-permute-start = (bf16[512,256]{1,0:T(8,128)(2,1)S(1)}, bf16[512,256]{1,0:T(8,128)(2,1)S(1)}, u32[]{:S(2)}, u32[]{:S(2)}) collective-permute-start(bf16[512,256]{1,0:T(8,128)(2,1)S(1)} %bitcast.45), channel_id=1, source_target_pairs={{0,16},{16,32},{32,48},{48,64},{64,80},{80,96},{96,112},{112,128},... | collective-permute-start | bytes 786440 | tf_op jit(solution)/shard_map/ppermute | solution.py:27
  30.4 0.2 convolution_convert_fusion
  30.7 0.2 fusion
  30.9 6.6 %collective-permute-done = bf16[512,256]{1,0:T(8,128)(2,1)S(1)} collective-permute-done((bf16[512,256]{1,0:T(8,128)(2,1)S(1)}, bf16[512,256]{1,0:T(8,128)(2,1)S(1)}, u32[]{:S(2)}, u32[]{:S(2)}) %collective-permute-start) | collective-permute-done | bytes 262176 | tf_op jit(solution)/shard_map/ppermute | solution.py:27
  37.5 0.2 fusion.1
  37.8 0.8 pad_maximum_fusion.1
  38.5 9.9 %all-to-all-start.1 = ((bf16[16,48,256]{2,1,0:T(8,128)(2,1)}), bf16[16,48,256]{2,1,0:T(8,128)(2,1)S(1)}, u32[]{:S(2)}, u32[]{:S(2)}) async-start(bf16[16,48,256]{2,1,0:T(8,128)(2,1)} %pad_maximum_fusion.1), calls=%async_computation.1 | async-start | bytes 786432 | tf_op jit(solution)/shard_map/all_to_all | solution.py:180
  48.6 12.9 %all-to-all-done.1 = bf16[16,48,256]{2,1,0:T(8,128)(2,1)S(1)} async-done(((bf16[16,48,256]{2,1,0:T(8,128)(2,1)}), bf16[16,48,256]{2,1,0:T(8,128)(2,1)S(1)}, u32[]{:S(2)}, u32[]{:S(2)}) %all-to-all-start.1) | async-done | bytes 393248 | tf_op jit(solution)/shard_map/all_to_all | solution.py:180
  61.5 0.7 copy-done.3
  62.9 0.5 copy.31
  63.6 0.4 divide_bitcast_fusion
  64.2 1.1 copy-done
  65.3 8.0 %shard_map.73.rest_0_ = f32[1024,512]{1,0:T(8,128)S(1)} custom-call(bf16[1024,512]{1,0:T(8,128)(2,1)S(1)} %copy-done, bf16[1536,256]{1,0:T(8,128)(2,1)S(1)} %pad_maximum_fusion.kv_ref, s32[4,1,768]{2,1,0:T(1,128)S(1)} %get-tuple-element.11.lo_ref, s32[4,1,768]{2,1,0:T(1,128)S(1)} %get-tuple-element.10.hi_ref, s32[1024,1]{1,0:T(8,128)S(1)} %iota_add_fusion.t_ref, ...), custom_call_target="tpu_custom_call" | custom-call | flops 1610612736 | bytes 6029312 | tf_op jit(solution)/shard_map/pallas_call | solution.py:97
  73.3 1.3 %copy-done.1 = f32[1024,512]{1,0:T(8,128)} copy-done((f32[1024,512]{1,0:T(8,128)}, f32[1024,512]{1,0:T(8,128)S(1)}, u32[]{:S(2)}) %copy-start.1) | copy-done | bytes 2097176
  74.6 10.8 %all-gather.3.cloned.1.call-done = bf16[64,48,256]{2,1,0:T(8,128)(2,1)} async-done(((bf16[16,48,256]{2,1,0:T(8,128)(2,1)}), bf16[64,48,256]{2,1,0:T(8,128)(2,1)}) %all-gather.3.cloned.1.call-update) | async-done | bytes 1572880 | tf_op jit(solution)/shard_map/all_gather | solution.py:181
  85.5 1.2 %slice.51 = bf16[4,16,16,256]{3,2,1,0:T(8,128)(2,1)S(1)} slice(bf16[4,16,48,256]{3,2,1,0:T(8,128)(2,1)} %bitcast.39), slice={[0:4], [0:16], [32:48], [0:256]} | slice | bytes 1048576 | tf_op jit(solution)/shard_map/slice | solution.py:183
  86.7 1.3 %slice.49 = bf16[4,16,32,256]{3,2,1,0:T(8,128)(2,1)S(1)} slice(bf16[4,16,48,256]{3,2,1,0:T(8,128)(2,1)} %bitcast.40), slice={[0:4], [0:16], [0:32], [0:256]} | slice | bytes 2097152 | tf_op jit(solution)/shard_map/slice | solution.py:182
  88.0 9.5 %shard_map.74.rest_0_ = f32[1024,512]{1,0:T(8,128)S(1)} custom-call(bf16[1024,512]{1,0:T(8,128)(2,1)S(1)} %copy-done, bf16[1024,256]{1,0:T(8,128)(2,1)S(1)} %bitcast.35, s32[1,1,1024]{2,1,0:T(1,128)S(1)} %reshape.345.lo_ref, s32[1,1,1024]{2,1,0:T(1,128)S(1)} %broadcast_in_dim.84.hi_ref, ...), custom_call_target="tpu_custom_call", output_to_operand_aliasing={{}: (6, {})} | custom-call | flops 2147483648 | bytes 5767168 | tf_op jit(solution)/shard_map/pallas_call | solution.py:97
  97.6 16.1 %shard_map.75 = bf16[1024,512]{1,0:T(8,128)(2,1)} custom-call(bf16[1024,512]{1,0:T(8,128)(2,1)S(1)} %copy-done, bf16[2048,256]{1,0:T(8,128)(2,1)S(1)} %bitcast.34, s32[4,1,2048]{2,1,0:T(1,128)S(1)} %broadcast_select_fusion.lo_ref, s32[1,1,2048]{2,1,0:T(1,128)S(1)} %broadcast_in_dim.83.hi_ref, s32[1024,1]{1,0:T(8,128)S(1)} %iota_add_fusion.t_ref, ...), custom_call_target="tpu_custom_call" | custom-call | flops 4294967296 | bytes 6291456 | tf_op jit(solution)/shard_map/pallas_call | solution.py:97
  (54 shorter events, 1.8 us)
Async XLA Ops:
  6.5 8.3 %copy-start.5 = (s32[64,64]{1,0:T(8,128)S(1)}, s32[64,64]{1,0:T(8,128)}, u32[]{:S(2)}) copy-start(s32[64,64]{1,0:T(8,128)} %param.13) | copy-start | bytes 49156
  9.2 16.3 %all-to-all-start = ((bf16[16,64,256]{2,1,0:T(8,128)(2,1)}), bf16[16,64,256]{2,1,0:T(8,128)(2,1)S(1)}, u32[]{:S(2)}, u32[]{:S(2)}) async-start(bf16[16,64,256]{2,1,0:T(8,128)(2,1)} %bitcast.1), calls=%async_computation | async-start | bytes 1048576 | tf_op jit(solution)/shard_map/all_to_all | solution.py:124
  25.8 11.8 %collective-permute-start = (bf16[512,256]{1,0:T(8,128)(2,1)S(1)}, bf16[512,256]{1,0:T(8,128)(2,1)S(1)}, u32[]{:S(2)}, u32[]{:S(2)}) collective-permute-start(bf16[512,256]{1,0:T(8,128)(2,1)S(1)} %bitcast.45), channel_id=1, source_target_pairs={{0,16},{16,32},{32,48},{48,64},{64,80},{80,96},{96,112},{112,128},... | collective-permute-start | bytes 786440 | tf_op jit(solution)/shard_map/ppermute | solution.py:27
  37.5 25.4 %copy-start.4 = (f32[3,4,1024]{2,1,0:T(4,128)S(1)}, f32[3,4,1024]{2,1,0:T(4,128)}, u32[]{:S(2)}) copy-start(f32[3,4,1024]{2,1,0:T(4,128)} %param.12) | copy-start | bytes 147460
  38.5 23.0 %all-to-all-start.1 = ((bf16[16,48,256]{2,1,0:T(8,128)(2,1)}), bf16[16,48,256]{2,1,0:T(8,128)(2,1)S(1)}, u32[]{:S(2)}, u32[]{:S(2)}) async-start(bf16[16,48,256]{2,1,0:T(8,128)(2,1)} %pad_maximum_fusion.1), calls=%async_computation.1 | async-start | bytes 786432 | tf_op jit(solution)/shard_map/all_to_all | solution.py:180
  48.4 37.1 %all-gather.3.cloned.1.call-start = ((), (), s32[]{:S(2)}) async-start(), calls=%async_computation.2 | async-start | bytes 1966080 | tf_op jit(solution)/shard_map/all_gather | solution.py:181
  61.5 0.7 copy-start.3
  64.1 1.2 %copy-start = (bf16[1024,512]{1,0:T(8,128)(2,1)S(1)}, bf16[1024,512]{1,0:T(8,128)(2,1)}, u32[]{:S(2)}) copy-start(bf16[1024,512]{1,0:T(8,128)(2,1)} %q_ref.5) | copy-start | bytes 3145732
  73.3 1.4 %copy-start.1 = (f32[1024,512]{1,0:T(8,128)}, f32[1024,512]{1,0:T(8,128)S(1)}, u32[]{:S(2)}) copy-start(f32[1024,512]{1,0:T(8,128)S(1)} %shard_map.73.rest_0_) | copy-start | bytes 6291460
  85.5 2.6 %copy-start.2 = (f32[1024,512]{1,0:T(8,128)S(1)}, f32[1024,512]{1,0:T(8,128)}, u32[]{:S(2)}) copy-start(f32[1024,512]{1,0:T(8,128)} %copy-done.1) | copy-start | bytes 6291460
Sparse Core Ops, SparseCore 0:
  62.4 22.9 all-gather.2

commit v6 on v5

--- a/solution.py
+++ b/solution.py
@@ -19,6 +19,7 @@
 QB = 256
 CAP = 2
 BIG = 1 << 30
+CORES = 2
 
 
 def shifted(block, axis, distance):
@@ -148,7 +149,7 @@
 
     block_count = local_rows // QB
     tiles_shard = local_rows // TILE
-    share = (H // G) // local_heads
+    share = CORES
     part = head_index % share
     groups = [[g * share + i for i in range(share)] for g in range(head_count // share)]
     sel_share = CAP * TILE // share
@@ -178,7 +179,12 @@
     )
     mail = jnp.concatenate([sel_part, comp_part], axis=1)
     arrived = lax.all_to_all(mail, "ctx", split_axis=0, concat_axis=0, tiled=True)
-    gathered = lax.all_gather(arrived, "head", axis=0, axis_index_groups=groups)
+    spread = jnp.broadcast_to(arrived[None], (share,) + arrived.shape).reshape(
+        (share * ctx_count,) + arrived.shape[1:]
+    )
+    gathered = lax.all_to_all(
+        spread, "head", 0, 0, axis_index_groups=groups, tiled=True
+    ).reshape((share,) + arrived.shape)
     sel_kv = gathered[:, :, :sel_share].reshape(share * ctx_count * sel_share, 2 * HD)
     comp_kv = gathered[:, :, sel_share:].reshape(share * ctx_count * comp_share, 2 * HD)
     sel_rows = sel_kv.shape[0]

time: 123 us -> 100 us (0.81)
  the two profiles are of different devices: /device:TPU:32 before, /device:TPU:9 now
where the time goes in v6:
time: 100 us; the launch traced here: 99.4 us
  Pallas kernels  33.5 us (34%)
  starting transfers between devices  22.1 us (22%)
  waiting for transfers between devices  20.7 us (21%)
  local copies, waits for them, and re-layouts  10.4 us (10%)
  blocking collectives  8.1 us (8%)
  other arithmetic  3.9 us (4%)
    pallas_call x3, Pallas kernels, branch(): pl.pallas_call(kernel, grid=(blocks,), in_specs=in_specs, out_specs=pl.Bl...  33.5 us
    all_to_all x1, starting transfers between devices, local(): lax.all_to_all(mail, 'ctx', split_axis=0, concat_axis=0, tiled=True)  11.6 us
    all_to_all x1, waiting for transfers between devices, local(): lax.all_to_all(mail, 'ctx', split_axis=0, concat_axis=0, tiled=True)  10.5 us
    all_to_all x1, blocking collectives, local(): lax.all_to_all(spread, 'head', 0, 0, axis_index_groups=groups, tiled=True)  8.1 us
    all_to_all x1, starting transfers between devices, local(): lax.all_to_all(outbox_kv, 'head', 0, 0, tiled=True)  6.14 us
    ppermute x1, waiting for transfers between devices, shifted(): return lax.ppermute(block, axis, route)  5.16 us
    all_to_all x1, waiting for transfers between devices, local(): lax.all_to_all(outbox_kv, 'head', 0, 0, tiled=True)  5.06 us
    unnamed x13, local copies, waits for them, and re-layouts  4.81 us
  transfers between devices with their start and end apart: 3, of which 3 were waited for; matrix products, arithmetic and copies ran while one was open for 5% of the time, Pallas kernels for 8%

profile of v6, /device:TPU:9, one launch (start us, length us, event | category | flops | bytes accessed | tf_op | source)
XLA Modules:
  0.0 99.4 jit_solution(1873357957548997690)
XLA Ops:
  0.0 0.9 reshape.312
  0.9 0.9 reshape.313
  1.8 0.8 broadcast_in_dim.36
  2.7 6.1 %all-to-all-start = ((bf16[16,64,256]{2,1,0:T(8,128)(2,1)}), bf16[16,64,256]{2,1,0:T(8,128)(2,1)S(1)}, u32[]{:S(2)}, u32[]{:S(2)}) async-start(bf16[16,64,256]{2,1,0:T(8,128)(2,1)} %bitcast.1), calls=%async_computation | async-start | bytes 1048576 | tf_op jit(solution)/shard_map/all_to_all | solution.py:125
  9.0 0.4 compare_reduce_fusion
  9.5 0.2 reduce_window_sum.18
  9.7 0.1 select_reduce_fusion
  9.8 0.1 fusion.7
  10.3 0.4 compare_reduce_fusion.1
  10.7 0.7 constant_dynamic-slice_fusion
  11.5 0.2 reduce_window_sum.17
  11.9 5.1 %all-to-all-done = bf16[16,64,256]{2,1,0:T(8,128)(2,1)S(1)} async-done(((bf16[16,64,256]{2,1,0:T(8,128)(2,1)}), bf16[16,64,256]{2,1,0:T(8,128)(2,1)S(1)}, u32[]{:S(2)}, u32[]{:S(2)}) %all-to-all-start) | async-done | bytes 524320 | tf_op jit(solution)/shard_map/all_to_all | solution.py:125
  17.0 4.4 %collective-permute-start = (bf16[512,256]{1,0:T(8,128)(2,1)S(1)}, bf16[512,256]{1,0:T(8,128)(2,1)S(1)}, u32[]{:S(2)}, u32[]{:S(2)}) collective-permute-start(bf16[512,256]{1,0:T(8,128)(2,1)S(1)} %bitcast.46), channel_id=1, source_target_pairs={{0,16},{16,32},{32,48},{48,64},{64,80},{80,96},{96,112},{112,128},... | collective-permute-start | bytes 786440 | tf_op jit(solution)/shard_map/ppermute | solution.py:28
  21.3 0.3 copy.24
  21.6 0.3 convolution_convert_fusion
  21.9 0.1 copy.25
  22.0 0.2 fusion
  22.3 5.2 %collective-permute-done = bf16[512,256]{1,0:T(8,128)(2,1)S(1)} collective-permute-done((bf16[512,256]{1,0:T(8,128)(2,1)S(1)}, bf16[512,256]{1,0:T(8,128)(2,1)S(1)}, u32[]{:S(2)}, u32[]{:S(2)}) %collective-permute-start) | collective-permute-done | bytes 262176 | tf_op jit(solution)/shard_map/ppermute | solution.py:28
  27.4 0.2 fusion.1
  27.7 0.9 pad_maximum_fusion.1
  28.7 11.6 %all-to-all-start.1 = ((bf16[16,96,256]{2,1,0:T(8,128)(2,1)}), bf16[16,96,256]{2,1,0:T(8,128)(2,1)}, u32[]{:S(2)}, u32[]{:S(2)}) async-start(bf16[16,96,256]{2,1,0:T(8,128)(2,1)} %pad_maximum_fusion.1), calls=%async_computation.1 | async-start | bytes 1572864 | tf_op jit(solution)/shard_map/all_to_all | solution.py:181
  40.7 0.5 copy.21
  41.2 0.4 divide_bitcast_fusion
  41.9 1.1 %copy-done = bf16[1024,512]{1,0:T(8,128)(2,1)S(1)} copy-done((bf16[1024,512]{1,0:T(8,128)(2,1)S(1)}, bf16[1024,512]{1,0:T(8,128)(2,1)}, u32[]{:S(2)}) %copy-start) | copy-done | bytes 1048600
  43.0 7.9 %shard_map.73.rest_0_ = f32[1024,512]{1,0:T(8,128)S(1)} custom-call(bf16[1024,512]{1,0:T(8,128)(2,1)S(1)} %copy-done, bf16[1536,256]{1,0:T(8,128)(2,1)S(1)} %pad_maximum_fusion.kv_ref, s32[4,1,768]{2,1,0:T(1,128)S(1)} %get-tuple-element.11.lo_ref, s32[4,1,768]{2,1,0:T(1,128)S(1)} %get-tuple-element.10.hi_ref, s32[1024,1]{1,0:T(8,128)S(1)} %iota_add_fusion.t_ref, ...), custom_call_target="tpu_custom_call" | custom-call | flops 1610612736 | bytes 6029312 | tf_op jit(solution)/shard_map/pallas_call | solution.py:98
  50.8 1.3 %copy-done.1 = f32[1024,512]{1,0:T(8,128)} copy-done((f32[1024,512]{1,0:T(8,128)}, f32[1024,512]{1,0:T(8,128)S(1)}, u32[]{:S(2)}) %copy-start.1) | copy-done | bytes 2097176
  52.2 10.5 %all-to-all-done.1 = bf16[16,96,256]{2,1,0:T(8,128)(2,1)} async-done(((bf16[16,96,256]{2,1,0:T(8,128)(2,1)}), bf16[16,96,256]{2,1,0:T(8,128)(2,1)}, u32[]{:S(2)}, u32[]{:S(2)}) %all-to-all-start.1) | async-done | bytes 786464 | tf_op jit(solution)/shard_map/all_to_all | solution.py:181
  62.7 1.3 %broadcast_in_dim.38 = bf16[2,16,96,256]{3,2,1,0:T(8,128)(2,1)S(1)} broadcast(bf16[16,96,256]{2,1,0:T(8,128)(2,1)} %all-to-all-done.1), dimensions={1,2,3} | broadcast | bytes 2359296 | tf_op jit(solution)/shard_map/broadcast_in_dim | solution.py:182
  64.0 8.1 %all_to_all.15 = bf16[32,96,256]{2,1,0:T(8,128)(2,1)S(1)} all-to-all(bf16[32,96,256]{2,1,0:T(8,128)(2,1)S(1)} %bitcast.42), channel_id=1, replica_groups={{0,1},{2,3},{4,5},{6,7},{8,9},{10,11},{12,13},{14,15},{16,17},{18,19},{..., dimensions={0} | all-to-all | bytes 3145728 | tf_op jit(solution)/shard_map/all_to_all | solution.py:185
  72.3 1.5 %copy-done.2 = f32[1024,512]{1,0:T(8,128)S(1)} copy-done((f32[1024,512]{1,0:T(8,128)S(1)}, f32[1024,512]{1,0:T(8,128)}, u32[]{:S(2)}) %copy-start.2) | copy-done | bytes 2097176
  73.7 9.6 %shard_map.74.rest_0_ = f32[1024,512]{1,0:T(8,128)S(1)} custom-call(bf16[1024,512]{1,0:T(8,128)(2,1)S(1)} %copy-done, bf16[1024,256]{1,0:T(8,128)(2,1)S(1)} %bitcast.35, s32[1,1,1024]{2,1,0:T(1,128)S(1)} %reshape.326.lo_ref, s32[1,1,1024]{2,1,0:T(1,128)S(1)} %broadcast_in_dim.50.hi_ref, ...), custom_call_target="tpu_custom_call", output_to_operand_aliasing={{}: (6, {})} | custom-call | flops 2147483648 | bytes 5767168 | tf_op jit(solution)/shard_map/pallas_call | solution.py:98
  83.3 16.1 %shard_map.75 = bf16[1024,512]{1,0:T(8,128)(2,1)} custom-call(bf16[1024,512]{1,0:T(8,128)(2,1)S(1)} %copy-done, bf16[2048,256]{1,0:T(8,128)(2,1)S(1)} %bitcast.34, s32[4,1,2048]{2,1,0:T(1,128)S(1)} %broadcast_select_fusion.lo_ref, s32[1,1,2048]{2,1,0:T(1,128)S(1)} %broadcast_in_dim.49.hi_ref, s32[1024,1]{1,0:T(8,128)S(1)} %iota_add_fusion.t_ref, ...), custom_call_target="tpu_custom_call" | custom-call | flops 4294967296 | bytes 6291456 | tf_op jit(solution)/shard_map/pallas_call | solution.py:98
  (44 shorter events, 1.6 us)
Async XLA Ops:
  0.0 8.9 %copy-start.4 = (s32[64,64]{1,0:T(8,128)S(1)}, s32[64,64]{1,0:T(8,128)}, u32[]{:S(2)}) copy-start(s32[64,64]{1,0:T(8,128)} %param.13) | copy-start | bytes 49156
  2.7 14.3 %all-to-all-start = ((bf16[16,64,256]{2,1,0:T(8,128)(2,1)}), bf16[16,64,256]{2,1,0:T(8,128)(2,1)S(1)}, u32[]{:S(2)}, u32[]{:S(2)}) async-start(bf16[16,64,256]{2,1,0:T(8,128)(2,1)} %bitcast.1), calls=%async_computation | async-start | bytes 1048576 | tf_op jit(solution)/shard_map/all_to_all | solution.py:125
  17.0 10.5 %collective-permute-start = (bf16[512,256]{1,0:T(8,128)(2,1)S(1)}, bf16[512,256]{1,0:T(8,128)(2,1)S(1)}, u32[]{:S(2)}, u32[]{:S(2)}) collective-permute-start(bf16[512,256]{1,0:T(8,128)(2,1)S(1)} %bitcast.46), channel_id=1, source_target_pairs={{0,16},{16,32},{32,48},{48,64},{64,80},{80,96},{96,112},{112,128},... | collective-permute-start | bytes 786440 | tf_op jit(solution)/shard_map/ppermute | solution.py:28
  27.7 13.0 %copy-start.3 = (f32[3,4,1024]{2,1,0:T(4,128)S(1)}, f32[3,4,1024]{2,1,0:T(4,128)}, u32[]{:S(2)}) copy-start(f32[3,4,1024]{2,1,0:T(4,128)} %param.12) | copy-start | bytes 147460
  28.7 34.0 %all-to-all-start.1 = ((bf16[16,96,256]{2,1,0:T(8,128)(2,1)}), bf16[16,96,256]{2,1,0:T(8,128)(2,1)}, u32[]{:S(2)}, u32[]{:S(2)}) async-start(bf16[16,96,256]{2,1,0:T(8,128)(2,1)} %pad_maximum_fusion.1), calls=%async_computation.1 | async-start | bytes 1572864 | tf_op jit(solution)/shard_map/all_to_all | solution.py:181
  41.7 1.2 %copy-start = (bf16[1024,512]{1,0:T(8,128)(2,1)S(1)}, bf16[1024,512]{1,0:T(8,128)(2,1)}, u32[]{:S(2)}) copy-start(bf16[1024,512]{1,0:T(8,128)(2,1)} %q_ref.5) | copy-start | bytes 3145732
  50.8 1.4 %copy-start.1 = (f32[1024,512]{1,0:T(8,128)}, f32[1024,512]{1,0:T(8,128)S(1)}, u32[]{:S(2)}) copy-start(f32[1024,512]{1,0:T(8,128)S(1)} %shard_map.73.rest_0_) | copy-start | bytes 6291460
  72.1 1.6 %copy-start.2 = (f32[1024,512]{1,0:T(8,128)S(1)}, f32[1024,512]{1,0:T(8,128)}, u32[]{:S(2)}) copy-start(f32[1024,512]{1,0:T(8,128)} %copy-done.1) | copy-start | bytes 6291460

commit v7 on v6

--- a/solution.py
+++ b/solution.py
@@ -28,14 +28,23 @@
     return lax.ppermute(block, axis, route)
 
 
-def branch_kernel(q_ref, kv_ref, lo_ref, hi_ref, t_ref, g_ref, *rest, sink, key_rows, row_step, heads):
-    if len(rest) == 2:
-        acc_ref, o_ref = rest
+def branch_kernel(*refs, sink, key_rows, row_step, heads, picks, with_acc):
+    if picks:
+        pick_ref, refs = refs[0], refs[1:]
+        refs, pool_ref = refs[:-1], refs[-1]
+    q_ref, kv_ref, lo_ref, hi_ref, t_ref, g_ref = refs[:6]
+    if with_acc:
+        acc_ref, o_ref = refs[6:]
     else:
         acc_ref = None
-        (o_ref,) = rest
+        (o_ref,) = refs[6:]
     block = pl.program_id(0)
-    if row_step:
+    if picks:
+        for k in range(picks):
+            begin = pl.multiple_of(pick_ref[block, k] * TILE, TILE)
+            pool_ref[k * TILE : (k + 1) * TILE, :] = kv_ref[pl.ds(begin, TILE), :]
+        kv = pool_ref[...]
+    elif row_step:
         start = pl.multiple_of(block * row_step, row_step)
         kv = kv_ref[pl.ds(start, key_rows), :]
     else:
@@ -65,29 +74,34 @@
         o_ref[:, h * HD : (h + 1) * HD] = r.astype(o_ref.dtype)
 
 
-def branch(q, kv, lo, hi, t, gate, acc, *, sink, key_rows, row_step, out_dtype):
+def branch(q, kv, lo, hi, t, gate, acc, *, sink, key_rows, row_step, out_dtype, pick=None):
     rows, width = q.shape
     heads = width // HD
     blocks = rows // QB
-    lo_map = (lambda i: (i, 0, 0)) if lo.shape[0] > 1 else (lambda i: (0, 0, 0))
-    hi_map = (lambda i: (i, 0, 0)) if hi.shape[0] > 1 else (lambda i: (0, 0, 0))
+    lo_map = (lambda i, *_: (i, 0, 0)) if lo.shape[0] > 1 else (lambda i, *_: (0, 0, 0))
+    hi_map = (lambda i, *_: (i, 0, 0)) if hi.shape[0] > 1 else (lambda i, *_: (0, 0, 0))
+    row_map = lambda i, *_: (i, 0)
     in_specs = [
-        pl.BlockSpec((QB, width), lambda i: (i, 0)),
-        pl.BlockSpec(kv.shape, lambda i: (0, 0)),
+        pl.BlockSpec((QB, width), row_map),
+        pl.BlockSpec(kv.shape, lambda i, *_: (0, 0)),
         pl.BlockSpec((1,) + lo.shape[1:], lo_map),
         pl.BlockSpec((1,) + hi.shape[1:], hi_map),
-        pl.BlockSpec((QB, 1), lambda i: (i, 0)),
-        pl.BlockSpec((QB, gate.shape[1]), lambda i: (i, 0)),
+        pl.BlockSpec((QB, 1), row_map),
+        pl.BlockSpec((QB, gate.shape[1]), row_map),
     ]
     args = [q, kv, lo, hi, t, gate]
     aliases = {}
+    prefix = 0 if pick is None else 1
     if acc is not None:
-        in_specs.append(pl.BlockSpec((QB, width), lambda i: (i, 0)))
+        in_specs.append(pl.BlockSpec((QB, width), row_map))
         args.append(acc)
         if acc.dtype == out_dtype:
-            aliases = {len(args) - 1: 0}
+            aliases = {len(args) - 1 + prefix: 0}
+    picks = 0 if pick is None else pick.shape[1]
+    scratch = [] if pick is None else [pltpu.VMEM((key_rows, kv.shape[1]), kv.dtype)]
     kernel = functools.partial(
-        branch_kernel, sink=sink, key_rows=key_rows, row_step=row_step, heads=heads
+        branch_kernel, sink=sink, key_rows=key_rows, row_step=row_step, heads=heads,
+        picks=picks, with_acc=acc is not None,
     )
     flops = 4 * rows * heads * key_rows * HD
     cost = pl.CostEstimate(
@@ -95,11 +109,17 @@
         transcendentals=rows * heads * key_rows,
         bytes_accessed=q.size * 2 + kv.size * 2 + rows * width * 8,
     )
+    if pick is not None:
+        args = [pick] + args
     return pl.pallas_call(
         kernel,
-        grid=(blocks,),
-        in_specs=in_specs,
-        out_specs=pl.BlockSpec((QB, width), lambda i: (i, 0)),
+        grid_spec=pltpu.PrefetchScalarGridSpec(
+            num_scalar_prefetch=prefix,
+            grid=(blocks,),
+            in_specs=in_specs,
+            out_specs=pl.BlockSpec((QB, width), row_map),
+            scratch_shapes=scratch,
+        ),
         out_shape=jax.ShapeDtypeStruct((rows, width), out_dtype),
         input_output_aliases=aliases,
         compiler_params=pltpu.CompilerParams(
@@ -187,7 +207,6 @@
     ).reshape((share,) + arrived.shape)
     sel_kv = gathered[:, :, :sel_share].reshape(share * ctx_count * sel_share, 2 * HD)
     comp_kv = gathered[:, :, sel_share:].reshape(share * ctx_count * comp_share, 2 * HD)
-    sel_rows = sel_kv.shape[0]
     comp_count = comp_kv.shape[0]
     all_ids = jnp.arange(ctx_count * tiles_shard).reshape(ctx_count, tiles_shard)
     wanted = jnp.any(own_flat[:, None, None] == all_ids[None, :, :], axis=0)
@@ -209,8 +228,18 @@
         jnp.repeat(is_named, parts_per_slot, axis=2).transpose(0, 2, 1)[:, :, :, None],
         (block_count, share, ctx_count, sel_share),
     ).reshape(block_count, -1)
-    sel_lo = jnp.where(key_named, key_pos[None, :], BIG).reshape(block_count, 1, sel_rows)
-    never = jnp.full((1, 1, sel_rows), BIG, jnp.int32)
+    slot_named = key_named.reshape(block_count, share * ctx_count, TILE)[:, :, 0]
+    slot_base = key_pos.reshape(share * ctx_count, TILE)[:, 0]
+    slot_rank = jnp.cumsum(slot_named.astype(jnp.int32), axis=1) - 1
+    hit = slot_named[:, None, :] & (slot_rank[:, None, :] == jnp.arange(TOPK)[None, :, None])
+    pick = jnp.sum(
+        jnp.where(hit, jnp.arange(share * ctx_count)[None, None, :], 0), axis=2
+    ).astype(jnp.int32)
+    pick_base = jnp.sum(jnp.where(hit, slot_base[None, None, :], 0), axis=2)
+    pick_ok = jnp.any(hit, axis=2)
+    pick_pos = pick_base[:, :, None] + jnp.arange(TILE)[None, None, :]
+    sel_lo = jnp.where(pick_ok[:, :, None], pick_pos, BIG).reshape(block_count, 1, TOPK * TILE)
+    never = jnp.full((1, 1, TOPK * TILE), BIG, jnp.int32)
 
     comp_index = (
         jnp.arange(ctx_count)[None, :, None] * comp_local
@@ -247,7 +276,7 @@
     )
     return branch(
         queries, sel_kv, sel_lo, never, positions, gate_values[1], acc,
-        sink=True, key_rows=sel_rows, row_step=0, out_dtype=jnp.bfloat16,
+        sink=True, key_rows=TOPK * TILE, row_step=0, out_dtype=jnp.bfloat16, pick=pick,
     )
 
 

time: 100 us -> 94.7 us (0.947)
  the two profiles are of different devices: /device:TPU:9 before, /device:TPU:3 now
where the time goes in v7:
time: 94.7 us; the launch traced here: 94.1 us
  Pallas kernels  28.4 us (30%)
  starting transfers between devices  22.3 us (24%)
  waiting for transfers between devices  19.8 us (21%)
  local copies, waits for them, and re-layouts  10.8 us (11%)
  blocking collectives  7.9 us (8%)
  other arithmetic  4.41 us (5%)
    pallas_call x3, Pallas kernels, branch(): pl.pallas_call(kernel, grid_spec=pltpu.PrefetchScalarGridSpec(num_scalar_...  28.4 us
    all_to_all x1, starting transfers between devices, local(): lax.all_to_all(mail, 'ctx', split_axis=0, concat_axis=0, tiled=True)  12.3 us
    all_to_all x1, waiting for transfers between devices, local(): lax.all_to_all(mail, 'ctx', split_axis=0, concat_axis=0, tiled=True)  9.72 us
    all_to_all x1, blocking collectives, local(): lax.all_to_all(spread, 'head', 0, 0, axis_index_groups=groups, tiled=True)  7.9 us
    all_to_all x1, starting transfers between devices, local(): lax.all_to_all(outbox_kv, 'head', 0, 0, tiled=True)  6.23 us
    all_to_all x1, waiting for transfers between devices, local(): lax.all_to_all(outbox_kv, 'head', 0, 0, tiled=True)  5.73 us
    unnamed x13, local copies, waits for them, and re-layouts  4.87 us
    ppermute x1, waiting for transfers between devices, shifted(): return lax.ppermute(block, axis, route)  4.31 us
  transfers between devices with their start and end apart: 3, of which 3 were waited for; matrix products, arithmetic and copies ran while one was open for 7% of the time, Pallas kernels for 8%

profile of v7, /device:TPU:3, one launch (start us, length us, event | category | flops | bytes accessed | tf_op | source)
XLA Modules:
  0.0 94.1 jit_solution(7029254504507651362)
XLA Ops:
  0.0 0.9 reshape.334
  0.9 0.9 reshape.335
  1.8 0.8 broadcast_in_dim.101
  2.7 6.2 %all-to-all-start = ((bf16[16,64,256]{2,1,0:T(8,128)(2,1)}), bf16[16,64,256]{2,1,0:T(8,128)(2,1)S(1)}, u32[]{:S(2)}, u32[]{:S(2)}) async-start(bf16[16,64,256]{2,1,0:T(8,128)(2,1)} %bitcast.3), calls=%async_computation | async-start | bytes 1048576 | tf_op jit(solution)/shard_map/all_to_all | solution.py:145
  9.1 0.4 compare_reduce_fusion.1
  9.6 0.2 reduce_window_sum.28
  10.4 0.2 reduce_window_sum.29
  10.6 0.1 fusion.5
  10.7 0.2 select_reduce_fusion
  11.1 0.4 compare_reduce_fusion
  11.5 0.7 constant_dynamic-slice_fusion
  12.3 0.2 reduce_window_sum.30
  12.6 5.7 %all-to-all-done = bf16[16,64,256]{2,1,0:T(8,128)(2,1)S(1)} async-done(((bf16[16,64,256]{2,1,0:T(8,128)(2,1)}), bf16[16,64,256]{2,1,0:T(8,128)(2,1)S(1)}, u32[]{:S(2)}, u32[]{:S(2)}) %all-to-all-start) | async-done | bytes 524320 | tf_op jit(solution)/shard_map/all_to_all | solution.py:145
  18.4 3.8 %collective-permute-start = (bf16[512,256]{1,0:T(8,128)(2,1)S(1)}, bf16[512,256]{1,0:T(8,128)(2,1)S(1)}, u32[]{:S(2)}, u32[]{:S(2)}) collective-permute-start(bf16[512,256]{1,0:T(8,128)(2,1)S(1)} %bitcast.46), channel_id=1, source_target_pairs={{0,16},{16,32},{32,48},{48,64},{64,80},{80,96},{96,112},{112,128},... | collective-permute-start | bytes 786440 | tf_op jit(solution)/shard_map/ppermute | solution.py:28
  22.2 0.3 copy.24
  22.5 0.3 convolution_convert_fusion
  22.9 0.2 fusion
  23.1 4.3 %collective-permute-done = bf16[512,256]{1,0:T(8,128)(2,1)S(1)} collective-permute-done((bf16[512,256]{1,0:T(8,128)(2,1)S(1)}, bf16[512,256]{1,0:T(8,128)(2,1)S(1)}, u32[]{:S(2)}, u32[]{:S(2)}) %collective-permute-start) | collective-permute-done | bytes 262176 | tf_op jit(solution)/shard_map/ppermute | solution.py:28
  27.4 0.2 fusion.1
  27.7 0.9 pad_maximum_fusion.1
  28.6 12.3 %all-to-all-start.1 = ((bf16[16,96,256]{2,1,0:T(8,128)(2,1)}), bf16[16,96,256]{2,1,0:T(8,128)(2,1)}, u32[]{:S(2)}, u32[]{:S(2)}) async-start(bf16[16,96,256]{2,1,0:T(8,128)(2,1)} %pad_maximum_fusion.1), calls=%async_computation.1 | async-start | bytes 1572864 | tf_op jit(solution)/shard_map/all_to_all | solution.py:201
  41.5 0.5 copy.21
  42.1 0.4 divide_bitcast_fusion
  42.7 1.2 %copy-done = bf16[1024,512]{1,0:T(8,128)(2,1)S(1)} copy-done((bf16[1024,512]{1,0:T(8,128)(2,1)S(1)}, bf16[1024,512]{1,0:T(8,128)(2,1)}, u32[]{:S(2)}) %copy-start) | copy-done | bytes 1048600
  43.9 7.9 %shard_map.73.refs_6_ = f32[1024,512]{1,0:T(8,128)S(1)} custom-call(bf16[1024,512]{1,0:T(8,128)(2,1)S(1)} %copy-done, bf16[1536,256]{1,0:T(8,128)(2,1)S(1)} %pad_maximum_fusion.refs_1_, s32[4,1,768]{2,1,0:T(1,128)S(1)} %get-tuple-element.13.refs_2_, s32[4,1,768]{2,1,0:T(1,128)S(1)} %get-tuple-element.12.refs_3_, s32[1024,1]{1,0:T(8,128)S(1)} %iota_add_fusion.refs_4_.refs_5_, ...), custom_call_target="tpu_custom_call" | custom-call | flops 1610612736 | bytes 6029312 | tf_op jit(solution)/shard_map/pallas_call | solution.py:114
  51.8 1.3 %copy-done.1 = f32[1024,512]{1,0:T(8,128)} copy-done((f32[1024,512]{1,0:T(8,128)}, f32[1024,512]{1,0:T(8,128)S(1)}, u32[]{:S(2)}) %copy-start.1) | copy-done | bytes 2097176
  53.1 9.7 %all-to-all-done.1 = bf16[16,96,256]{2,1,0:T(8,128)(2,1)} async-done(((bf16[16,96,256]{2,1,0:T(8,128)(2,1)}), bf16[16,96,256]{2,1,0:T(8,128)(2,1)}, u32[]{:S(2)}, u32[]{:S(2)}) %all-to-all-start.1) | async-done | bytes 786464 | tf_op jit(solution)/shard_map/all_to_all | solution.py:201
  62.8 1.3 %broadcast_in_dim.103 = bf16[2,16,96,256]{3,2,1,0:T(8,128)(2,1)S(1)} broadcast(bf16[16,96,256]{2,1,0:T(8,128)(2,1)} %all-to-all-done.1), dimensions={1,2,3} | broadcast | bytes 2359296 | tf_op jit(solution)/shard_map/broadcast_in_dim | solution.py:202
  64.2 7.9 %all_to_all.15 = bf16[32,96,256]{2,1,0:T(8,128)(2,1)S(1)} all-to-all(bf16[32,96,256]{2,1,0:T(8,128)(2,1)S(1)} %bitcast.42), channel_id=1, replica_groups={{0,1},{2,3},{4,5},{6,7},{8,9},{10,11},{12,13},{14,15},{16,17},{18,19},{..., dimensions={0} | all-to-all | bytes 3145728 | tf_op jit(solution)/shard_map/all_to_all | solution.py:205
  72.2 1.5 %copy-done.2 = f32[1024,512]{1,0:T(8,128)S(1)} copy-done((f32[1024,512]{1,0:T(8,128)S(1)}, f32[1024,512]{1,0:T(8,128)}, u32[]{:S(2)}) %copy-start.2) | copy-done | bytes 2097176
  73.7 9.6 %shard_map.74.refs_7_ = f32[1024,512]{1,0:T(8,128)S(1)} custom-call(bf16[1024,512]{1,0:T(8,128)(2,1)S(1)} %copy-done, bf16[1024,256]{1,0:T(8,128)(2,1)S(1)} %bitcast.35, s32[1,1,1024]{2,1,0:T(1,128)S(1)} %reshape.347.refs_2_, s32[1,1,1024]{2,1,0:T(1,128)S(1)} %broadcast_15_refs_3__refs_4_.2.refs_3_.refs_4_, ...), custom_call_target="tpu_custom_call", output_to_operand_aliasing={{}: (6, {})} | custom-call | flops 2147483648 | bytes 5767168 | tf_op jit(solution)/shard_map/pallas_call | solution.py:114
  83.3 10.9 %shard_map.75 = bf16[1024,512]{1,0:T(8,128)(2,1)} custom-call(s32[4,16]{1,0:T(4,128)S(1)} %get-tuple-element.6.refs_0_, bf16[1024,512]{1,0:T(8,128)(2,1)S(1)} %copy-done, bf16[2048,256]{1,0:T(8,128)(2,1)S(1)} %bitcast.34, s32[4,1,1024]{2,1,0:T(1,128)S(1)} %add_select_fusion.1.refs_3_, s32[1,1,1024]{2,1,0:T(1,128)S(1)} %broadcast_15_refs_3__refs_4_.2.refs_3_.refs_4_, ...), custom_call_target="tpu_custom_call" | custom-call | flops 2147483648 | bytes 6291456 | tf_op jit(solution)/shard_map/pallas_call | solution.py:114
  (53 shorter events, 2.2 us)
Async XLA Ops:
  0.0 8.9 %copy-start.4 = (s32[64,64]{1,0:T(8,128)S(1)}, s32[64,64]{1,0:T(8,128)}, u32[]{:S(2)}) copy-start(s32[64,64]{1,0:T(8,128)} %param.13) | copy-start | bytes 49156
  2.7 15.7 %all-to-all-start = ((bf16[16,64,256]{2,1,0:T(8,128)(2,1)}), bf16[16,64,256]{2,1,0:T(8,128)(2,1)S(1)}, u32[]{:S(2)}, u32[]{:S(2)}) async-start(bf16[16,64,256]{2,1,0:T(8,128)(2,1)} %bitcast.3), calls=%async_computation | async-start | bytes 1048576 | tf_op jit(solution)/shard_map/all_to_all | solution.py:145
  18.4 9.0 %collective-permute-start = (bf16[512,256]{1,0:T(8,128)(2,1)S(1)}, bf16[512,256]{1,0:T(8,128)(2,1)S(1)}, u32[]{:S(2)}, u32[]{:S(2)}) collective-permute-start(bf16[512,256]{1,0:T(8,128)(2,1)S(1)} %bitcast.46), channel_id=1, source_target_pairs={{0,16},{16,32},{32,48},{48,64},{64,80},{80,96},{96,112},{112,128},... | collective-permute-start | bytes 786440 | tf_op jit(solution)/shard_map/ppermute | solution.py:28
  27.7 13.8 %copy-start.3 = (f32[3,4,1024]{2,1,0:T(4,128)S(1)}, f32[3,4,1024]{2,1,0:T(4,128)}, u32[]{:S(2)}) copy-start(f32[3,4,1024]{2,1,0:T(4,128)} %param.12) | copy-start | bytes 147460
  28.6 34.2 %all-to-all-start.1 = ((bf16[16,96,256]{2,1,0:T(8,128)(2,1)}), bf16[16,96,256]{2,1,0:T(8,128)(2,1)}, u32[]{:S(2)}, u32[]{:S(2)}) async-start(bf16[16,96,256]{2,1,0:T(8,128)(2,1)} %pad_maximum_fusion.1), calls=%async_computation.1 | async-start | bytes 1572864 | tf_op jit(solution)/shard_map/all_to_all | solution.py:201
  42.6 1.2 %copy-start = (bf16[1024,512]{1,0:T(8,128)(2,1)S(1)}, bf16[1024,512]{1,0:T(8,128)(2,1)}, u32[]{:S(2)}) copy-start(bf16[1024,512]{1,0:T(8,128)(2,1)} %refs_1_.1) | copy-start | bytes 3145732
  51.8 1.4 %copy-start.1 = (f32[1024,512]{1,0:T(8,128)}, f32[1024,512]{1,0:T(8,128)S(1)}, u32[]{:S(2)}) copy-start(f32[1024,512]{1,0:T(8,128)S(1)} %shard_map.73.refs_6_) | copy-start | bytes 6291460
  72.1 1.6 %copy-start.2 = (f32[1024,512]{1,0:T(8,128)S(1)}, f32[1024,512]{1,0:T(8,128)}, u32[]{:S(2)}) copy-start(f32[1024,512]{1,0:T(8,128)} %copy-done.1) | copy-start | bytes 6291460

commit v8 on v7

--- a/solution.py
+++ b/solution.py
@@ -145,9 +145,8 @@
     group_kv = lax.all_to_all(outbox_kv, "head", 0, 0, tiled=True).reshape(
         local_rows, 2 * HD
     )
-    previous = shifted(group_kv[local_rows - WIN :], "ctx", 1)
-    window_kv = jnp.concatenate([previous, group_kv], axis=0)
-    extended = window_kv[WIN - STRIDE :]
+    tail_rows = shifted(group_kv[: KERN - STRIDE], "ctx", -1)
+    extended = jnp.concatenate([group_kv, tail_rows], axis=0)
     comp_weight = jnp.concatenate(
         [
             lax.dynamic_slice_in_dim(comp_k_weight, group_index * HD, HD, 1),
@@ -246,9 +245,7 @@
         + jnp.arange(share)[:, None, None] * comp_share
         + jnp.arange(comp_share)[None, None, :]
     ).reshape(-1)
-    comp_block = comp_index - 1
-    comp_lo = jnp.where(comp_block >= 0, comp_block * STRIDE + KERN - 1, BIG)
-    comp_lo = comp_lo.astype(jnp.int32).reshape(1, 1, comp_count)
+    comp_lo = (comp_index * STRIDE + KERN - 1).astype(jnp.int32).reshape(1, 1, comp_count)
     comp_hi = jnp.full((1, 1, comp_count), BIG, jnp.int32)
 
     win_rows = QB + WIN
@@ -266,6 +263,8 @@
     )
     gate_values = jax.nn.sigmoid(gate_logits).transpose(0, 2, 1)
 
+    previous = shifted(group_kv[local_rows - WIN :], "ctx", 1)
+    window_kv = jnp.concatenate([previous, group_kv], axis=0)
     acc = branch(
         queries, window_kv, win_lo, win_hi, positions, gate_values[2], None,
         sink=False, key_rows=win_rows, row_step=QB, out_dtype=jnp.float32,

time: 94.7 us -> 102 us (1.077)
  the two profiles are of different devices: /device:TPU:3 before, /device:TPU:32 now
where the time goes in v8:
time: 102 us; the launch traced here: 101 us
  Pallas kernels  28.4 us (28%)
  waiting for transfers between devices  26.7 us (26%)
  starting transfers between devices  26.2 us (26%)
  local copies, waits for them, and re-layouts  9.61 us (9%)
  blocking collectives  5 us (5%)
  other arithmetic  4.41 us (4%)
    pallas_call x3, Pallas kernels, branch(): pl.pallas_call(kernel, grid_spec=pltpu.PrefetchScalarGridSpec(num_scalar_...  28.4 us
    ppermute x2, waiting for transfers between devices, shifted(): return lax.ppermute(block, axis, route)  19.6 us
    all_to_all x1, starting transfers between devices, local(): lax.all_to_all(mail, 'ctx', split_axis=0, concat_axis=0, tiled=True)  11.7 us
    ppermute x2, starting transfers between devices, shifted(): return lax.ppermute(block, axis, route)  9.05 us
    all_to_all x1, waiting for transfers between devices, local(): lax.all_to_all(outbox_kv, 'head', 0, 0, tiled=True)  7.07 us
    all_to_all x1, starting transfers between devices, local(): lax.all_to_all(outbox_kv, 'head', 0, 0, tiled=True)  5.5 us
    all_to_all x1, blocking collectives, local(): lax.all_to_all(spread, 'head', 0, 0, axis_index_groups=groups, tiled=True)  5 us
    unnamed x13, local copies, waits for them, and re-layouts  3.72 us
  transfers between devices with their start and end apart: 4, of which 3 were waited for; matrix products, arithmetic and copies ran while one was open for 6% of the time, Pallas kernels for 8%

profile of v8, /device:TPU:32, one launch (start us, length us, event | category | flops | bytes accessed | tf_op | source)
XLA Modules:
  0.0 101.0 jit_solution(16634411763487148606)
XLA Ops:
  0.0 0.9 reshape.319
  0.9 0.9 reshape.320
  1.8 0.8 broadcast_in_dim.99
  2.7 5.5 %all-to-all-start = ((bf16[16,64,256]{2,1,0:T(8,128)(2,1)}), bf16[16,64,256]{2,1,0:T(8,128)(2,1)S(1)}, u32[]{:S(2)}, u32[]{:S(2)}) async-start(bf16[16,64,256]{2,1,0:T(8,128)(2,1)} %bitcast.3), calls=%async_computation | async-start | bytes 1048576 | tf_op jit(solution)/shard_map/all_to_all | solution.py:145
  8.4 0.4 compare_reduce_fusion.1
  8.9 0.2 reduce_window_sum.28
  9.7 0.2 reduce_window_sum.29
  9.9 0.1 fusion.4
  10.0 0.2 select_reduce_fusion
  10.4 0.4 compare_reduce_fusion
  10.8 0.7 constant_dynamic-slice_fusion
  11.6 0.2 reduce_window_sum.30
  11.9 7.1 %all-to-all-done = bf16[16,64,256]{2,1,0:T(8,128)(2,1)S(1)} async-done(((bf16[16,64,256]{2,1,0:T(8,128)(2,1)}), bf16[16,64,256]{2,1,0:T(8,128)(2,1)S(1)}, u32[]{:S(2)}, u32[]{:S(2)}) %all-to-all-start) | async-done | bytes 524320 | tf_op jit(solution)/shard_map/all_to_all | solution.py:145
  19.0 4.2 %collective-permute-start = (bf16[16,256]{1,0:T(8,128)(2,1)S(1)}, bf16[16,256]{1,0:T(8,128)(2,1)S(1)}, u32[]{:S(2)}, u32[]{:S(2)}) collective-permute-start(bf16[16,256]{1,0:T(8,128)(2,1)S(1)} %slice.51), channel_id=1, source_target_pairs={{16,0},{32,16},{48,32},{64,48},{80,64},{96,80},{112,96},{128,112},... | collective-permute-start | bytes 24584 | tf_op jit(solution)/shard_map/ppermute | solution.py:28
  23.2 0.3 copy.24
  23.5 0.3 convolution_convert_fusion
  23.8 0.2 fusion.1
  24.1 1.9 %collective-permute-done = bf16[16,256]{1,0:T(8,128)(2,1)S(1)} collective-permute-done((bf16[16,256]{1,0:T(8,128)(2,1)S(1)}, bf16[16,256]{1,0:T(8,128)(2,1)S(1)}, u32[]{:S(2)}, u32[]{:S(2)}) %collective-permute-start) | collective-permute-done | bytes 8224 | tf_op jit(solution)/shard_map/ppermute | solution.py:28
  26.1 0.2 fusion
  26.3 0.9 pad_maximum_fusion
  27.3 11.7 %all-to-all-start.1 = ((bf16[16,96,256]{2,1,0:T(8,128)(2,1)}), bf16[16,96,256]{2,1,0:T(8,128)(2,1)}, u32[]{:S(2)}, u32[]{:S(2)}) async-start(bf16[16,96,256]{2,1,0:T(8,128)(2,1)} %pad_maximum_fusion), calls=%async_computation.1 | async-start | bytes 1572864 | tf_op jit(solution)/shard_map/all_to_all | solution.py:200
  39.4 0.5 copy.21
  40.1 0.4 divide_bitcast_fusion
  40.5 4.9 %collective-permute-start.1 = (bf16[512,256]{1,0:T(8,128)(2,1)S(1)}, bf16[512,256]{1,0:T(8,128)(2,1)S(1)}, u32[]{:S(2)}, u32[]{:S(2)}) collective-permute-start(bf16[512,256]{1,0:T(8,128)(2,1)S(1)} %bitcast.47), channel_id=1, source_target_pairs={{0,16},{16,32},{32,48},{48,64},{64,80},{80,96},{96,112},{112,128},... | collective-permute-start | bytes 786440 | tf_op jit(solution)/shard_map/ppermute | solution.py:28
  45.5 17.7 %collective-permute-done.1 = bf16[512,256]{1,0:T(8,128)(2,1)S(1)} collective-permute-done((bf16[512,256]{1,0:T(8,128)(2,1)S(1)}, bf16[512,256]{1,0:T(8,128)(2,1)S(1)}, u32[]{:S(2)}, u32[]{:S(2)}) %collective-permute-start.1) | collective-permute-done | bytes 262176 | tf_op jit(solution)/shard_map/ppermute | solution.py:28
  63.3 7.9 %shard_map.73.refs_6_ = f32[1024,512]{1,0:T(8,128)S(1)} custom-call(bf16[1024,512]{1,0:T(8,128)(2,1)S(1)} %copy-done, bf16[1536,256]{1,0:T(8,128)(2,1)S(1)} %pad_maximum_fusion.1.refs_1_, s32[4,1,768]{2,1,0:T(1,128)S(1)} %get-tuple-element.13.refs_2_, s32[4,1,768]{2,1,0:T(1,128)S(1)} %get-tuple-element.12.refs_3_, ...), custom_call_target="tpu_custom_call" | custom-call | flops 1610612736 | bytes 6029312 | tf_op jit(solution)/shard_map/pallas_call | solution.py:114
  71.2 1.3 %copy-done.1 = f32[1024,512]{1,0:T(8,128)} copy-done((f32[1024,512]{1,0:T(8,128)}, f32[1024,512]{1,0:T(8,128)S(1)}, u32[]{:S(2)}) %copy-start.1) | copy-done | bytes 2097176
  72.6 1.3 %broadcast_in_dim.101 = bf16[2,16,96,256]{3,2,1,0:T(8,128)(2,1)S(1)} broadcast(bf16[16,96,256]{2,1,0:T(8,128)(2,1)} %all-to-all-done.1), dimensions={1,2,3} | broadcast | bytes 2359296 | tf_op jit(solution)/shard_map/broadcast_in_dim | solution.py:201
  73.9 5.0 %all_to_all.15 = bf16[32,96,256]{2,1,0:T(8,128)(2,1)S(1)} all-to-all(bf16[32,96,256]{2,1,0:T(8,128)(2,1)S(1)} %bitcast.43), channel_id=1, replica_groups={{0,1},{2,3},{4,5},{6,7},{8,9},{10,11},{12,13},{14,15},{16,17},{18,19},{..., dimensions={0} | all-to-all | bytes 3145728 | tf_op jit(solution)/shard_map/all_to_all | solution.py:204
  79.1 1.5 %copy-done.2 = f32[1024,512]{1,0:T(8,128)S(1)} copy-done((f32[1024,512]{1,0:T(8,128)S(1)}, f32[1024,512]{1,0:T(8,128)}, u32[]{:S(2)}) %copy-start.2) | copy-done | bytes 2097176
  80.5 9.6 %shard_map.74.refs_7_ = f32[1024,512]{1,0:T(8,128)S(1)} custom-call(bf16[1024,512]{1,0:T(8,128)(2,1)S(1)} %copy-done, bf16[1024,256]{1,0:T(8,128)(2,1)S(1)} %bitcast.35, s32[1,1,1024]{2,1,0:T(1,128)S(1)} %sub.35.refs_2_, s32[1,1,1024]{2,1,0:T(1,128)S(1)} %broadcast_13_refs_3__refs_4_.2.refs_3_.refs_4_, ...), custom_call_target="tpu_custom_call", output_to_operand_aliasing={{}: (6, {})} | custom-call | flops 2147483648 | bytes 5767168 | tf_op jit(solution)/shard_map/pallas_call | solution.py:114
  90.1 10.9 %shard_map.75 = bf16[1024,512]{1,0:T(8,128)(2,1)} custom-call(s32[4,16]{1,0:T(4,128)S(1)} %get-tuple-element.6.refs_0_, bf16[1024,512]{1,0:T(8,128)(2,1)S(1)} %copy-done, bf16[2048,256]{1,0:T(8,128)(2,1)S(1)} %bitcast.34, s32[4,1,1024]{2,1,0:T(1,128)S(1)} %add_select_fusion.refs_3_, s32[1,1,1024]{2,1,0:T(1,128)S(1)} %broadcast_13_refs_3__refs_4_.2.refs_3_.refs_4_, ...), custom_call_target="tpu_custom_call" | custom-call | flops 2147483648 | bytes 6291456 | tf_op jit(solution)/shard_map/pallas_call | solution.py:114
  (56 shorter events, 2.2 us)
Async XLA Ops:
  0.0 8.2 %copy-start.4 = (s32[64,64]{1,0:T(8,128)S(1)}, s32[64,64]{1,0:T(8,128)}, u32[]{:S(2)}) copy-start(s32[64,64]{1,0:T(8,128)} %param.13) | copy-start | bytes 49156
  2.7 16.3 %all-to-all-start = ((bf16[16,64,256]{2,1,0:T(8,128)(2,1)}), bf16[16,64,256]{2,1,0:T(8,128)(2,1)S(1)}, u32[]{:S(2)}, u32[]{:S(2)}) async-start(bf16[16,64,256]{2,1,0:T(8,128)(2,1)} %bitcast.3), calls=%async_computation | async-start | bytes 1048576 | tf_op jit(solution)/shard_map/all_to_all | solution.py:145
  19.0 7.0 %collective-permute-start = (bf16[16,256]{1,0:T(8,128)(2,1)S(1)}, bf16[16,256]{1,0:T(8,128)(2,1)S(1)}, u32[]{:S(2)}, u32[]{:S(2)}) collective-permute-start(bf16[16,256]{1,0:T(8,128)(2,1)S(1)} %slice.51), channel_id=1, source_target_pairs={{16,0},{32,16},{48,32},{64,48},{80,64},{96,80},{112,96},{128,112},... | collective-permute-start | bytes 24584 | tf_op jit(solution)/shard_map/ppermute | solution.py:28
  26.3 13.1 %copy-start.3 = (f32[3,4,1024]{2,1,0:T(4,128)S(1)}, f32[3,4,1024]{2,1,0:T(4,128)}, u32[]{:S(2)}) copy-start(f32[3,4,1024]{2,1,0:T(4,128)} %param.12) | copy-start | bytes 147460
  27.3 45.3 %all-to-all-start.1 = ((bf16[16,96,256]{2,1,0:T(8,128)(2,1)}), bf16[16,96,256]{2,1,0:T(8,128)(2,1)}, u32[]{:S(2)}, u32[]{:S(2)}) async-start(bf16[16,96,256]{2,1,0:T(8,128)(2,1)} %pad_maximum_fusion), calls=%async_computation.1 | async-start | bytes 1572864 | tf_op jit(solution)/shard_map/all_to_all | solution.py:200
  40.5 22.7 %collective-permute-start.1 = (bf16[512,256]{1,0:T(8,128)(2,1)S(1)}, bf16[512,256]{1,0:T(8,128)(2,1)S(1)}, u32[]{:S(2)}, u32[]{:S(2)}) collective-permute-start(bf16[512,256]{1,0:T(8,128)(2,1)S(1)} %bitcast.47), channel_id=1, source_target_pairs={{0,16},{16,32},{32,48},{48,64},{64,80},{80,96},{96,112},{112,128},... | collective-permute-start | bytes 786440 | tf_op jit(solution)/shard_map/ppermute | solution.py:28
  45.5 17.7 %copy-start = (bf16[1024,512]{1,0:T(8,128)(2,1)S(1)}, bf16[1024,512]{1,0:T(8,128)(2,1)}, u32[]{:S(2)}) copy-start(bf16[1024,512]{1,0:T(8,128)(2,1)} %refs_1_.1) | copy-start | bytes 3145732
  71.2 1.4 %copy-start.1 = (f32[1024,512]{1,0:T(8,128)}, f32[1024,512]{1,0:T(8,128)S(1)}, u32[]{:S(2)}) copy-start(f32[1024,512]{1,0:T(8,128)S(1)} %shard_map.73.refs_6_) | copy-start | bytes 6291460
  78.9 1.6 %copy-start.2 = (f32[1024,512]{1,0:T(8,128)S(1)}, f32[1024,512]{1,0:T(8,128)}, u32[]{:S(2)}) copy-start(f32[1024,512]{1,0:T(8,128)} %copy-done.1) | copy-start | bytes 6291460

commit v9 on v7

--- a/solution.py
+++ b/solution.py
@@ -129,6 +129,78 @@
     )(*args)
 
 
+def sink_attend(q, keys, vals, bias):
+    s = lax.dot_general(
+        q, keys, (((1,), (1,)), ((), ())), preferred_element_type=jnp.float32
+    ) * HD ** (-0.5) + bias
+    m = jnp.maximum(jnp.max(s, axis=1, keepdims=True), 0.0)
+    p = jnp.exp(s - m)
+    l = jnp.sum(p, axis=1, keepdims=True) + jnp.exp(-m)
+    return jnp.dot(p.astype(jnp.bfloat16), vals, preferred_element_type=jnp.float32) / l
+
+
+def late_kernel(pick_ref, q_ref, ckv_ref, clo_ref, skv_ref, slo_ref, t_ref, gc_ref, gs_ref,
+                acc_ref, o_ref, pool_ref, *, heads, picks):
+    block = pl.program_id(0)
+    for k in range(picks):
+        begin = pl.multiple_of(pick_ref[block, k] * TILE, TILE)
+        pool_ref[k * TILE : (k + 1) * TILE, :] = skv_ref[pl.ds(begin, TILE), :]
+    t = t_ref[...]
+    comp_bias = jnp.where(clo_ref[0] <= t, 0.0, -jnp.inf)
+    sel_bias = jnp.where(slo_ref[0] <= t, 0.0, -jnp.inf)
+    ckv = ckv_ref[...]
+    skv = pool_ref[...]
+    for h in range(heads):
+        q = q_ref[:, h * HD : (h + 1) * HD]
+        oc = sink_attend(q, ckv[:, :HD], ckv[:, HD:], comp_bias)
+        osel = sink_attend(q, skv[:, :HD], skv[:, HD:], sel_bias)
+        r = acc_ref[:, h * HD : (h + 1) * HD] + gc_ref[:, h : h + 1] * oc
+        r = r + gs_ref[:, h : h + 1] * osel
+        o_ref[:, h * HD : (h + 1) * HD] = r.astype(o_ref.dtype)
+
+
+def late_branches(q, ckv, clo, skv, slo, pick, t, gate_c, gate_s, acc):
+    rows, width = q.shape
+    heads = width // HD
+    blocks = rows // QB
+    picks = pick.shape[1]
+    sel_keys = picks * TILE
+    row_map = lambda i, *_: (i, 0)
+    whole = lambda i, *_: (0, 0)
+    in_specs = [
+        pl.BlockSpec((QB, width), row_map),
+        pl.BlockSpec(ckv.shape, whole),
+        pl.BlockSpec((1,) + clo.shape[1:], lambda i, *_: (0, 0, 0)),
+        pl.BlockSpec(skv.shape, whole),
+        pl.BlockSpec((1,) + slo.shape[1:], lambda i, *_: (i, 0, 0)),
+        pl.BlockSpec((QB, 1), row_map),
+        pl.BlockSpec((QB, gate_c.shape[1]), row_map),
+        pl.BlockSpec((QB, gate_s.shape[1]), row_map),
+        pl.BlockSpec((QB, width), row_map),
+    ]
+    key_rows = ckv.shape[0] + sel_keys
+    cost = pl.CostEstimate(
+        flops=4 * rows * heads * key_rows * HD,
+        transcendentals=rows * heads * key_rows,
+        bytes_accessed=q.size * 2 + ckv.size * 2 + skv.size * 2 + rows * width * 6,
+    )
+    return pl.pallas_call(
+        functools.partial(late_kernel, heads=heads, picks=picks),
+        grid_spec=pltpu.PrefetchScalarGridSpec(
+            num_scalar_prefetch=1,
+            grid=(blocks,),
+            in_specs=in_specs,
+            out_specs=pl.BlockSpec((QB, width), row_map),
+            scratch_shapes=[pltpu.VMEM((sel_keys, skv.shape[1]), skv.dtype)],
+        ),
+        out_shape=jax.ShapeDtypeStruct((rows, width), jnp.bfloat16),
+        compiler_params=pltpu.CompilerParams(
+            dimension_semantics=("arbitrary",), vmem_limit_bytes=48 * 1024 * 1024
+        ),
+        cost_estimate=cost,
+    )(pick, q, ckv, clo, skv, slo, t, gate_c, gate_s, acc)
+
+
 def local(queries, keys, values, comp_k_weight, comp_v_weight, gate_logits, sel_tiles):
     ctx_count = lax.axis_size("ctx")
     head_count = lax.axis_size("head")
@@ -270,13 +342,9 @@
         queries, window_kv, win_lo, win_hi, positions, gate_values[2], None,
         sink=False, key_rows=win_rows, row_step=QB, out_dtype=jnp.float32,
     )
-    acc = branch(
-        queries, comp_kv, comp_lo, comp_hi, positions, gate_values[0], acc,
-        sink=True, key_rows=comp_count, row_step=0, out_dtype=jnp.float32,
-    )
-    return branch(
-        queries, sel_kv, sel_lo, never, positions, gate_values[1], acc,
-        sink=True, key_rows=TOPK * TILE, row_step=0, out_dtype=jnp.bfloat16, pick=pick,
+    return late_branches(
+        queries, comp_kv, comp_lo, sel_kv, sel_lo, pick, positions,
+        gate_values[0], gate_values[1], acc,
     )
 
 

time: 94.7 us -> 93.2 us (0.984)
  the two profiles are of different devices: /device:TPU:3 before, /device:TPU:9 now
where the time goes in v9:
time: 93.2 us; the launch traced here: 92.6 us
  Pallas kernels  28.1 us (30%)
  starting transfers between devices  22.1 us (24%)
  waiting for transfers between devices  20.1 us (22%)
  local copies, waits for them, and re-layouts  9.29 us (10%)
  blocking collectives  8.04 us (9%)
  other arithmetic  4.42 us (5%)
    pallas_call x1, Pallas kernels, late_branches(): pl.pallas_call(functools.partial(late_kernel, heads=heads, picks=picks),...  20.1 us
    all_to_all x1, starting transfers between devices, local(): lax.all_to_all(mail, 'ctx', split_axis=0, concat_axis=0, tiled=True)  11.6 us
    all_to_all x1, waiting for transfers between devices, local(): lax.all_to_all(mail, 'ctx', split_axis=0, concat_axis=0, tiled=True)  10.2 us
    all_to_all x1, blocking collectives, local(): lax.all_to_all(spread, 'head', 0, 0, axis_index_groups=groups, tiled=True)  8.04 us
    pallas_call x1, Pallas kernels, branch(): pl.pallas_call(kernel, grid_spec=pltpu.PrefetchScalarGridSpec(num_scalar_...  7.92 us
    all_to_all x1, starting transfers between devices, local(): lax.all_to_all(outbox_kv, 'head', 0, 0, tiled=True)  6.14 us
    ppermute x1, waiting for transfers between devices, shifted(): return lax.ppermute(block, axis, route)  5.46 us
    all_to_all x1, waiting for transfers between devices, local(): lax.all_to_all(outbox_kv, 'head', 0, 0, tiled=True)  4.42 us
  transfers between devices with their start and end apart: 3, of which 3 were waited for; matrix products, arithmetic and copies ran while one was open for 6% of the time, Pallas kernels for 9%

profile of v9, /device:TPU:9, one launch (start us, length us, event | category | flops | bytes accessed | tf_op | source)
XLA Modules:
  0.0 92.6 jit_solution(13095236834641607281)
XLA Ops:
  0.0 0.9 reshape.334
  0.9 0.9 reshape.335
  1.8 0.8 broadcast_in_dim.103
  2.7 6.1 %all-to-all-start = ((bf16[16,64,256]{2,1,0:T(8,128)(2,1)}), bf16[16,64,256]{2,1,0:T(8,128)(2,1)S(1)}, u32[]{:S(2)}, u32[]{:S(2)}) async-start(bf16[16,64,256]{2,1,0:T(8,128)(2,1)} %bitcast.3), calls=%async_computation | async-start | bytes 1048576 | tf_op jit(solution)/shard_map/all_to_all | solution.py:217
  9.1 0.4 compare_reduce_fusion.1
  9.5 0.2 reduce_window_sum.28
  9.7 0.1 fusion.9
  9.8 0.1 select_reduce_fusion.2
  10.3 0.2 reduce_window_sum.29
  10.5 0.1 fusion.5
  10.7 0.2 select_reduce_fusion
  11.0 0.4 compare_reduce_fusion
  11.4 0.7 constant_dynamic-slice_fusion
  12.2 0.2 reduce_window_sum.30
  12.5 4.4 %all-to-all-done = bf16[16,64,256]{2,1,0:T(8,128)(2,1)S(1)} async-done(((bf16[16,64,256]{2,1,0:T(8,128)(2,1)}), bf16[16,64,256]{2,1,0:T(8,128)(2,1)S(1)}, u32[]{:S(2)}, u32[]{:S(2)}) %all-to-all-start) | async-done | bytes 524320 | tf_op jit(solution)/shard_map/all_to_all | solution.py:217
  16.9 0.3 copy.23
  17.3 4.4 %collective-permute-start = (bf16[512,256]{1,0:T(8,128)(2,1)S(1)}, bf16[512,256]{1,0:T(8,128)(2,1)S(1)}, u32[]{:S(2)}, u32[]{:S(2)}) collective-permute-start(bf16[512,256]{1,0:T(8,128)(2,1)S(1)} %bitcast.46), channel_id=1, source_target_pairs={{0,16},{16,32},{32,48},{48,64},{64,80},{80,96},{96,112},{112,128},... | collective-permute-start | bytes 786440 | tf_op jit(solution)/shard_map/ppermute | solution.py:28
  21.6 0.3 convolution_convert_fusion
  22.0 0.2 fusion
  22.3 5.5 %collective-permute-done = bf16[512,256]{1,0:T(8,128)(2,1)S(1)} collective-permute-done((bf16[512,256]{1,0:T(8,128)(2,1)S(1)}, bf16[512,256]{1,0:T(8,128)(2,1)S(1)}, u32[]{:S(2)}, u32[]{:S(2)}) %collective-permute-start) | collective-permute-done | bytes 262176 | tf_op jit(solution)/shard_map/ppermute | solution.py:28
  27.7 0.2 fusion.1
  28.0 0.9 %pad_maximum_fusion.1 = bf16[16,96,256]{2,1,0:T(8,128)(2,1)} fusion(bf16[16,32,256]{2,1,0:T(8,128)(2,1)S(1)} %broadcast_in_dim.104, bf16[16,64,256]{2,1,0:T(8,128)(2,1)S(1)} %bitcast.43), kind=kLoop, calls=%fused_computation.9 | loop fusion | flops 1572864 | bytes 1572864 | tf_op jit(solution)/shard_map/concatenate | solution.py:272
  29.0 11.6 %all-to-all-start.1 = ((bf16[16,96,256]{2,1,0:T(8,128)(2,1)}), bf16[16,96,256]{2,1,0:T(8,128)(2,1)}, u32[]{:S(2)}, u32[]{:S(2)}) async-start(bf16[16,96,256]{2,1,0:T(8,128)(2,1)} %pad_maximum_fusion.1), calls=%async_computation.1 | async-start | bytes 1572864 | tf_op jit(solution)/shard_map/all_to_all | solution.py:273
  41.0 0.5 copy.20
  41.7 0.4 divide_bitcast_fusion
  42.4 1.2 %copy-done = bf16[1024,512]{1,0:T(8,128)(2,1)S(1)} copy-done((bf16[1024,512]{1,0:T(8,128)(2,1)S(1)}, bf16[1024,512]{1,0:T(8,128)(2,1)}, u32[]{:S(2)}) %copy-start) | copy-done | bytes 1048600
  43.5 7.9 %shard_map.73.acc_ref = f32[1024,512]{1,0:T(8,128)S(1)} custom-call(bf16[1024,512]{1,0:T(8,128)(2,1)S(1)} %copy-done, bf16[1536,256]{1,0:T(8,128)(2,1)S(1)} %pad_maximum_fusion.refs_1_, s32[4,1,768]{2,1,0:T(1,128)S(1)} %get-tuple-element.13.refs_2_, s32[4,1,768]{2,1,0:T(1,128)S(1)} %get-tuple-element.12.refs_3_, s32[1024,1]{1,0:T(8,128)S(1)} %iota_add_fusion.refs_4_.t_ref, ...), custom_call_target="tpu_custom_call" | custom-call | flops 1610612736 | bytes 6029312 | tf_op jit(solution)/shard_map/pallas_call | solution.py:114
  51.5 1.3 %copy-done.1 = f32[1024,512]{1,0:T(8,128)} copy-done((f32[1024,512]{1,0:T(8,128)}, f32[1024,512]{1,0:T(8,128)S(1)}, u32[]{:S(2)}) %copy-start.1) | copy-done | bytes 2097176
  52.8 10.2 %all-to-all-done.1 = bf16[16,96,256]{2,1,0:T(8,128)(2,1)} async-done(((bf16[16,96,256]{2,1,0:T(8,128)(2,1)}), bf16[16,96,256]{2,1,0:T(8,128)(2,1)}, u32[]{:S(2)}, u32[]{:S(2)}) %all-to-all-start.1) | async-done | bytes 786464 | tf_op jit(solution)/shard_map/all_to_all | solution.py:273
  63.0 1.3 %broadcast_in_dim.105 = bf16[2,16,96,256]{3,2,1,0:T(8,128)(2,1)S(1)} broadcast(bf16[16,96,256]{2,1,0:T(8,128)(2,1)} %all-to-all-done.1), dimensions={1,2,3} | broadcast | bytes 2359296 | tf_op jit(solution)/shard_map/broadcast_in_dim | solution.py:274
  64.3 8.0 %all_to_all.15 = bf16[32,96,256]{2,1,0:T(8,128)(2,1)S(1)} all-to-all(bf16[32,96,256]{2,1,0:T(8,128)(2,1)S(1)} %bitcast.42), channel_id=1, replica_groups={{0,1},{2,3},{4,5},{6,7},{8,9},{10,11},{12,13},{14,15},{16,17},{18,19},{..., dimensions={0} | all-to-all | bytes 3145728 | tf_op jit(solution)/shard_map/all_to_all | solution.py:277
  72.5 20.1 %shard_map.74 = bf16[1024,512]{1,0:T(8,128)(2,1)} custom-call(s32[4,16]{1,0:T(4,128)S(1)} %get-tuple-element.6.pick_ref, bf16[1024,512]{1,0:T(8,128)(2,1)S(1)} %copy-done, bf16[1024,256]{1,0:T(8,128)(2,1)S(1)} %bitcast.35, s32[1,1,1024]{2,1,0:T(1,128)S(1)} %reshape.347.clo_ref, bf16[2048,256]{1,0:T(8,128)(2,1)S(1)} %bitcast.34, ...), custom_call_target="tpu_custom_call" | custom-call | flops 4294967296 | bytes 5767168 | tf_op jit(solution)/shard_map/pallas_call | solution.py:187
  (49 shorter events, 2.0 us)
Async XLA Ops:
  0.0 8.8 %copy-start.3 = (s32[64,64]{1,0:T(8,128)S(1)}, s32[64,64]{1,0:T(8,128)}, u32[]{:S(2)}) copy-start(s32[64,64]{1,0:T(8,128)} %param.13) | copy-start | bytes 49156
  2.7 14.3 %all-to-all-start = ((bf16[16,64,256]{2,1,0:T(8,128)(2,1)}), bf16[16,64,256]{2,1,0:T(8,128)(2,1)S(1)}, u32[]{:S(2)}, u32[]{:S(2)}) async-start(bf16[16,64,256]{2,1,0:T(8,128)(2,1)} %bitcast.3), calls=%async_computation | async-start | bytes 1048576 | tf_op jit(solution)/shard_map/all_to_all | solution.py:217
  17.3 10.5 %collective-permute-start = (bf16[512,256]{1,0:T(8,128)(2,1)S(1)}, bf16[512,256]{1,0:T(8,128)(2,1)S(1)}, u32[]{:S(2)}, u32[]{:S(2)}) collective-permute-start(bf16[512,256]{1,0:T(8,128)(2,1)S(1)} %bitcast.46), channel_id=1, source_target_pairs={{0,16},{16,32},{32,48},{48,64},{64,80},{80,96},{96,112},{112,128},... | collective-permute-start | bytes 786440 | tf_op jit(solution)/shard_map/ppermute | solution.py:28
  28.0 13.0 %copy-start.2 = (f32[3,4,1024]{2,1,0:T(4,128)S(1)}, f32[3,4,1024]{2,1,0:T(4,128)}, u32[]{:S(2)}) copy-start(f32[3,4,1024]{2,1,0:T(4,128)} %param.12) | copy-start | bytes 147460
  29.0 34.0 %all-to-all-start.1 = ((bf16[16,96,256]{2,1,0:T(8,128)(2,1)}), bf16[16,96,256]{2,1,0:T(8,128)(2,1)}, u32[]{:S(2)}, u32[]{:S(2)}) async-start(bf16[16,96,256]{2,1,0:T(8,128)(2,1)} %pad_maximum_fusion.1), calls=%async_computation.1 | async-start | bytes 1572864 | tf_op jit(solution)/shard_map/all_to_all | solution.py:273
  42.3 1.2 %copy-start = (bf16[1024,512]{1,0:T(8,128)(2,1)S(1)}, bf16[1024,512]{1,0:T(8,128)(2,1)}, u32[]{:S(2)}) copy-start(bf16[1024,512]{1,0:T(8,128)(2,1)} %q_ref.1) | copy-start | bytes 3145732
  51.4 1.4 %copy-start.1 = (f32[1024,512]{1,0:T(8,128)}, f32[1024,512]{1,0:T(8,128)S(1)}, u32[]{:S(2)}) copy-start(f32[1024,512]{1,0:T(8,128)S(1)} %shard_map.73.acc_ref) | copy-start | bytes 6291460

commit v10 on v9

--- a/solution.py
+++ b/solution.py
@@ -243,7 +243,6 @@
     tiles_shard = local_rows // TILE
     share = CORES
     part = head_index % share
-    groups = [[g * share + i for i in range(share)] for g in range(head_count // share)]
     sel_share = CAP * TILE // share
     comp_share = comp_local // share
     group_tiles = lax.dynamic_slice_in_dim(sel_tiles, group_index * TOPK, TOPK, 1)
@@ -271,12 +270,10 @@
     )
     mail = jnp.concatenate([sel_part, comp_part], axis=1)
     arrived = lax.all_to_all(mail, "ctx", split_axis=0, concat_axis=0, tiled=True)
-    spread = jnp.broadcast_to(arrived[None], (share,) + arrived.shape).reshape(
-        (share * ctx_count,) + arrived.shape[1:]
-    )
-    gathered = lax.all_to_all(
-        spread, "head", 0, 0, axis_index_groups=groups, tiled=True
-    ).reshape((share,) + arrived.shape)
+    partner = lax.ppermute(arrived, "head", [(i, i ^ 1) for i in range(head_count)])
+    gathered = jnp.where(
+        part == 0, jnp.stack([arrived, partner]), jnp.stack([partner, arrived])
+    )
     sel_kv = gathered[:, :, :sel_share].reshape(share * ctx_count * sel_share, 2 * HD)
     comp_kv = gathered[:, :, sel_share:].reshape(share * ctx_count * comp_share, 2 * HD)
     comp_count = comp_kv.shape[0]

time: 93.2 us -> 98.8 us (1.060)
  waiting for transfers between devices: 20.1 us -> 29.5 us
  blocking collectives: 8.04 us -> 0 us
  starting transfers between devices: 22.1 us -> 25.5 us
  other arithmetic: 4.42 us -> 5.81 us
    all_to_all x1, waiting for transfers between devices: 10.2 us -> 19.4 us  [local(): lax.all_to_all(mail, 'ctx', split_axis=0, concat_axis=0, tiled=True)]
    all_to_all x1 -> x0, blocking collectives: 8.04 us -> none  [local(): lax.all_to_all(spread, 'head', 0, 0, axis_index_groups=groups, tiled=True)]
    ppermute x0 -> x1, starting transfers between devices: none -> 3.41 us  [local(): lax.ppermute(arrived, 'head', [(i, i ^ 1) for i in range(head_count)])]
    squeeze x1, local copies, waits for them, and re-layouts: 0.1 us -> 1.46 us  [local(): gate_values[2]]
    broadcast_in_dim x1 -> x0, local copies, waits for them, and re-layouts: 1.33 us -> none  [local(): jnp.broadcast_to(arrived[None], (share,) + arrived.shape)]
    transpose x1, other arithmetic: 0.41 us -> 1.57 us  [local(): gate_values = jax.nn.sigmoid(gate_logits).transpose(0, 2, 1)]
  transfers between devices with their start and end apart: 3 -> 4, of which waited for: 3 -> 3; matrix products, arithmetic and copies ran while one was open for 6% -> 9% of each run, Pallas kernels for 9% -> 8%
where the time goes in v10:
time: 98.8 us; the launch traced here: 98.3 us
  waiting for transfers between devices  29.5 us (30%)
  Pallas kernels  27.5 us (28%)
  starting transfers between devices  25.5 us (26%)
  local copies, waits for them, and re-layouts  9.32 us (9%)
  other arithmetic  5.81 us (6%)
    pallas_call x1, Pallas kernels, late_branches(): pl.pallas_call(functools.partial(late_kernel, heads=heads, picks=picks),...  19.7 us
    all_to_all x1, waiting for transfers between devices, local(): lax.all_to_all(mail, 'ctx', split_axis=0, concat_axis=0, tiled=True)  19.4 us
    all_to_all x1, starting transfers between devices, local(): lax.all_to_all(mail, 'ctx', split_axis=0, concat_axis=0, tiled=True)  11.6 us
    pallas_call x1, Pallas kernels, branch(): pl.pallas_call(kernel, grid_spec=pltpu.PrefetchScalarGridSpec(num_scalar_...  7.82 us
    all_to_all x1, starting transfers between devices, local(): lax.all_to_all(outbox_kv, 'head', 0, 0, tiled=True)  6.14 us
    ppermute x1, waiting for transfers between devices, shifted(): return lax.ppermute(block, axis, route)  5.46 us
    all_to_all x1, waiting for transfers between devices, local(): lax.all_to_all(outbox_kv, 'head', 0, 0, tiled=True)  4.65 us
    ppermute x1, starting transfers between devices, shifted(): return lax.ppermute(block, axis, route)  4.37 us
  transfers between devices with their start and end apart: 4, of which 3 were waited for; matrix products, arithmetic and copies ran while one was open for 9% of the time, Pallas kernels for 8%

profile of v10, /device:TPU:9, one launch (start us, length us, event | category | flops | bytes accessed | tf_op | source)
XLA Modules:
  0.0 98.3 jit_solution(10422814677062730974)
XLA Ops:
  0.0 0.9 reshape.327
  0.9 0.9 reshape.328
  1.8 0.8 broadcast_in_dim.97
  2.7 6.1 %all-to-all-start = ((bf16[16,64,256]{2,1,0:T(8,128)(2,1)}), bf16[16,64,256]{2,1,0:T(8,128)(2,1)S(1)}, u32[]{:S(2)}, u32[]{:S(2)}) async-start(bf16[16,64,256]{2,1,0:T(8,128)(2,1)} %bitcast.3), calls=%async_computation | async-start | bytes 1048576 | tf_op jit(solution)/shard_map/all_to_all | solution.py:217
  9.1 0.4 compare_reduce_fusion.1
  9.5 0.2 reduce_window_sum.28
  9.7 0.1 fusion.9
  10.2 0.2 reduce_window_sum.29
  10.5 0.4 compare_reduce_fusion
  10.9 0.7 constant_dynamic-slice_fusion
  11.6 0.1 fusion.5
  11.8 0.2 reduce_window_sum.30
  12.1 0.2 select_reduce_fusion
  12.3 4.6 %all-to-all-done = bf16[16,64,256]{2,1,0:T(8,128)(2,1)S(1)} async-done(((bf16[16,64,256]{2,1,0:T(8,128)(2,1)}), bf16[16,64,256]{2,1,0:T(8,128)(2,1)S(1)}, u32[]{:S(2)}, u32[]{:S(2)}) %all-to-all-start) | async-done | bytes 524320 | tf_op jit(solution)/shard_map/all_to_all | solution.py:217
  16.9 0.3 copy.23
  17.3 4.4 %collective-permute-start = (bf16[512,256]{1,0:T(8,128)(2,1)S(1)}, bf16[512,256]{1,0:T(8,128)(2,1)S(1)}, u32[]{:S(2)}, u32[]{:S(2)}) collective-permute-start(bf16[512,256]{1,0:T(8,128)(2,1)S(1)} %bitcast.45), channel_id=1, source_target_pairs={{0,16},{16,32},{32,48},{48,64},{64,80},{80,96},{96,112},{112,128},... | collective-permute-start | bytes 786440 | tf_op jit(solution)/shard_map/ppermute | solution.py:28
  21.6 0.3 convolution_convert_fusion
  22.0 0.2 fusion
  22.3 5.5 %collective-permute-done = bf16[512,256]{1,0:T(8,128)(2,1)S(1)} collective-permute-done((bf16[512,256]{1,0:T(8,128)(2,1)S(1)}, bf16[512,256]{1,0:T(8,128)(2,1)S(1)}, u32[]{:S(2)}, u32[]{:S(2)}) %collective-permute-start) | collective-permute-done | bytes 262176 | tf_op jit(solution)/shard_map/ppermute | solution.py:28
  27.7 0.2 fusion.1
  28.0 0.9 pad_maximum_fusion.1
  29.0 11.6 %all-to-all-start.1 = ((bf16[16,96,256]{2,1,0:T(8,128)(2,1)}), bf16[16,96,256]{2,1,0:T(8,128)(2,1)S(1)}, u32[]{:S(2)}, u32[]{:S(2)}) async-start(bf16[16,96,256]{2,1,0:T(8,128)(2,1)} %pad_maximum_fusion.1), calls=%async_computation.1 | async-start | bytes 1572864 | tf_op jit(solution)/shard_map/all_to_all | solution.py:272
  41.0 0.5 copy.20
  41.9 1.6 %divide_bitcast_fusion = f32[3,1024,4]{2,1,0:T(8,128)} fusion(f32[3,4,1024]{1,2,0:T(8,128)S(1)} %copy.20), kind=kLoop, calls=%fused_computation.2 | loop fusion | flops 36864 | bytes 98304 | tf_op jit(solution)/shard_map/transpose | solution.py:336
  43.4 19.4 %all-to-all-done.1 = bf16[16,96,256]{2,1,0:T(8,128)(2,1)S(1)} async-done(((bf16[16,96,256]{2,1,0:T(8,128)(2,1)}), bf16[16,96,256]{2,1,0:T(8,128)(2,1)S(1)}, u32[]{:S(2)}, u32[]{:S(2)}) %all-to-all-start.1) | async-done | bytes 786464 | tf_op jit(solution)/shard_map/all_to_all | solution.py:272
  62.9 3.4 %collective-permute-start.1 = (bf16[16,96,256]{2,1,0:T(8,128)(2,1)S(1)}, bf16[16,96,256]{2,1,0:T(8,128)(2,1)S(1)}, u32[]{:S(2)}, u32[]{:S(2)}) collective-permute-start(bf16[16,96,256]{2,1,0:T(8,128)(2,1)S(1)} %all-to-all-done.1), channel_id=1, source_target_pairs={{0,1},{1,0},{2,3},{3,2},{4,5},{5,4},{6,7},{7,6},{8,9},{9,8},{10,11... | collective-permute-start | bytes 2359304 | tf_op jit(solution)/shard_map/ppermute | solution.py:273
  66.3 1.5 %slice_bitcast_fusion = (f32[1024,4]{1,0:T(8,128)S(1)}, f32[1024,4]{1,0:T(8,128)S(1)}, f32[1024,4]{1,0:T(8,128)S(1)}) fusion(f32[3,1024,4]{2,1,0:T(8,128)} %divide_bitcast_fusion), kind=kLoop, calls=%fused_computation.12 | loop fusion | bytes 98304 | tf_op jit(solution)/shard_map/squeeze | solution.py:339
  67.9 1.2 %copy-done = bf16[1024,512]{1,0:T(8,128)(2,1)S(1)} copy-done((bf16[1024,512]{1,0:T(8,128)(2,1)S(1)}, bf16[1024,512]{1,0:T(8,128)(2,1)}, u32[]{:S(2)}) %copy-start) | copy-done | bytes 1048600
  69.0 7.8 %shard_map.73.acc_ref = f32[1024,512]{1,0:T(8,128)S(1)} custom-call(bf16[1024,512]{1,0:T(8,128)(2,1)S(1)} %copy-done, bf16[1536,256]{1,0:T(8,128)(2,1)S(1)} %pad_maximum_fusion.refs_1_, s32[4,1,768]{2,1,0:T(1,128)S(1)} %get-tuple-element.13.refs_2_, s32[4,1,768]{2,1,0:T(1,128)S(1)} %get-tuple-element.12.refs_3_, s32[1024,1]{1,0:T(8,128)S(1)} %iota_add_fusion.refs_4_.t_ref, ...), custom_call_target="tpu_custom_call" | custom-call | flops 1610612736 | bytes 6029312 | tf_op jit(solution)/shard_map/pallas_call | solution.py:114
  76.9 1.3 %copy-done.1 = f32[1024,512]{1,0:T(8,128)} copy-done((f32[1024,512]{1,0:T(8,128)}, f32[1024,512]{1,0:T(8,128)S(1)}, u32[]{:S(2)}) %copy-start.1) | copy-done | bytes 2097176
  78.2 0.3 maximum_select_fusion
  78.6 19.7 %shard_map.74 = bf16[1024,512]{1,0:T(8,128)(2,1)} custom-call(s32[4,16]{1,0:T(4,128)S(1)} %get-tuple-element.6.pick_ref, bf16[1024,512]{1,0:T(8,128)(2,1)S(1)} %copy-done, bf16[1024,256]{1,0:T(8,128)(2,1)S(1)} %bitcast.35, s32[1,1,1024]{2,1,0:T(1,128)S(1)} %reshape.338.clo_ref, bf16[2048,256]{1,0:T(8,128)(2,1)S(1)} %bitcast.34, ...), custom_call_target="tpu_custom_call" | custom-call | flops 4294967296 | bytes 5767168 | tf_op jit(solution)/shard_map/pallas_call | solution.py:187
  (50 shorter events, 2.0 us)
Async XLA Ops:
  0.0 8.8 %copy-start.3 = (s32[64,64]{1,0:T(8,128)S(1)}, s32[64,64]{1,0:T(8,128)}, u32[]{:S(2)}) copy-start(s32[64,64]{1,0:T(8,128)} %param.13) | copy-start | bytes 49156
  2.7 14.3 %all-to-all-start = ((bf16[16,64,256]{2,1,0:T(8,128)(2,1)}), bf16[16,64,256]{2,1,0:T(8,128)(2,1)S(1)}, u32[]{:S(2)}, u32[]{:S(2)}) async-start(bf16[16,64,256]{2,1,0:T(8,128)(2,1)} %bitcast.3), calls=%async_computation | async-start | bytes 1048576 | tf_op jit(solution)/shard_map/all_to_all | solution.py:217
  17.3 10.5 %collective-permute-start = (bf16[512,256]{1,0:T(8,128)(2,1)S(1)}, bf16[512,256]{1,0:T(8,128)(2,1)S(1)}, u32[]{:S(2)}, u32[]{:S(2)}) collective-permute-start(bf16[512,256]{1,0:T(8,128)(2,1)S(1)} %bitcast.45), channel_id=1, source_target_pairs={{0,16},{16,32},{32,48},{48,64},{64,80},{80,96},{96,112},{112,128},... | collective-permute-start | bytes 786440 | tf_op jit(solution)/shard_map/ppermute | solution.py:28
  28.0 13.0 %copy-start.2 = (f32[3,4,1024]{2,1,0:T(4,128)S(1)}, f32[3,4,1024]{2,1,0:T(4,128)}, u32[]{:S(2)}) copy-start(f32[3,4,1024]{2,1,0:T(4,128)} %param.12) | copy-start | bytes 147460
  29.0 33.9 %all-to-all-start.1 = ((bf16[16,96,256]{2,1,0:T(8,128)(2,1)}), bf16[16,96,256]{2,1,0:T(8,128)(2,1)S(1)}, u32[]{:S(2)}, u32[]{:S(2)}) async-start(bf16[16,96,256]{2,1,0:T(8,128)(2,1)} %pad_maximum_fusion.1), calls=%async_computation.1 | async-start | bytes 1572864 | tf_op jit(solution)/shard_map/all_to_all | solution.py:272
  62.9 15.3 %collective-permute-start.1 = (bf16[16,96,256]{2,1,0:T(8,128)(2,1)S(1)}, bf16[16,96,256]{2,1,0:T(8,128)(2,1)S(1)}, u32[]{:S(2)}, u32[]{:S(2)}) collective-permute-start(bf16[16,96,256]{2,1,0:T(8,128)(2,1)S(1)} %all-to-all-done.1), channel_id=1, source_target_pairs={{0,1},{1,0},{2,3},{3,2},{4,5},{5,4},{6,7},{7,6},{8,9},{9,8},{10,11... | collective-permute-start | bytes 2359304 | tf_op jit(solution)/shard_map/ppermute | solution.py:273
  67.8 1.2 %copy-start = (bf16[1024,512]{1,0:T(8,128)(2,1)S(1)}, bf16[1024,512]{1,0:T(8,128)(2,1)}, u32[]{:S(2)}) copy-start(bf16[1024,512]{1,0:T(8,128)(2,1)} %q_ref.1) | copy-start | bytes 3145732
  76.9 1.4 %copy-start.1 = (f32[1024,512]{1,0:T(8,128)}, f32[1024,512]{1,0:T(8,128)S(1)}, u32[]{:S(2)}) copy-start(f32[1024,512]{1,0:T(8,128)S(1)} %shard_map.73.acc_ref) | copy-start | bytes 6291460
